TPU v7x, 32 devices: a whole 2x2x4 slice. The times are simulated.
32 devices in a mesh: ctx: 8 (over z, y), tp: 4 (over x, core).
Axes of the slice: x: 2, y: 2, z: 4, core: 2. Of those that a mesh axis runs over, the one named last changes fastest.
Arguments:
- tokens: bfloat16 [6144, 4096], P('ctx'), may hold values from -6 to 6
- in_weight: bfloat16 [4096, 3, 4096], P('ctx', None, 'tp'), may hold values from -0.09375 to 0.09375
- short_taps: float32 [3, 4096, 7], P(None, 'tp'), may hold values from -2.5 to 2.5
- medium_taps: float32 [4096, 128], P('tp'), may hold values from -2 to 2
- medium_decay: float32 [4096], P('tp'), may hold values from 0.01 to 0.3
- skip_gain: float32 [4096], P('tp'), may hold values from 0.5 to 1.5
- out_weight: bfloat16 [4096, 4096], P('tp'), may hold values from -0.09375 to 0.09375
Outputs:
- mixed: bfloat16 [6144, 4096], P('ctx', 'tp')
All inputs are finite; a program needn't handle non-finite values.
Results may differ from a plain program's by a relative error of at most 0.0072.
Values may be sent and summed in bfloat16 or wider, within the bound.
No kernel may reach another device: no remote copies, remote signals or barrier semaphores. Data moves between devices by JAX's collectives and lax.ppermute only.
A program may use at most 192 MiB of HBM per device.

v0:
```python
import functools

import jax
import jax.numpy as jnp
from jax import lax
from jax.sharding import PartitionSpec as P


from jax.experimental import pallas as pl
from jax.experimental.pallas import tpu as pltpu

HALO = 136
CHUNK = 64
LANES = 128


def filter_kernel(term_count, *refs):
    fields = refs[: 3 * term_count]
    taps, medium, skip, out, raw, prod, shifted, smooth_q = refs[3 * term_count :]
    ext = fields[0].shape[0]
    local = ext - HALO
    taps_count = 7
    short_count = taps.shape[0] // 3
    for slot in range(3):
        group = fields[slot * term_count : (slot + 1) * term_count]
        total = group[0][0:8, :]
        for term in group[1:]:
            total = total + term[0:8, :]
        raw[slot, 0:8, :] = total.astype(jnp.bfloat16).astype(jnp.float32)

    def gather_body(index, carry):
        row = pl.multiple_of(8 + index * CHUNK, 8)
        for slot in range(3):
            group = fields[slot * term_count : (slot + 1) * term_count]
            total = group[0][pl.ds(row, CHUNK), :]
            for term in group[1:]:
                total = total + term[pl.ds(row, CHUNK), :]
            raw[slot, pl.ds(row, CHUNK), :] = total.astype(jnp.bfloat16).astype(jnp.float32)
        return carry

    lax.fori_loop(0, (ext - 8) // CHUNK, gather_body, 0)

    def smooth(slot, row):
        window = raw[slot, pl.ds(row - 8, CHUNK + 8), :]
        total = jnp.zeros((CHUNK, LANES), jnp.float32)
        for lag in range(taps_count):
            weight = taps[pl.ds(slot * short_count + lag, 1), :]
            total = total + weight * window[8 - lag : 8 - lag + CHUNK]
        return total

    def product_body(index, carry):
        row = pl.multiple_of(8 + index * CHUNK, 8)
        prod[pl.ds(row, CHUNK), :] = smooth(1, row) * smooth(2, row)
        return carry

    lax.fori_loop(0, (ext - 8) // CHUNK, product_body, 0)

    def query_body(index, carry):
        row = pl.multiple_of(index * CHUNK, 8)
        smooth_q[pl.ds(row, CHUNK), :] = smooth(0, row + HALO)
        return carry

    lax.fori_loop(0, local // CHUNK, query_body, 0)

    def shift_body(index, carry):
        row = pl.multiple_of(16 + index * CHUNK, 8)
        window = prod[pl.ds(row - 8, CHUNK + 8), :]
        for shift in range(8):
            shifted[shift, pl.ds(row, CHUNK), :] = window[8 - shift : 8 - shift + CHUNK]
        return carry

    lax.fori_loop(0, (ext - 16) // CHUNK, shift_body, 0)
    tail = 16 + ((ext - 16) // CHUNK) * CHUNK
    if tail < ext:
        window = prod[tail - 8 : ext, :]
        for shift in range(8):
            shifted[shift, tail:ext, :] = window[8 - shift : 8 - shift + ext - tail]

    def chunk_body(index, carry):
        row = pl.multiple_of(index * CHUNK, CHUNK)
        at = pl.multiple_of(row + HALO, 8)
        total = skip[...] * prod[pl.ds(at, CHUNK), :]
        groups = medium.shape[0] // 8
        reach = 8 * (groups - 1)
        start = pl.multiple_of(at - reach, 8)
        for shift in range(8):
            window = shifted[shift, pl.ds(start, CHUNK + reach), :]
            for group in range(groups):
                offset = reach - 8 * group
                weight = medium[pl.ds(8 * group + shift, 1), :]
                total = total + weight * window[offset : offset + CHUNK]
        out[pl.ds(row, CHUNK), :] = (smooth_q[pl.ds(row, CHUNK), :] * total).astype(out.dtype)
        return carry

    lax.fori_loop(0, local // CHUNK, chunk_body, 0)


def channel_filter(fields, taps, medium, skip, first, tiles):
    term_count = len(fields[0])
    ext = fields[0][0].shape[0]
    local = ext - HALO
    channels = tiles * LANES

    def field_spec(field):
        return pl.BlockSpec((ext, LANES), lambda t: (0, first + t))

    return pl.pallas_call(
        functools.partial(filter_kernel, term_count),
        grid=(tiles,),
        in_specs=[field_spec(0)] * (3 * term_count)
        + [
            pl.BlockSpec((taps.shape[0], LANES), lambda t: (0, first + t)),
            pl.BlockSpec((medium.shape[0], LANES), lambda t: (0, first + t)),
            pl.BlockSpec((1, LANES), lambda t: (0, first + t)),
        ],
        out_specs=pl.BlockSpec((local, LANES), lambda t: (0, t)),
        out_shape=jax.ShapeDtypeStruct((local, channels), jnp.bfloat16),
        scratch_shapes=[
            pltpu.VMEM((3, ext, LANES), jnp.float32),
            pltpu.VMEM((ext, LANES), jnp.float32),
            pltpu.VMEM((8, ext, LANES), jnp.float32),
            pltpu.VMEM((local, LANES), jnp.float32),
        ],
    )(*[term for field in fields for term in field], taps, medium, skip)

def ring_order(count):
    if count % 2:
        return list(range(count))
    return list(range(0, count, 2)) + list(range(count - 1, 0, -2))


def ring_projection(tokens, in_weight, riders):
    count = lax.axis_size("ctx")
    rows = in_weight.shape[0]
    order = ring_order(count)
    place = [0] * count
    for at, member in enumerate(order):
        place[member] = at
    forward = [(order[k], order[(k + 1) % count]) for k in range(count)]
    backward = [(order[k], order[(k - 1) % count]) for k in range(count)]
    me = lax.axis_index("ctx")
    order_table = jnp.array(order, jnp.int32)
    my_place = jnp.array(place, jnp.int32)[me]

    def product(cols, block):
        return tuple(
            jnp.dot(cols, block[:, field, :], preferred_element_type=jnp.float32)
            for field in range(block.shape[1])
        )

    def plus(left, right):
        return tuple(a + b for a, b in zip(left, right))

    def partial(block, source, start, width):
        cols = lax.dynamic_slice_in_dim(tokens, source * rows + start, width, 1)
        return product(cols, block)

    total = partial(in_weight, me, 0, rows)
    full_steps = (count - 1) // 2
    half = rows // 2

    def sources(step):
        return (
            order_table[(my_place - step) % count],
            order_table[(my_place + step) % count],
        )

    def add_pair(total, ahead, behind, step):
        from_behind, from_ahead = sources(step)
        total = plus(total, partial(ahead, from_behind, 0, rows))
        return plus(total, partial(behind, from_ahead, 0, rows))

    def ring_step(step, carry):
        ahead, behind, total = carry
        moved_ahead = lax.ppermute(ahead, "ctx", forward)
        moved_behind = lax.ppermute(behind, "ctx", backward)
        total = add_pair(total, ahead, behind, step - 1)
        return (moved_ahead, moved_behind, total)

    if full_steps == 0:
        return tuple((part,) for part in total), riders
    ahead = lax.ppermute(in_weight, "ctx", forward)
    behind = lax.ppermute(in_weight, "ctx", backward)
    carry = (ahead, behind, total)
    if full_steps >= 2:
        carry = ring_step(2, carry)
    carry, riders = lax.optimization_barrier((carry, riders))

    def carried_step(step, state):
        return (ring_step(step, state[0]), state[1])

    carry, riders = lax.fori_loop(3, full_steps + 1, carried_step, (carry, riders))
    ahead, behind, total = carry
    if count % 2 == 0:
        last_ahead = lax.ppermute(ahead[:half], "ctx", forward)
        last_behind = lax.ppermute(behind[half:], "ctx", backward)
        from_behind_full, from_ahead_full = sources(full_steps)
        first_terms = partial(ahead, from_behind_full, 0, rows)
        second_terms = partial(behind, from_ahead_full, 0, rows)
        from_behind, from_ahead = sources(full_steps + 1)
        cols = jnp.concatenate(
            [
                lax.dynamic_slice_in_dim(tokens, from_behind * rows, half, 1),
                lax.dynamic_slice_in_dim(tokens, from_ahead * rows + half, rows - half, 1),
            ],
            axis=1,
        )
        block = jnp.concatenate([last_ahead, last_behind], axis=0)
        last_terms = product(cols, block)
        terms = tuple(zip(total, first_terms, second_terms, last_terms))
    else:
        from_behind_full, from_ahead_full = sources(full_steps)
        first_terms = partial(ahead, from_behind_full, 0, rows)
        second_terms = partial(behind, from_ahead_full, 0, rows)
        terms = tuple(zip(total, first_terms, second_terms))
    return terms, riders


def tp_bits(count):
    bits = []
    bit = 1
    while bit < count:
        bits.append(bit)
        bit *= 2
    return bits


def spread_weights(out_weight):
    count = lax.axis_size("tp")
    me = lax.axis_index("tp")
    width = out_weight.shape[1] // count
    weights = [lax.dynamic_slice_in_dim(out_weight, me * width, width, 1)]
    for partner in range(1, count):
        pairs = [(k, k ^ partner) for k in range(count)]
        sent = lax.dynamic_slice_in_dim(out_weight, (me ^ partner) * width, width, 1)
        weights.append(lax.ppermute(sent, "tp", pairs))
    return tuple(weights)


def output_projection(gated, weights):
    count = lax.axis_size("tp")
    pieces = {0: gated}
    for bit in reversed(tp_bits(count)):
        pairs = [(k, k ^ bit) for k in range(count)]
        moved = {key ^ bit: lax.ppermute(piece, "tp", pairs) for key, piece in pieces.items()}
        pieces.update(moved)
    total = None
    for key in sorted(pieces):
        part = jnp.dot(pieces[key], weights[key], preferred_element_type=jnp.float32)
        total = part if total is None else total + part
    return total

def halo_rows(tail):
    ctx_count = lax.axis_size("ctx")
    tp_count = lax.axis_size("tp")
    shift = [(k, k + 1) for k in range(ctx_count - 1)]
    if tp_count % 2:
        return lax.ppermute(tail, "ctx", shift)
    width = tail.shape[1] // 2
    side = lax.axis_index("tp") % 2
    mine = lax.ppermute(lax.dynamic_slice_in_dim(tail, side * width, width, 1), "ctx", shift)
    other = lax.ppermute(mine, "tp", [(k, k ^ 1) for k in range(tp_count)])
    return jnp.where(
        side == 0,
        jnp.concatenate([mine, other], axis=1),
        jnp.concatenate([other, mine], axis=1),
    )


def per_device(tokens, in_weight, short_taps, medium_taps, medium_decay, skip_gain, out_weight):
    row_count = tokens.shape[0]
    channel_count = in_weight.shape[2]
    ctx_count = lax.axis_size("ctx")
    medium_count = medium_taps.shape[1]
    short_count = short_taps.shape[2]
    earlier = halo_rows(tokens[row_count - HALO :])
    earlier, in_weight = lax.optimization_barrier((earlier, in_weight))
    widened = jnp.concatenate([earlier, tokens], axis=0)
    features, weights = ring_projection(widened, in_weight, spread_weights(out_weight))
    lag_values = lax.broadcasted_iota(jnp.float32, (1, medium_count), 1)
    filters = medium_taps * jnp.exp(-medium_decay[:, None] * lag_values)
    taps = jnp.pad(
        jnp.transpose(short_taps, (0, 2, 1)), ((0, 0), (0, 8 - short_count), (0, 0))
    ).reshape(3 * 8, channel_count)
    tiles = channel_count // LANES
    parts = 2 if tiles % 2 == 0 else 1
    share = tiles // parts
    medium = jnp.transpose(filters)
    skip = skip_gain.reshape(1, channel_count)
    total = None
    for part in range(parts):
        gated = channel_filter(features, taps, medium, skip, part * share, share)
        rows = slice(part * share * LANES, (part + 1) * share * LANES)
        piece = output_projection(gated, tuple(w[rows] for w in weights))
        total = piece if total is None else total + piece
    return total.astype(jnp.bfloat16)

def solution(mesh):
    return jax.shard_map(
        per_device,
        mesh=mesh,
        in_specs=(
            P("ctx", None),
            P("ctx", None, "tp"),
            P(None, "tp", None),
            P("tp", None),
            P("tp"),
            P("tp"),
            P("tp", None),
        ),
        out_specs=P("ctx", "tp"),
        check_vma=False,
    )
```

profile of v0, /device:TPU:1, one launch (start us, length us, event | category | flops | bytes accessed | tf_op | source)
XLA Modules:
  0.0 363.8 jit_solution(11104609540229839255)
XLA Ops:
  1.4 4.0 %collective-permute-start = (bf16[136,2048]{1,0:T(8,128)(2,1)S(1)}, bf16[136,2048]{1,0:T(8,128)(2,1)S(1)}, u32[]{:S(2)}, u32[]{:S(2)}) collective-permute-start(bf16[136,2048]{1,0:T(8,128)(2,1)S(1)} %constant_dynamic-slice_fusion.6), channel_id=1, source_target_pairs={{0,4},{4,8},{8,12},{12,16},{16,20},{20,24},{24,28},{1,5},{5,9},{9,... | collective-permute-start | bytes 1671176 | tf_op jit(solution)/shard_map/ppermute | solution.py:261
  5.4 11.2 %collective-permute-done = bf16[136,2048]{1,0:T(8,128)(2,1)S(1)} collective-permute-done((bf16[136,2048]{1,0:T(8,128)(2,1)S(1)}, bf16[136,2048]{1,0:T(8,128)(2,1)S(1)}, u32[]{:S(2)}, u32[]{:S(2)}) %collective-permute-start) | collective-permute-done | bytes 557088 | tf_op jit(solution)/shard_map/ppermute | solution.py:261
  18.2 1.6 collective-permute-done.1
  20.1 3.2 collective-permute-start.2
  23.3 6.4 %constant_dynamic-slice_fusion.2 = (bf16[1024,1024]{1,0:T(8,128)(2,1)}, bf16[1024,1024]{1,0:T(8,128)(2,1)}, bf16[1024,1024]{1,0:T(8,128)(2,1)S(1)}, bf16[1024,1024]{1,0:T(8,128)(2,1)}) fusion(bf16[1024,4096]{1,0:T(8,128)(2,1)} %param.15, s32[]{:T(128)S(6)} %select_n.138, s32[]{:T(128)S(6)} %select_n.136, s32[]{:T(128)S(6)} %select_n.135, s32[]{:T(128)S(6)} %select_n.137), kind=kLoop, calls=%fused_computation.125 | loop fusion | bytes 16777232 | tf_op jit(solution)/shard_map/dynamic_slice | solution.py:235
  43.6 2.0 copy.10
  45.7 3.4 constant_dynamic-update-slice_fusion
  50.5 40.3 %collective-permute-done.2 = bf16[512,3,1024]{2,0,1:T(8,128)(2,1)} collective-permute-done((bf16[512,3,1024]{2,0,1:T(8,128)(2,1)}, bf16[512,3,1024]{2,0,1:T(8,128)(2,1)}, u32[]{:S(2)}, u32[]{:S(2)}) %collective-permute-start.2) | collective-permute-done | bytes 3145760 | tf_op jit(solution)/shard_map/ppermute | solution.py:182
  90.8 2.1 collective-permute-start.3
  95.2 2.4 fusion.11
  97.6 2.4 fusion.10
  100.0 2.4 fusion.9
  102.4 2.4 add_add_fusion.5
  104.8 2.6 add_add_fusion.4
  107.4 2.5 add_add_fusion.3
  109.9 13.4 %collective-permute-done.8 = bf16[1024,1024]{1,0:T(8,128)(2,1)} collective-permute-done((bf16[1024,1024]{1,0:T(8,128)(2,1)}, bf16[1024,1024]{1,0:T(8,128)(2,1)}, u32[]{:S(2)}, u32[]{:S(2)}) %collective-permute-start.8) | collective-permute-done | bytes 2097184 | tf_op jit(solution)/shard_map/ppermute | solution.py:236
  123.3 36.3 %collective-permute-done.3 = bf16[512,3,1024]{2,0,1:T(8,128)(2,1)} collective-permute-done((bf16[512,3,1024]{2,0,1:T(8,128)(2,1)}, bf16[512,3,1024]{2,0,1:T(8,128)(2,1)}, u32[]{:S(2)}, u32[]{:S(2)}) %collective-permute-start.3) | collective-permute-done | bytes 3145760 | tf_op jit(solution)/shard_map/ppermute | solution.py:175
  159.6 1.6 collective-permute-done.5
  164.4 2.4 fusion.28
  166.8 2.4 fusion.22
  169.2 2.4 fusion.16
  171.5 3.0 add_add_fusion.2.refs_0_
  174.5 3.0 add_add_fusion.1.refs_4_
  177.6 3.2 add_add_fusion.refs_8_
  180.7 48.1 %collective-permute-done.9 = bf16[512,3,1024]{2,0,1:T(8,128)(2,1)} collective-permute-done((bf16[512,3,1024]{2,0,1:T(8,128)(2,1)}, bf16[512,3,1024]{2,0,1:T(8,128)(2,1)}, u32[]{:S(2)}, u32[]{:S(2)}) %collective-permute-start.9) | collective-permute-done | bytes 3145760 | tf_op jit(solution)/shard_map/while/body/eval_jaxpr/ppermute | solution.py:175
  233.7 4.2 %fusion.8.refs_1_ = f32[904,1024]{1,0:T(8,128)} fusion(bf16[512,3,1024]{2,0,1:T(8,128)(2,1)} %collective-permute-done.9, bf16[904,4096]{1,0:T(8,128)(2,1)S(1)} %constant_dynamic-update-slice_fusion, s32[]{:T(128)S(6)} %select_n.147), kind=kOutput, calls=%fused_computation.25 | convolution fusion | flops 947912704 | bytes 5677060 | tf_op jit(solution)/shard_map/dot_general | solution.py:147
  237.9 4.2 %fusion.5.refs_5_ = f32[904,1024]{1,0:T(8,128)} fusion(bf16[512,3,1024]{2,0,1:T(8,128)(2,1)} %collective-permute-done.9, bf16[904,4096]{1,0:T(8,128)(2,1)S(1)} %constant_dynamic-update-slice_fusion, s32[]{:T(128)S(6)} %select_n.147), kind=kOutput, calls=%fused_computation.19 | convolution fusion | flops 947912704 | bytes 5677060 | tf_op jit(solution)/shard_map/dot_general | solution.py:147
  242.1 4.2 %fusion.7.refs_2_ = f32[904,1024]{1,0:T(8,128)} fusion(bf16[512,3,1024]{2,0,1:T(8,128)(2,1)} %collective-permute-done.10, bf16[904,4096]{1,0:T(8,128)(2,1)S(1)} %constant_dynamic-update-slice_fusion, s32[]{:T(128)S(6)} %select_n.150), kind=kOutput, calls=%fused_computation.23 | convolution fusion | flops 947912704 | bytes 5677060 | tf_op jit(solution)/shard_map/dot_general | solution.py:147
  246.3 4.3 %fusion.4.refs_6_ = f32[904,1024]{1,0:T(8,128)} fusion(bf16[512,3,1024]{2,0,1:T(8,128)(2,1)} %collective-permute-done.10, bf16[904,4096]{1,0:T(8,128)(2,1)S(1)} %constant_dynamic-update-slice_fusion, s32[]{:T(128)S(6)} %select_n.150), kind=kOutput, calls=%fused_computation.17 | convolution fusion | flops 947912704 | bytes 5677060 | tf_op jit(solution)/shard_map/dot_general | solution.py:147
  250.6 4.2 %fusion.2.refs_9_ = f32[904,1024]{1,0:T(8,128)} fusion(bf16[512,3,1024]{2,0,1:T(8,128)(2,1)} %collective-permute-done.9, bf16[904,4096]{1,0:T(8,128)(2,1)S(1)} %constant_dynamic-update-slice_fusion, s32[]{:T(128)S(6)} %select_n.147), kind=kOutput, calls=%fused_computation.13 | convolution fusion | flops 947912704 | bytes 5677060 | tf_op jit(solution)/shard_map/dot_general | solution.py:147
  254.8 4.1 %fusion.1.refs_10_ = f32[904,1024]{1,0:T(8,128)} fusion(bf16[512,3,1024]{2,0,1:T(8,128)(2,1)} %collective-permute-done.10, bf16[904,4096]{1,0:T(8,128)(2,1)S(1)} %constant_dynamic-update-slice_fusion, s32[]{:T(128)S(6)} %select_n.150), kind=kOutput, calls=%fused_computation.11 | convolution fusion | flops 947912704 | bytes 5677060 | tf_op jit(solution)/shard_map/dot_general | solution.py:147
  259.0 4.0 %collective-permute-done.11 = bf16[256,3,1024]{2,0,1:T(8,128)(2,1)S(1)} collective-permute-done((bf16[256,3,1024]{2,0,1:T(8,128)(2,1)S(1)}, bf16[256,3,1024]{2,0,1:T(8,128)(2,1)S(1)}, u32[]{:S(2)}, u32[]{:S(2)}) %collective-permute-start.11) | collective-permute-done | bytes 1572896 | tf_op jit(solution)/shard_map/ppermute | solution.py:195
  263.1 3.0 collective-permute-done.12
  266.2 3.0 fusion.6.refs_3_
  269.2 2.9 fusion.3.refs_7_
  272.1 3.0 fusion.refs_11_
  275.1 27.2 %shard_map.91 = bf16[768,512]{1,0:T(8,128)(2,1)} custom-call(f32[904,1024]{1,0:T(8,128)} %add_add_fusion.2.refs_0_, f32[904,1024]{1,0:T(8,128)} %fusion.8.refs_1_, f32[904,1024]{1,0:T(8,128)} %fusion.7.refs_2_, f32[904,1024]{1,0:T(8,128)} %fusion.6.refs_3_, f32[904,1024]{1,0:T(8,128)} %add_add_fusion.1.refs_4_, f32[904,1024]{1,0:T(8,128)} %fusion.5.refs_5_, ...), custom_call_target="tpu_custom_call" | custom-call | tf_op jit(solution)/shard_map/pallas_call | solution.py:107
  303.5 26.9 %shard_map.92 = bf16[768,512]{1,0:T(8,128)(2,1)} custom-call(f32[904,1024]{1,0:T(8,128)} %add_add_fusion.2.refs_0_, f32[904,1024]{1,0:T(8,128)} %fusion.8.refs_1_, f32[904,1024]{1,0:T(8,128)} %fusion.7.refs_2_, f32[904,1024]{1,0:T(8,128)} %fusion.6.refs_3_, f32[904,1024]{1,0:T(8,128)} %add_add_fusion.1.refs_4_, f32[904,1024]{1,0:T(8,128)} %fusion.5.refs_5_, ...), custom_call_target="tpu_custom_call" | custom-call | tf_op jit(solution)/shard_map/pallas_call | solution.py:107
  330.8 5.0 %collective-permute-start.16 = (bf16[768,512]{1,0:T(8,128)(2,1)}, bf16[768,512]{1,0:T(8,128)(2,1)S(1)}, u32[]{:S(2)}, u32[]{:S(2)}) collective-permute-start(bf16[768,512]{1,0:T(8,128)(2,1)} %shard_map.92), channel_id=1, source_target_pairs={{0,1},{1,0},{2,3},{3,2},{4,5},{5,4},{6,7},{7,6},{8,9},{9,8},{10,11... | collective-permute-start | bytes 2359304 | tf_op jit(solution)/shard_map/ppermute | solution.py:245
  335.7 2.1 fusion.41
  339.4 2.2 fusion.45
  341.6 3.4 collective-permute-done.17
  345.1 2.2 fusion.37
  347.3 5.7 %collective-permute-start.18 = (bf16[768,512]{1,0:T(8,128)(2,1)S(1)}, bf16[768,512]{1,0:T(8,128)(2,1)}, u32[]{:S(2)}, u32[]{:S(2)}) collective-permute-start(bf16[768,512]{1,0:T(8,128)(2,1)S(1)} %collective-permute-done.17), channel_id=1, source_target_pairs={{0,1},{1,0},{2,3},{3,2},{4,5},{5,4},{6,7},{7,6},{8,9},{9,8},{10,11... | collective-permute-start | bytes 2359304 | tf_op jit(solution)/shard_map/ppermute | solution.py:245
  352.9 2.2 fusion.39
  355.2 2.2 fusion.47
  357.4 2.2 fusion.43
  359.6 4.2 %add_convert_fusion = bf16[768,1024]{1,0:T(8,128)(2,1)} fusion(f32[768,1024]{1,0:T(8,128)S(1)} %fusion.37, f32[768,1024]{1,0:T(8,128)S(1)} %fusion.41, f32[768,1024]{1,0:T(8,128)S(1)} %fusion.39, f32[768,1024]{1,0:T(8,128)S(1)} %fusion.43, f32[768,1024]{1,0:T(8,128)S(1)} %fusion.45, f32[768,1024]{1,0:T(8,128)S(1)} %fusion.49, f32[768,1024]{1,0:T(8,128)S(1)} %fusion.47, ...), kind=kOutput, calls=%fused_computation.6 | convolution fusion | flops 811597824 | bytes 25427968 | tf_op jit(solution)/shard_map/dot_general | solution.py:249
  (55 shorter events, 22.0 us)
Async XLA Ops:
  1.4 15.3 %collective-permute-start = (bf16[136,2048]{1,0:T(8,128)(2,1)S(1)}, bf16[136,2048]{1,0:T(8,128)(2,1)S(1)}, u32[]{:S(2)}, u32[]{:S(2)}) collective-permute-start(bf16[136,2048]{1,0:T(8,128)(2,1)S(1)} %constant_dynamic-slice_fusion.6), channel_id=1, source_target_pairs={{0,4},{4,8},{8,12},{12,16},{16,20},{20,24},{24,28},{1,5},{5,9},{9,... | collective-permute-start | bytes 1671176 | tf_op jit(solution)/shard_map/ppermute | solution.py:261
  16.7 3.1 collective-permute-start.1
  20.1 70.7 %collective-permute-start.2 = (bf16[512,3,1024]{2,0,1:T(8,128)(2,1)}, bf16[512,3,1024]{2,0,1:T(8,128)(2,1)}, u32[]{:S(2)}, u32[]{:S(2)}) collective-permute-start(bf16[512,3,1024]{2,0,1:T(8,128)(2,1)} %param.10), channel_id=1, source_target_pairs={{0,8},{8,16},{16,24},{24,28},{28,20},{20,12},{12,4},{4,0},{1,9},{9... | collective-permute-start | bytes 9437192 | tf_op jit(solution)/shard_map/ppermute | solution.py:182
  23.3 69.6 %collective-permute-start.4 = (bf16[512,3,1024]{2,0,1:T(8,128)(2,1)}, bf16[512,3,1024]{2,0,1:T(8,128)(2,1)}, u32[]{:S(2)}, u32[]{:S(2)}) collective-permute-start(bf16[512,3,1024]{2,0,1:T(8,128)(2,1)} %param.10), channel_id=1, source_target_pairs={{0,4},{8,0},{16,8},{24,16},{28,24},{20,28},{12,20},{4,12},{1,5},{9... | collective-permute-start | bytes 9437192 | tf_op jit(solution)/shard_map/ppermute | solution.py:183
  23.3 8.7 %copy-start.6 = (s32[8]{0:T(128)S(1)}, s32[8]{0:T(128)}, u32[]{:S(2)}) copy-start(s32[8]{0:T(128)} %constant.127.clone) | copy-start | bytes 100
  23.3 14.6 %copy-start.3 = (s32[8]{0:T(128)S(1)}, s32[8]{0:T(128)}, u32[]{:S(2)}) copy-start(s32[8]{0:T(128)} %constant.126.clone) | copy-start | bytes 100
  23.3 22.3 %copy-start.4 = (f32[1024]{0:T(1024)S(1)}, f32[1024]{0:T(1024)}, u32[]{:S(2)}) copy-start(f32[1024]{0:T(1024)} %param.13) | copy-start | bytes 12292
  29.7 80.2 %collective-permute-start.6 = (bf16[1024,1024]{1,0:T(8,128)(2,1)}, bf16[1024,1024]{1,0:T(8,128)(2,1)}, u32[]{:S(2)}, u32[]{:S(2)}) collective-permute-start(bf16[1024,1024]{1,0:T(8,128)(2,1)} %get-tuple-element.58), channel_id=1, source_target_pairs={{0,1},{1,0},{2,3},{3,2},{4,5},{5,4},{6,7},{7,6},{8,9},{9,8},{10,11... | collective-permute-start | bytes 6291464 | tf_op jit(solution)/shard_map/ppermute | solution.py:236
  30.4 79.5 %collective-permute-start.7 = (bf16[1024,1024]{1,0:T(8,128)(2,1)}, bf16[1024,1024]{1,0:T(8,128)(2,1)}, u32[]{:S(2)}, u32[]{:S(2)}) collective-permute-start(bf16[1024,1024]{1,0:T(8,128)(2,1)} %get-tuple-element.60), channel_id=1, source_target_pairs={{0,2},{1,3},{2,0},{3,1},{4,6},{5,7},{6,4},{7,5},{8,10},{9,11},{10,... | collective-permute-start | bytes 6291464 | tf_op jit(solution)/shard_map/ppermute | solution.py:236
  31.6 91.7 %collective-permute-start.8 = (bf16[1024,1024]{1,0:T(8,128)(2,1)}, bf16[1024,1024]{1,0:T(8,128)(2,1)}, u32[]{:S(2)}, u32[]{:S(2)}) collective-permute-start(bf16[1024,1024]{1,0:T(8,128)(2,1)} %get-tuple-element.57), channel_id=1, source_target_pairs={{0,3},{1,2},{2,1},{3,0},{4,7},{5,6},{6,5},{7,4},{8,11},{9,10},{10,... | collective-permute-start | bytes 6291464 | tf_op jit(solution)/shard_map/ppermute | solution.py:236
  45.7 3.7 %copy-start.5 = (bf16[512,3,1024]{2,0,1:T(8,128)(2,1)S(1)}, bf16[512,3,1024]{2,0,1:T(8,128)(2,1)}, u32[]{:S(2)}) copy-start(bf16[512,3,1024]{2,0,1:T(8,128)(2,1)} %param.10) | copy-start | bytes 9437188
  90.8 68.8 %collective-permute-start.3 = (bf16[512,3,1024]{2,0,1:T(8,128)(2,1)}, bf16[512,3,1024]{2,0,1:T(8,128)(2,1)}, u32[]{:S(2)}, u32[]{:S(2)}) collective-permute-start(bf16[512,3,1024]{2,0,1:T(8,128)(2,1)} %collective-permute-done.2), channel_id=1, source_target_pairs={{0,8},{8,16},{16,24},{24,28},{28,20},{20,12},{12,4},{4,0},{1,9},{9... | collective-permute-start | bytes 9437192 | tf_op jit(solution)/shard_map/ppermute | solution.py:175
  92.9 68.3 %collective-permute-start.5 = (bf16[512,3,1024]{2,0,1:T(8,128)(2,1)}, bf16[512,3,1024]{2,0,1:T(8,128)(2,1)S(1)}, u32[]{:S(2)}, u32[]{:S(2)}) collective-permute-start(bf16[512,3,1024]{2,0,1:T(8,128)(2,1)} %collective-permute-done.4), channel_id=1, source_target_pairs={{0,4},{8,0},{16,8},{24,16},{28,24},{20,28},{12,20},{4,12},{1,5},{9... | collective-permute-start | bytes 9437192 | tf_op jit(solution)/shard_map/ppermute | solution.py:176
  107.4 55.4 %copy-start.2 = (f32[3,1024,7]{1,2,0:T(8,128)S(1)}, f32[3,1024,7]{1,2,0:T(8,128)}, u32[]{:S(2)}) copy-start(f32[3,1024,7]{1,2,0:T(8,128)} %param.11) | copy-start | bytes 258052
  107.4 56.0 %copy-start.1 = (f32[1024,128]{0,1:T(8,128)S(1)}, f32[1024,128]{0,1:T(8,128)}, u32[]{:S(2)}) copy-start(f32[1024,128]{0,1:T(8,128)} %copy.10) | copy-start | bytes 1572868
  161.3 67.5 %collective-permute-start.9 = (bf16[512,3,1024]{2,0,1:T(8,128)(2,1)}, bf16[512,3,1024]{2,0,1:T(8,128)(2,1)}, u32[]{:S(2)}, u32[]{:S(2)}) collective-permute-start(bf16[512,3,1024]{2,0,1:T(8,128)(2,1)} %collective-permute-done.3), channel_id=1, source_target_pairs={{0,8},{8,16},{16,24},{24,28},{28,20},{20,12},{12,4},{4,0},{1,9},{9... | collective-permute-start | bytes 9437192 | tf_op jit(solution)/shard_map/while/body/eval_jaxpr/ppermute | solution.py:175
  162.6 69.2 %collective-permute-start.10 = (bf16[512,3,1024]{2,0,1:T(8,128)(2,1)S(1)}, bf16[512,3,1024]{2,0,1:T(8,128)(2,1)}, u32[]{:S(2)}, u32[]{:S(2)}) collective-permute-start(bf16[512,3,1024]{2,0,1:T(8,128)(2,1)S(1)} %collective-permute-done.5), channel_id=1, source_target_pairs={{0,4},{8,0},{16,8},{24,16},{28,24},{20,28},{12,20},{4,12},{1,5},{9... | collective-permute-start | bytes 9437192 | tf_op jit(solution)/shard_map/while/body/eval_jaxpr/ppermute | solution.py:176
  230.3 32.6 %collective-permute-start.11 = (bf16[256,3,1024]{2,0,1:T(8,128)(2,1)S(1)}, bf16[256,3,1024]{2,0,1:T(8,128)(2,1)S(1)}, u32[]{:S(2)}, u32[]{:S(2)}) collective-permute-start(bf16[256,3,1024]{2,0,1:T(8,128)(2,1)S(1)} %slice.154), channel_id=1, source_target_pairs={{0,8},{8,16},{16,24},{24,28},{28,20},{20,12},{12,4},{4,0},{1,9},{9... | collective-permute-start | bytes 4718600 | tf_op jit(solution)/shard_map/ppermute | solution.py:195
  233.4 32.7 %collective-permute-start.12 = (bf16[256,3,1024]{2,0,1:T(8,128)(2,1)S(1)}, bf16[256,3,1024]{2,0,1:T(8,128)(2,1)S(1)}, u32[]{:S(2)}, u32[]{:S(2)}) collective-permute-start(bf16[256,3,1024]{2,0,1:T(8,128)(2,1)S(1)} %slice.155), channel_id=1, source_target_pairs={{0,4},{8,0},{16,8},{24,16},{28,24},{20,28},{12,20},{4,12},{1,5},{9... | collective-permute-start | bytes 4718600 | tf_op jit(solution)/shard_map/ppermute | solution.py:196
  302.2 36.7 %collective-permute-start.14 = (bf16[768,512]{1,0:T(8,128)(2,1)}, bf16[768,512]{1,0:T(8,128)(2,1)S(1)}, u32[]{:S(2)}, u32[]{:S(2)}) collective-permute-start(bf16[768,512]{1,0:T(8,128)(2,1)} %shard_map.91), channel_id=1, source_target_pairs={{0,2},{1,3},{2,0},{3,1},{4,6},{5,7},{6,4},{7,5},{8,10},{9,11},{10,... | collective-permute-start | bytes 2359304 | tf_op jit(solution)/shard_map/ppermute | solution.py:245
  330.4 7.4 %copy-start = (bf16[768,512]{1,0:T(8,128)(2,1)S(1)}, bf16[768,512]{1,0:T(8,128)(2,1)}, u32[]{:S(2)}) copy-start(bf16[768,512]{1,0:T(8,128)(2,1)} %shard_map.91) | copy-start | bytes 2359300
  330.4 14.6 %collective-permute-start.17 = (bf16[768,512]{1,0:T(8,128)(2,1)}, bf16[768,512]{1,0:T(8,128)(2,1)S(1)}, u32[]{:S(2)}, u32[]{:S(2)}) collective-permute-start(bf16[768,512]{1,0:T(8,128)(2,1)} %shard_map.92), channel_id=1, source_target_pairs={{0,2},{1,3},{2,0},{3,1},{4,6},{5,7},{6,4},{7,5},{8,10},{9,11},{10,... | collective-permute-start | bytes 2359304 | tf_op jit(solution)/shard_map/ppermute | solution.py:245
  330.8 22.2 %collective-permute-start.16 = (bf16[768,512]{1,0:T(8,128)(2,1)}, bf16[768,512]{1,0:T(8,128)(2,1)S(1)}, u32[]{:S(2)}, u32[]{:S(2)}) collective-permute-start(bf16[768,512]{1,0:T(8,128)(2,1)} %shard_map.92), channel_id=1, source_target_pairs={{0,1},{1,0},{2,3},{3,2},{4,5},{5,4},{6,7},{7,6},{8,9},{9,8},{10,11... | collective-permute-start | bytes 2359304 | tf_op jit(solution)/shard_map/ppermute | solution.py:245
  338.9 16.3 %collective-permute-start.13 = (bf16[768,512]{1,0:T(8,128)(2,1)S(1)}, bf16[768,512]{1,0:T(8,128)(2,1)S(1)}, u32[]{:S(2)}, u32[]{:S(2)}) collective-permute-start(bf16[768,512]{1,0:T(8,128)(2,1)S(1)} %copy-done), channel_id=1, source_target_pairs={{0,1},{1,0},{2,3},{3,2},{4,5},{5,4},{6,7},{7,6},{8,9},{9,8},{10,11... | collective-permute-start | bytes 2359304 | tf_op jit(solution)/shard_map/ppermute | solution.py:245
  339.0 18.4 %collective-permute-start.15 = (bf16[768,512]{1,0:T(8,128)(2,1)S(1)}, bf16[768,512]{1,0:T(8,128)(2,1)S(1)}, u32[]{:S(2)}, u32[]{:S(2)}) collective-permute-start(bf16[768,512]{1,0:T(8,128)(2,1)S(1)} %collective-permute-done.14), channel_id=1, source_target_pairs={{0,1},{1,0},{2,3},{3,2},{4,5},{5,4},{6,7},{7,6},{8,9},{9,8},{10,11... | collective-permute-start | bytes 2359304 | tf_op jit(solution)/shard_map/ppermute | solution.py:245
  347.3 12.3 %collective-permute-start.18 = (bf16[768,512]{1,0:T(8,128)(2,1)S(1)}, bf16[768,512]{1,0:T(8,128)(2,1)}, u32[]{:S(2)}, u32[]{:S(2)}) collective-permute-start(bf16[768,512]{1,0:T(8,128)(2,1)S(1)} %collective-permute-done.17), channel_id=1, source_target_pairs={{0,1},{1,0},{2,3},{3,2},{4,5},{5,4},{6,7},{7,6},{8,9},{9,8},{10,11... | collective-permute-start | bytes 2359304 | tf_op jit(solution)/shard_map/ppermute | solution.py:245
where the time goes:
time: 365 us; the launch traced here: 364 us
  waiting for transfers between devices  163 us (45%)
  matrix products  86.8 us (24%)
  Pallas kernels  54.1 us (15%)
  starting transfers between devices  29.3 us (8%)
  local copies, waits for them, and re-layouts  19 us (5%)
  between operations  10.6 us (3%)
    ppermute x2, waiting for transfers between devices, ring_step(): moved_ahead = lax.ppermute(ahead, 'ctx', forward)  84.4 us
    dot_general x24, matrix products, product(): jnp.dot(cols, block[:, field, :], preferred_element_type=jnp.float32)  68.5 us
    pallas_call x2, Pallas kernels, channel_filter(): pl.pallas_call(functools.partial(filter_kernel, term_count), grid=(tiles,...  54.1 us
    ppermute x1, waiting for transfers between devices, ring_projection(): ahead = lax.ppermute(in_weight, 'ctx', forward)  40.3 us
    dot_general x8, matrix products, output_projection(): jnp.dot(pieces[key], weights[key], preferred_element_type=jnp.float32)  18.3 us
    ppermute x3, waiting for transfers between devices, spread_weights(): weights.append(lax.ppermute(sent, 'tp', pairs))  13.4 us
    ppermute x6, starting transfers between devices, output_projection(): lax.ppermute(piece, 'tp', pairs)  12.8 us
    ppermute x1, waiting for transfers between devices, halo_rows(): lax.ppermute(lax.dynamic_slice_in_dim(tail, side * width, width, 1), 'ctx...  11.2 us
  transfers between devices with their start and end apart: 19, of which 10 were waited for; matrix products, arithmetic and copies ran while one was open for 25% of the time, Pallas kernels for 7%

commit v1 on v0

--- a/solution.py
+++ b/solution.py
@@ -244,11 +244,8 @@
         pairs = [(k, k ^ bit) for k in range(count)]
         moved = {key ^ bit: lax.ppermute(piece, "tp", pairs) for key, piece in pieces.items()}
         pieces.update(moved)
-    total = None
-    for key in sorted(pieces):
-        part = jnp.dot(pieces[key], weights[key], preferred_element_type=jnp.float32)
-        total = part if total is None else total + part
-    return total
+    stacked = jnp.concatenate([pieces[key] for key in sorted(pieces)], axis=1)
+    return jnp.dot(stacked, weights, preferred_element_type=jnp.float32)
 
 def halo_rows(tail):
     ctx_count = lax.axis_size("ctx")
@@ -276,22 +273,27 @@
     earlier = halo_rows(tokens[row_count - HALO :])
     earlier, in_weight = lax.optimization_barrier((earlier, in_weight))
     widened = jnp.concatenate([earlier, tokens], axis=0)
-    features, weights = ring_projection(widened, in_weight, spread_weights(out_weight))
+    blocks = spread_weights(out_weight)
+    tiles = channel_count // LANES
+    parts = 2 if tiles % 2 == 0 else 1
+    share = tiles // parts
+    width = share * LANES
+    stacked = tuple(
+        jnp.concatenate([w[part * width : (part + 1) * width] for w in blocks], axis=0)
+        for part in range(parts)
+    )
+    features, stacked = ring_projection(widened, in_weight, stacked)
     lag_values = lax.broadcasted_iota(jnp.float32, (1, medium_count), 1)
     filters = medium_taps * jnp.exp(-medium_decay[:, None] * lag_values)
     taps = jnp.pad(
         jnp.transpose(short_taps, (0, 2, 1)), ((0, 0), (0, 8 - short_count), (0, 0))
     ).reshape(3 * 8, channel_count)
-    tiles = channel_count // LANES
-    parts = 2 if tiles % 2 == 0 else 1
-    share = tiles // parts
     medium = jnp.transpose(filters)
     skip = skip_gain.reshape(1, channel_count)
     total = None
     for part in range(parts):
         gated = channel_filter(features, taps, medium, skip, part * share, share)
-        rows = slice(part * share * LANES, (part + 1) * share * LANES)
-        piece = output_projection(gated, tuple(w[rows] for w in weights))
+        piece = output_projection(gated, stacked[part])
         total = piece if total is None else total + piece
     return total.astype(jnp.bfloat16)
 

time: 365 us -> 389 us (1.066)
  waiting for transfers between devices: 163 us -> 185 us
  matrix products: 86.8 us -> 79.9 us
  other arithmetic: 1.16 us -> 6.53 us
    ppermute x3, waiting for transfers between devices: 13.4 us -> 56.7 us  [spread_weights(): weights.append(lax.ppermute(sent, 'tp', pairs))]
    ppermute x1, waiting for transfers between devices: 40.3 us -> 0.01 us  [ring_projection(): ahead = lax.ppermute(in_weight, 'ctx', forward)]
    ppermute x1, waiting for transfers between devices: 3.96 us -> 12.8 us  [ring_projection(): last_ahead = lax.ppermute(ahead[:half], 'ctx', forward)]
    dot_general x8 -> x2, matrix products: 18.3 us -> 10.1 us  [output_projection(): return jnp.dot(stacked, weights, preferred_element_type=jnp.float32)]
    ppermute x2, waiting for transfers between devices: 84.4 us -> 92.4 us  [ring_step(): moved_ahead = lax.ppermute(ahead, 'ctx', forward)]
    slice x0 -> x4, local copies, waits for them, and re-layouts: none -> 6.85 us  [per_device(): w[part * width:(part + 1) * width]]
    ppermute x6, waiting for transfers between devices: 3.42 us -> 8.91 us  [output_projection(): lax.ppermute(piece, 'tp', pairs)]
    concatenate x0 -> x1, other arithmetic: none -> 4.14 us  [per_device(): jnp.concatenate([w[part * width:(part + 1) * width] for w in blocks], axi...]
  transfers between devices with their start and end apart: 19 -> 19, of which waited for: 10 -> 9; matrix products, arithmetic and copies ran while one was open for 25% -> 24% of each run, Pallas kernels for 7% -> 7%
where the time goes in v1:
time: 389 us; the launch traced here: 388 us
  waiting for transfers between devices  185 us (48%)
  matrix products  79.9 us (21%)
  Pallas kernels  54.1 us (14%)
  starting transfers between devices  30 us (8%)
  local copies, waits for them, and re-layouts  21.5 us (6%)
  between operations  10.8 us (3%)
  other arithmetic  6.53 us (2%)
    ppermute x2, waiting for transfers between devices, ring_step(): moved_ahead = lax.ppermute(ahead, 'ctx', forward)  92.4 us
    dot_general x24, matrix products, product(): jnp.dot(cols, block[:, field, :], preferred_element_type=jnp.float32)  69.8 us
    ppermute x3, waiting for transfers between devices, spread_weights(): weights.append(lax.ppermute(sent, 'tp', pairs))  56.7 us
    pallas_call x2, Pallas kernels, channel_filter(): pl.pallas_call(functools.partial(filter_kernel, term_count), grid=(tiles,...  54.1 us
    ppermute x1, waiting for transfers between devices, ring_projection(): last_ahead = lax.ppermute(ahead[:half], 'ctx', forward)  12.8 us
    ppermute x6, starting transfers between devices, output_projection(): lax.ppermute(piece, 'tp', pairs)  12.6 us
    ppermute x1, waiting for transfers between devices, halo_rows(): lax.ppermute(lax.dynamic_slice_in_dim(tail, side * width, width, 1), 'ctx...  11.2 us
    dot_general x2, matrix products, output_projection(): return jnp.dot(stacked, weights, preferred_element_type=jnp.float32)  10.1 us
  transfers between devices with their start and end apart: 19, of which 9 were waited for; matrix products, arithmetic and copies ran while one was open for 24% of the time, Pallas kernels for 7%

profile of v1, /device:TPU:1, one launch (start us, length us, event | category | flops | bytes accessed | tf_op | source)
XLA Modules:
  0.0 388.1 jit_solution(5925045367361159057)
XLA Ops:
  1.4 4.0 %collective-permute-start = (bf16[136,2048]{1,0:T(8,128)(2,1)S(1)}, bf16[136,2048]{1,0:T(8,128)(2,1)S(1)}, u32[]{:S(2)}, u32[]{:S(2)}) collective-permute-start(bf16[136,2048]{1,0:T(8,128)(2,1)S(1)} %constant_dynamic-slice_fusion.6), channel_id=1, source_target_pairs={{0,4},{4,8},{8,12},{12,16},{16,20},{20,24},{24,28},{1,5},{5,9},{9,... | collective-permute-start | bytes 1671176 | tf_op jit(solution)/shard_map/ppermute | solution.py:258
  5.4 11.2 %collective-permute-done = bf16[136,2048]{1,0:T(8,128)(2,1)S(1)} collective-permute-done((bf16[136,2048]{1,0:T(8,128)(2,1)S(1)}, bf16[136,2048]{1,0:T(8,128)(2,1)S(1)}, u32[]{:S(2)}, u32[]{:S(2)}) %collective-permute-start) | collective-permute-done | bytes 557088 | tf_op jit(solution)/shard_map/ppermute | solution.py:258
  18.2 5.6 %constant_dynamic-slice_fusion.5 = (bf16[1024,1024]{1,0:T(8,128)(2,1)S(1)}, bf16[1024,1024]{1,0:T(8,128)(2,1)}, bf16[1024,1024]{1,0:T(8,128)(2,1)}) fusion(bf16[1024,4096]{1,0:T(8,128)(2,1)} %param.15, s32[]{:T(128)S(6)} %select_n.136, s32[]{:T(128)S(6)} %select_n.138, s32[]{:T(128)S(6)} %select_n.137), kind=kLoop, calls=%fused_computation.131 | loop fusion | bytes 12582924 | tf_op jit(solution)/shard_map/dynamic_slice | solution.py:235
  40.6 3.2 collective-permute-start.2
  43.8 1.7 fusion.110
  45.6 3.4 constant_dynamic-update-slice_fusion
  49.3 3.0 fusion.52
  52.3 3.0 fusion.50
  55.2 2.4 fusion.48
  57.6 14.7 %collective-permute-done.8 = bf16[1024,1024]{1,0:T(8,128)(2,1)} collective-permute-done((bf16[1024,1024]{1,0:T(8,128)(2,1)}, bf16[1024,1024]{1,0:T(8,128)(2,1)}, u32[]{:S(2)}, u32[]{:S(2)}) %collective-permute-start.8) | collective-permute-done | bytes 2097184 | tf_op jit(solution)/shard_map/ppermute | solution.py:236
  72.3 1.7 fusion.113
  74.1 41.9 %collective-permute-done.7 = bf16[1024,1024]{1,0:T(8,128)(2,1)} collective-permute-done((bf16[1024,1024]{1,0:T(8,128)(2,1)}, bf16[1024,1024]{1,0:T(8,128)(2,1)}, u32[]{:S(2)}, u32[]{:S(2)}) %collective-permute-start.7) | collective-permute-done | bytes 2097184 | tf_op jit(solution)/shard_map/ppermute | solution.py:236
  116.0 1.7 fusion.112
  117.7 1.7 fusion.111
  119.4 3.2 collective-permute-start.3
  122.7 4.1 %pad_maximum_fusion = (bf16[2048,1024]{1,0:T(8,128)(2,1)}, bf16[2048,1024]{1,0:T(8,128)(2,1)}) fusion(bf16[512,1024]{1,0:T(8,128)(2,1)S(1)} %get-tuple-element.65, bf16[512,1024]{1,0:T(8,128)(2,1)S(1)} %get-tuple-element.63, bf16[512,1024]{1,0:T(8,128)(2,1)S(1)} %get-tuple-element.61, bf16[512,1024]{1,0:T(8,128)(2,1)S(1)} %get-tuple-element.54, ...), kind=kLoop, calls=%fused_computation | loop fusion | flops 33554432 | bytes 16777216 | tf_op jit(solution)/shard_map/concatenate | solution.py:282
  126.8 2.4 fusion.29
  129.2 2.4 fusion.28
  131.6 2.5 fusion.27
  134.1 2.6 add_add_fusion.5
  136.7 2.4 add_add_fusion.4
  139.1 2.5 add_add_fusion.3
  141.6 47.8 %collective-permute-done.3 = bf16[512,3,1024]{2,0,1:T(8,128)(2,1)} collective-permute-done((bf16[512,3,1024]{2,0,1:T(8,128)(2,1)}, bf16[512,3,1024]{2,0,1:T(8,128)(2,1)}, u32[]{:S(2)}, u32[]{:S(2)}) %collective-permute-start.3) | collective-permute-done | bytes 3145760 | tf_op jit(solution)/shard_map/ppermute | solution.py:175
  189.4 1.8 collective-permute-done.5
  194.4 2.4 fusion.46
  196.8 2.4 fusion.40
  199.1 2.4 fusion.34
  201.5 4.3 %add_add_fusion.2.refs_0_ = f32[904,1024]{1,0:T(8,128)} fusion(f32[904,1024]{1,0:T(8,128)S(1)} %add_add_fusion.5, f32[904,1024]{1,0:T(8,128)S(1)} %fusion.46, bf16[512,3,1024]{2,0,1:T(8,128)(2,1)} %collective-permute-done.5, bf16[904,4096]{1,0:T(8,128)(2,1)S(1)} %constant_dynamic-update-slice_fusion, s32[]{:T(128)S(6)} %select_n.144), kind=kOutput, calls=%fused_computation.4 | convolution fusion | flops 949764096 | bytes 13082628 | tf_op jit(solution)/shard_map/while/body/eval_jaxpr/dot_general | solution.py:147
  205.8 4.2 %add_add_fusion.1.refs_4_ = f32[904,1024]{1,0:T(8,128)} fusion(f32[904,1024]{1,0:T(8,128)S(1)} %add_add_fusion.4, f32[904,1024]{1,0:T(8,128)S(1)} %fusion.40, bf16[512,3,1024]{2,0,1:T(8,128)(2,1)} %collective-permute-done.5, bf16[904,4096]{1,0:T(8,128)(2,1)S(1)} %constant_dynamic-update-slice_fusion, s32[]{:T(128)S(6)} %select_n.144), kind=kOutput, calls=%fused_computation.3 | convolution fusion | flops 949764096 | bytes 13082628 | tf_op jit(solution)/shard_map/while/body/eval_jaxpr/dot_general | solution.py:147
  210.0 4.2 %add_add_fusion.refs_8_ = f32[904,1024]{1,0:T(8,128)} fusion(f32[904,1024]{1,0:T(8,128)S(1)} %add_add_fusion.3, f32[904,1024]{1,0:T(8,128)S(1)} %fusion.34, bf16[512,3,1024]{2,0,1:T(8,128)(2,1)} %collective-permute-done.5, bf16[904,4096]{1,0:T(8,128)(2,1)S(1)} %constant_dynamic-update-slice_fusion, s32[]{:T(128)S(6)} %select_n.144), kind=kOutput, calls=%fused_computation.2 | convolution fusion | flops 949764096 | bytes 13082628 | tf_op jit(solution)/shard_map/while/body/eval_jaxpr/dot_general | solution.py:147
  214.2 44.6 %collective-permute-done.9 = bf16[512,3,1024]{2,0,1:T(8,128)(2,1)S(1)} collective-permute-done((bf16[512,3,1024]{2,0,1:T(8,128)(2,1)}, bf16[512,3,1024]{2,0,1:T(8,128)(2,1)S(1)}, u32[]{:S(2)}, u32[]{:S(2)}) %collective-permute-start.9) | collective-permute-done | bytes 3145760 | tf_op jit(solution)/shard_map/while/body/eval_jaxpr/ppermute | solution.py:175
  260.9 3.0 fusion.26.refs_1_
  263.9 3.0 fusion.23.refs_5_
  266.9 3.0 fusion.25.refs_2_
  269.9 3.1 fusion.22.refs_6_
  273.0 2.9 fusion.20.refs_9_
  275.9 2.9 fusion.19.refs_10_
  278.9 12.8 %collective-permute-done.11 = bf16[256,3,1024]{2,0,1:T(8,128)(2,1)S(1)} collective-permute-done((bf16[256,3,1024]{2,0,1:T(8,128)(2,1)S(1)}, bf16[256,3,1024]{2,0,1:T(8,128)(2,1)S(1)}, u32[]{:S(2)}, u32[]{:S(2)}) %collective-permute-start.11) | collective-permute-done | bytes 1572896 | tf_op jit(solution)/shard_map/ppermute | solution.py:195
  293.3 3.1 fusion.24.refs_3_
  296.4 3.0 fusion.21.refs_7_
  299.3 2.9 fusion.18.refs_11_
  302.3 27.2 %shard_map.92 = bf16[768,512]{1,0:T(8,128)(2,1)} custom-call(f32[904,1024]{1,0:T(8,128)} %add_add_fusion.2.refs_0_, f32[904,1024]{1,0:T(8,128)} %fusion.26.refs_1_, f32[904,1024]{1,0:T(8,128)} %fusion.25.refs_2_, f32[904,1024]{1,0:T(8,128)} %fusion.24.refs_3_, f32[904,1024]{1,0:T(8,128)} %add_add_fusion.1.refs_4_, f32[904,1024]{1,0:T(8,128)} %fusion.23.refs_5_, ...), custom_call_target="tpu_custom_call" | custom-call | tf_op jit(solution)/shard_map/pallas_call | solution.py:107
  330.8 26.9 %shard_map.91 = bf16[768,512]{1,0:T(8,128)(2,1)} custom-call(f32[904,1024]{1,0:T(8,128)} %add_add_fusion.2.refs_0_, f32[904,1024]{1,0:T(8,128)} %fusion.26.refs_1_, f32[904,1024]{1,0:T(8,128)} %fusion.25.refs_2_, f32[904,1024]{1,0:T(8,128)} %fusion.24.refs_3_, f32[904,1024]{1,0:T(8,128)} %add_add_fusion.1.refs_4_, f32[904,1024]{1,0:T(8,128)} %fusion.23.refs_5_, ...), custom_call_target="tpu_custom_call" | custom-call | tf_op jit(solution)/shard_map/pallas_call | solution.py:107
  358.0 4.9 %collective-permute-start.16 = (bf16[768,512]{1,0:T(8,128)(2,1)S(1)}, bf16[768,512]{1,0:T(8,128)(2,1)S(1)}, u32[]{:S(2)}, u32[]{:S(2)}) collective-permute-start(bf16[768,512]{1,0:T(8,128)(2,1)S(1)} %copy-done.4), channel_id=1, source_target_pairs={{0,1},{1,0},{2,3},{3,2},{4,5},{5,4},{6,7},{7,6},{8,9},{9,8},{10,11... | collective-permute-start | bytes 2359304 | tf_op jit(solution)/shard_map/ppermute | solution.py:245
  363.4 8.9 %collective-permute-done.14 = bf16[768,512]{1,0:T(8,128)(2,1)S(1)} collective-permute-done((bf16[768,512]{1,0:T(8,128)(2,1)}, bf16[768,512]{1,0:T(8,128)(2,1)S(1)}, u32[]{:S(2)}, u32[]{:S(2)}) %collective-permute-start.14) | collective-permute-done | bytes 786464 | tf_op jit(solution)/shard_map/ppermute | solution.py:245
  372.3 5.6 %collective-permute-start.15 = (bf16[768,512]{1,0:T(8,128)(2,1)S(1)}, bf16[768,512]{1,0:T(8,128)(2,1)S(1)}, u32[]{:S(2)}, u32[]{:S(2)}) collective-permute-start(bf16[768,512]{1,0:T(8,128)(2,1)S(1)} %collective-permute-done.14), channel_id=1, source_target_pairs={{0,1},{1,0},{2,3},{3,2},{4,5},{5,4},{6,7},{7,6},{8,9},{9,8},{10,11... | collective-permute-start | bytes 2359304 | tf_op jit(solution)/shard_map/ppermute | solution.py:245
  377.9 5.6 %fusion.8 = f32[768,1024]{1,0:T(8,128)S(1)} fusion(bf16[2048,1024]{1,0:T(8,128)(2,1)} %get-tuple-element.52, bf16[768,512]{1,0:T(8,128)(2,1)S(1)} %collective-permute-done.18, bf16[768,512]{1,0:T(8,128)(2,1)S(1)} %collective-permute-done.17, bf16[768,512]{1,0:T(8,128)(2,1)S(1)} %collective-permute-done.16, bf16[768,512]{1,0:T(8,128)(2,1)S(1)} %copy-done.4), kind=kOutput, calls=%fused_computation.16 | convolution fusion | flops 3233808384 | bytes 10485760 | tf_op jit(solution)/shard_map/dot_general | solution.py:248
  383.6 4.5 %add_convert_fusion = bf16[768,1024]{1,0:T(8,128)(2,1)} fusion(f32[768,1024]{1,0:T(8,128)S(1)} %fusion.8, bf16[2048,1024]{1,0:T(8,128)(2,1)S(1)} %copy-done, bf16[768,512]{1,0:T(8,128)(2,1)S(1)} %collective-permute-done.15, bf16[768,512]{1,0:T(8,128)(2,1)S(1)} %collective-permute-done.14, bf16[768,512]{1,0:T(8,128)(2,1)S(1)} %collective-permute-done.13, ...), kind=kOutput, calls=%fused_computation.24 | convolution fusion | flops 3235381248 | bytes 12058624 | tf_op jit(solution)/shard_map/dot_general | solution.py:248
  (60 shorter events, 18.5 us)
Async XLA Ops:
  1.4 15.3 %collective-permute-start = (bf16[136,2048]{1,0:T(8,128)(2,1)S(1)}, bf16[136,2048]{1,0:T(8,128)(2,1)S(1)}, u32[]{:S(2)}, u32[]{:S(2)}) collective-permute-start(bf16[136,2048]{1,0:T(8,128)(2,1)S(1)} %constant_dynamic-slice_fusion.6), channel_id=1, source_target_pairs={{0,4},{4,8},{8,12},{12,16},{16,20},{20,24},{24,28},{1,5},{5,9},{9,... | collective-permute-start | bytes 1671176 | tf_op jit(solution)/shard_map/ppermute | solution.py:258
  16.7 22.4 %collective-permute-start.1 = (bf16[136,2048]{1,0:T(8,128)(2,1)S(1)}, bf16[136,2048]{1,0:T(8,128)(2,1)}, u32[]{:S(2)}, u32[]{:S(2)}) collective-permute-start(bf16[136,2048]{1,0:T(8,128)(2,1)S(1)} %collective-permute-done), channel_id=1, source_target_pairs={{0,1},{1,0},{2,3},{3,2},{4,5},{5,4},{6,7},{7,6},{8,9},{9,8},{10,11... | collective-permute-start | bytes 1671176 | tf_op jit(solution)/shard_map/ppermute | solution.py:259
  18.2 7.8 %copy-start.9 = (s32[8]{0:T(128)S(1)}, s32[8]{0:T(128)}, u32[]{:S(2)}) copy-start(s32[8]{0:T(128)} %constant.127.clone) | copy-start | bytes 100
  18.2 13.7 %copy-start.6 = (s32[8]{0:T(128)S(1)}, s32[8]{0:T(128)}, u32[]{:S(2)}) copy-start(s32[8]{0:T(128)} %constant.126.clone) | copy-start | bytes 100
  18.2 20.7 %copy-start.7 = (f32[1024]{0:T(1024)S(1)}, f32[1024]{0:T(1024)}, u32[]{:S(2)}) copy-start(f32[1024]{0:T(1024)} %param.13) | copy-start | bytes 12292
  23.8 48.5 %collective-permute-start.8 = (bf16[1024,1024]{1,0:T(8,128)(2,1)}, bf16[1024,1024]{1,0:T(8,128)(2,1)}, u32[]{:S(2)}, u32[]{:S(2)}) collective-permute-start(bf16[1024,1024]{1,0:T(8,128)(2,1)} %get-tuple-element.56), channel_id=1, source_target_pairs={{0,3},{1,2},{2,1},{3,0},{4,7},{5,6},{6,5},{7,4},{8,11},{9,10},{10,... | collective-permute-start | bytes 6291464 | tf_op jit(solution)/shard_map/ppermute | solution.py:236
  24.9 91.0 %collective-permute-start.7 = (bf16[1024,1024]{1,0:T(8,128)(2,1)}, bf16[1024,1024]{1,0:T(8,128)(2,1)}, u32[]{:S(2)}, u32[]{:S(2)}) collective-permute-start(bf16[1024,1024]{1,0:T(8,128)(2,1)} %get-tuple-element.57), channel_id=1, source_target_pairs={{0,2},{1,3},{2,0},{3,1},{4,6},{5,7},{6,4},{7,5},{8,10},{9,11},{10,... | collective-permute-start | bytes 6291464 | tf_op jit(solution)/shard_map/ppermute | solution.py:236
  25.2 92.5 %collective-permute-start.6 = (bf16[1024,1024]{1,0:T(8,128)(2,1)S(1)}, bf16[1024,1024]{1,0:T(8,128)(2,1)}, u32[]{:S(2)}, u32[]{:S(2)}) collective-permute-start(bf16[1024,1024]{1,0:T(8,128)(2,1)S(1)} %get-tuple-element.55), channel_id=1, source_target_pairs={{0,1},{1,0},{2,3},{3,2},{4,5},{5,4},{6,7},{7,6},{8,9},{9,8},{10,11... | collective-permute-start | bytes 6291464 | tf_op jit(solution)/shard_map/ppermute | solution.py:236
  40.6 78.9 %collective-permute-start.2 = (bf16[512,3,1024]{2,0,1:T(8,128)(2,1)}, bf16[512,3,1024]{2,0,1:T(8,128)(2,1)}, u32[]{:S(2)}, u32[]{:S(2)}) collective-permute-start(bf16[512,3,1024]{2,0,1:T(8,128)(2,1)} %param.10), channel_id=1, source_target_pairs={{0,8},{8,16},{16,24},{24,28},{28,20},{20,12},{12,4},{4,0},{1,9},{9... | collective-permute-start | bytes 9437192 | tf_op jit(solution)/shard_map/ppermute | solution.py:182
  43.8 78.9 %collective-permute-start.4 = (bf16[512,3,1024]{2,0,1:T(8,128)(2,1)}, bf16[512,3,1024]{2,0,1:T(8,128)(2,1)}, u32[]{:S(2)}, u32[]{:S(2)}) collective-permute-start(bf16[512,3,1024]{2,0,1:T(8,128)(2,1)} %param.10), channel_id=1, source_target_pairs={{0,4},{8,0},{16,8},{24,16},{28,24},{20,28},{12,20},{4,12},{1,5},{9... | collective-permute-start | bytes 9437192 | tf_op jit(solution)/shard_map/ppermute | solution.py:183
  45.6 3.7 copy-start.8
  119.4 70.0 %collective-permute-start.3 = (bf16[512,3,1024]{2,0,1:T(8,128)(2,1)}, bf16[512,3,1024]{2,0,1:T(8,128)(2,1)}, u32[]{:S(2)}, u32[]{:S(2)}) collective-permute-start(bf16[512,3,1024]{2,0,1:T(8,128)(2,1)} %collective-permute-done.2), channel_id=1, source_target_pairs={{0,8},{8,16},{16,24},{24,28},{28,20},{20,12},{12,4},{4,0},{1,9},{9... | collective-permute-start | bytes 9437192 | tf_op jit(solution)/shard_map/ppermute | solution.py:175
  122.7 68.6 %collective-permute-start.5 = (bf16[512,3,1024]{2,0,1:T(8,128)(2,1)}, bf16[512,3,1024]{2,0,1:T(8,128)(2,1)}, u32[]{:S(2)}, u32[]{:S(2)}) collective-permute-start(bf16[512,3,1024]{2,0,1:T(8,128)(2,1)} %collective-permute-done.4), channel_id=1, source_target_pairs={{0,4},{8,0},{16,8},{24,16},{28,24},{20,28},{12,20},{4,12},{1,5},{9... | collective-permute-start | bytes 9437192 | tf_op jit(solution)/shard_map/ppermute | solution.py:176
  131.5 2.5 copy-start.2
  134.1 2.6 copy-start.1
  139.1 53.6 %copy-start.5 = (f32[3,1024,7]{1,2,0:T(8,128)S(1)}, f32[3,1024,7]{1,2,0:T(8,128)}, u32[]{:S(2)}) copy-start(f32[3,1024,7]{1,2,0:T(8,128)} %param.11) | copy-start | bytes 258052
  191.2 67.6 %collective-permute-start.9 = (bf16[512,3,1024]{2,0,1:T(8,128)(2,1)}, bf16[512,3,1024]{2,0,1:T(8,128)(2,1)S(1)}, u32[]{:S(2)}, u32[]{:S(2)}) collective-permute-start(bf16[512,3,1024]{2,0,1:T(8,128)(2,1)} %collective-permute-done.3), channel_id=1, source_target_pairs={{0,8},{8,16},{16,24},{24,28},{28,20},{20,12},{12,4},{4,0},{1,9},{9... | collective-permute-start | bytes 9437192 | tf_op jit(solution)/shard_map/while/body/eval_jaxpr/ppermute | solution.py:175
  192.5 67.7 %collective-permute-start.10 = (bf16[512,3,1024]{2,0,1:T(8,128)(2,1)}, bf16[512,3,1024]{2,0,1:T(8,128)(2,1)S(1)}, u32[]{:S(2)}, u32[]{:S(2)}) collective-permute-start(bf16[512,3,1024]{2,0,1:T(8,128)(2,1)} %collective-permute-done.5), channel_id=1, source_target_pairs={{0,4},{8,0},{16,8},{24,16},{28,24},{20,28},{12,20},{4,12},{1,5},{9... | collective-permute-start | bytes 9437192 | tf_op jit(solution)/shard_map/while/body/eval_jaxpr/ppermute | solution.py:176
  258.9 32.8 %collective-permute-start.11 = (bf16[256,3,1024]{2,0,1:T(8,128)(2,1)S(1)}, bf16[256,3,1024]{2,0,1:T(8,128)(2,1)S(1)}, u32[]{:S(2)}, u32[]{:S(2)}) collective-permute-start(bf16[256,3,1024]{2,0,1:T(8,128)(2,1)S(1)} %slice.160), channel_id=1, source_target_pairs={{0,8},{8,16},{16,24},{24,28},{28,20},{20,12},{12,4},{4,0},{1,9},{9... | collective-permute-start | bytes 4718600 | tf_op jit(solution)/shard_map/ppermute | solution.py:195
  260.4 32.8 %collective-permute-start.12 = (bf16[256,3,1024]{2,0,1:T(8,128)(2,1)S(1)}, bf16[256,3,1024]{2,0,1:T(8,128)(2,1)S(1)}, u32[]{:S(2)}, u32[]{:S(2)}) collective-permute-start(bf16[256,3,1024]{2,0,1:T(8,128)(2,1)S(1)} %slice.161), channel_id=1, source_target_pairs={{0,4},{8,0},{16,8},{24,16},{28,24},{20,28},{12,20},{4,12},{1,5},{9... | collective-permute-start | bytes 4718600 | tf_op jit(solution)/shard_map/ppermute | solution.py:196
  329.5 28.5 %copy-start.4 = (bf16[768,512]{1,0:T(8,128)(2,1)S(1)}, bf16[768,512]{1,0:T(8,128)(2,1)}, u32[]{:S(2)}) copy-start(bf16[768,512]{1,0:T(8,128)(2,1)} %shard_map.92) | copy-start | bytes 2359300
  329.5 33.4 %collective-permute-start.17 = (bf16[768,512]{1,0:T(8,128)(2,1)}, bf16[768,512]{1,0:T(8,128)(2,1)S(1)}, u32[]{:S(2)}, u32[]{:S(2)}) collective-permute-start(bf16[768,512]{1,0:T(8,128)(2,1)} %shard_map.92), channel_id=1, source_target_pairs={{0,2},{1,3},{2,0},{3,1},{4,6},{5,7},{6,4},{7,5},{8,10},{9,11},{10,... | collective-permute-start | bytes 2359304 | tf_op jit(solution)/shard_map/ppermute | solution.py:245
  357.7 25.9 %copy-start = (bf16[2048,1024]{1,0:T(8,128)(2,1)S(1)}, bf16[2048,1024]{1,0:T(8,128)(2,1)}, u32[]{:S(2)}) copy-start(bf16[2048,1024]{1,0:T(8,128)(2,1)} %get-tuple-element.51) | copy-start | bytes 12582916
  357.7 25.9 %copy-start.3 = (bf16[768,512]{1,0:T(8,128)(2,1)S(1)}, bf16[768,512]{1,0:T(8,128)(2,1)}, u32[]{:S(2)}) copy-start(bf16[768,512]{1,0:T(8,128)(2,1)} %shard_map.91) | copy-start | bytes 2359300
  357.7 14.7 %collective-permute-start.14 = (bf16[768,512]{1,0:T(8,128)(2,1)}, bf16[768,512]{1,0:T(8,128)(2,1)S(1)}, u32[]{:S(2)}, u32[]{:S(2)}) collective-permute-start(bf16[768,512]{1,0:T(8,128)(2,1)} %shard_map.91), channel_id=1, source_target_pairs={{0,2},{1,3},{2,0},{3,1},{4,6},{5,7},{6,4},{7,5},{8,10},{9,11},{10,... | collective-permute-start | bytes 2359304 | tf_op jit(solution)/shard_map/ppermute | solution.py:245
  358.0 19.9 %collective-permute-start.16 = (bf16[768,512]{1,0:T(8,128)(2,1)S(1)}, bf16[768,512]{1,0:T(8,128)(2,1)S(1)}, u32[]{:S(2)}, u32[]{:S(2)}) collective-permute-start(bf16[768,512]{1,0:T(8,128)(2,1)S(1)} %copy-done.4), channel_id=1, source_target_pairs={{0,1},{1,0},{2,3},{3,2},{4,5},{5,4},{6,7},{7,6},{8,9},{9,8},{10,11... | collective-permute-start | bytes 2359304 | tf_op jit(solution)/shard_map/ppermute | solution.py:245
  362.9 15.0 %collective-permute-start.18 = (bf16[768,512]{1,0:T(8,128)(2,1)S(1)}, bf16[768,512]{1,0:T(8,128)(2,1)S(1)}, u32[]{:S(2)}, u32[]{:S(2)}) collective-permute-start(bf16[768,512]{1,0:T(8,128)(2,1)S(1)} %collective-permute-done.17), channel_id=1, source_target_pairs={{0,1},{1,0},{2,3},{3,2},{4,5},{5,4},{6,7},{7,6},{8,9},{9,8},{10,11... | collective-permute-start | bytes 2359304 | tf_op jit(solution)/shard_map/ppermute | solution.py:245
  363.0 20.5 %collective-permute-start.13 = (bf16[768,512]{1,0:T(8,128)(2,1)}, bf16[768,512]{1,0:T(8,128)(2,1)S(1)}, u32[]{:S(2)}, u32[]{:S(2)}) collective-permute-start(bf16[768,512]{1,0:T(8,128)(2,1)} %shard_map.91), channel_id=1, source_target_pairs={{0,1},{1,0},{2,3},{3,2},{4,5},{5,4},{6,7},{7,6},{8,9},{9,8},{10,11... | collective-permute-start | bytes 2359304 | tf_op jit(solution)/shard_map/ppermute | solution.py:245
  372.3 11.2 %collective-permute-start.15 = (bf16[768,512]{1,0:T(8,128)(2,1)S(1)}, bf16[768,512]{1,0:T(8,128)(2,1)S(1)}, u32[]{:S(2)}, u32[]{:S(2)}) collective-permute-start(bf16[768,512]{1,0:T(8,128)(2,1)S(1)} %collective-permute-done.14), channel_id=1, source_target_pairs={{0,1},{1,0},{2,3},{3,2},{4,5},{5,4},{6,7},{7,6},{8,9},{9,8},{10,11... | collective-permute-start | bytes 2359304 | tf_op jit(solution)/shard_map/ppermute | solution.py:245

commit v2 on v0

--- a/solution.py
+++ b/solution.py
@@ -14,31 +14,29 @@
 LANES = 128
 
 
-def filter_kernel(term_count, *refs):
+def filter_kernel(term_count, halo, *refs):
     fields = refs[: 3 * term_count]
     taps, medium, skip, out, raw, prod, shifted, smooth_q = refs[3 * term_count :]
-    ext = fields[0].shape[0]
-    local = ext - HALO
+    local = fields[0].shape[0]
+    ext = local + HALO
     taps_count = 7
     short_count = taps.shape[0] // 3
     for slot in range(3):
-        group = fields[slot * term_count : (slot + 1) * term_count]
-        total = group[0][0:8, :]
-        for term in group[1:]:
-            total = total + term[0:8, :]
-        raw[slot, 0:8, :] = total.astype(jnp.bfloat16).astype(jnp.float32)
+        raw[slot, 0:HALO, :] = halo[slot].astype(jnp.float32)
 
     def gather_body(index, carry):
-        row = pl.multiple_of(8 + index * CHUNK, 8)
+        row = pl.multiple_of(index * CHUNK, 8)
         for slot in range(3):
             group = fields[slot * term_count : (slot + 1) * term_count]
             total = group[0][pl.ds(row, CHUNK), :]
             for term in group[1:]:
                 total = total + term[pl.ds(row, CHUNK), :]
-            raw[slot, pl.ds(row, CHUNK), :] = total.astype(jnp.bfloat16).astype(jnp.float32)
-        return carry
-
-    lax.fori_loop(0, (ext - 8) // CHUNK, gather_body, 0)
+            raw[slot, pl.ds(row + HALO, CHUNK), :] = total.astype(jnp.bfloat16).astype(
+                jnp.float32
+            )
+        return carry
+
+    lax.fori_loop(0, local // CHUNK, gather_body, 0)
 
     def smooth(slot, row):
         window = raw[slot, pl.ds(row - 8, CHUNK + 8), :]
@@ -95,19 +93,20 @@
     lax.fori_loop(0, local // CHUNK, chunk_body, 0)
 
 
-def channel_filter(fields, taps, medium, skip, first, tiles):
+def channel_filter(halo, fields, taps, medium, skip, first, tiles):
     term_count = len(fields[0])
-    ext = fields[0][0].shape[0]
-    local = ext - HALO
+    local = fields[0][0].shape[0]
+    ext = local + HALO
     channels = tiles * LANES
 
     def field_spec(field):
-        return pl.BlockSpec((ext, LANES), lambda t: (0, first + t))
+        return pl.BlockSpec((local, LANES), lambda t: (0, first + t))
 
     return pl.pallas_call(
         functools.partial(filter_kernel, term_count),
         grid=(tiles,),
-        in_specs=[field_spec(0)] * (3 * term_count)
+        in_specs=[pl.BlockSpec((3, HALO, LANES), lambda t: (0, 0, t))]
+        + [field_spec(0)] * (3 * term_count)
         + [
             pl.BlockSpec((taps.shape[0], LANES), lambda t: (0, first + t)),
             pl.BlockSpec((medium.shape[0], LANES), lambda t: (0, first + t)),
@@ -121,7 +120,7 @@
             pltpu.VMEM((8, ext, LANES), jnp.float32),
             pltpu.VMEM((local, LANES), jnp.float32),
         ],
-    )(*[term for field in fields for term in field], taps, medium, skip)
+    )(halo, *[term for field in fields for term in field], taps, medium, skip)
 
 def ring_order(count):
     if count % 2:
@@ -273,10 +272,7 @@
     ctx_count = lax.axis_size("ctx")
     medium_count = medium_taps.shape[1]
     short_count = short_taps.shape[2]
-    earlier = halo_rows(tokens[row_count - HALO :])
-    earlier, in_weight = lax.optimization_barrier((earlier, in_weight))
-    widened = jnp.concatenate([earlier, tokens], axis=0)
-    features, weights = ring_projection(widened, in_weight, spread_weights(out_weight))
+    features, weights = ring_projection(tokens, in_weight, spread_weights(out_weight))
     lag_values = lax.broadcasted_iota(jnp.float32, (1, medium_count), 1)
     filters = medium_taps * jnp.exp(-medium_decay[:, None] * lag_values)
     taps = jnp.pad(
@@ -289,7 +285,15 @@
     skip = skip_gain.reshape(1, channel_count)
     total = None
     for part in range(parts):
-        gated = channel_filter(features, taps, medium, skip, part * share, share)
+        cols = slice(part * share * LANES, (part + 1) * share * LANES)
+        tail = jnp.stack(
+            [
+                sum(term[row_count - HALO :, cols] for term in field).astype(jnp.bfloat16)
+                for field in features
+            ]
+        )
+        halo = lax.ppermute(tail, "ctx", [(k, k + 1) for k in range(ctx_count - 1)])
+        gated = channel_filter(halo, features, taps, medium, skip, part * share, share)
         rows = slice(part * share * LANES, (part + 1) * share * LANES)
         piece = output_projection(gated, tuple(w[rows] for w in weights))
         total = piece if total is None else total + piece

time: 365 us -> 348 us (0.953)
  matrix products: 86.8 us -> 75.2 us
  waiting for transfers between devices: 163 us -> 155 us
  starting transfers between devices: 29.3 us -> 35.1 us
  local copies, waits for them, and re-layouts: 19 us -> 14.9 us
    ppermute x1, waiting for transfers between devices: 0.01 us -> 58.4 us  [ring_projection(): behind = lax.ppermute(in_weight, 'ctx', backward)]
    ppermute x1, waiting for transfers between devices: 40.3 us -> 0.01 us  [ring_projection(): ahead = lax.ppermute(in_weight, 'ctx', forward)]
    ppermute x2, waiting for transfers between devices: 84.4 us -> 44.8 us  [ring_step(): moved_ahead = lax.ppermute(ahead, 'ctx', forward)]
    ppermute x2, waiting for transfers between devices: 1.63 us -> 31.3 us  [ring_step(): moved_behind = lax.ppermute(behind, 'ctx', backward)]
    ppermute x1, waiting for transfers between devices: 3.96 us -> 19.1 us  [ring_projection(): last_ahead = lax.ppermute(ahead[:half], 'ctx', forward)]
    ppermute x3, waiting for transfers between devices: 13.4 us -> 0.01 us  [spread_weights(): weights.append(lax.ppermute(sent, 'tp', pairs))]
    ppermute x2, waiting for transfers between devices: 12.8 us -> 0.01 us  [per_device(): halo = lax.ppermute(tail, 'ctx', [(k, k + 1) for k in range(ctx_count - 1)])]
    dot_general x24, matrix products: 68.5 us -> 58 us  [product(): jnp.dot(cols, block[:, field, :], preferred_element_type=jnp.float32)]
  transfers between devices with their start and end apart: 19 -> 19, of which waited for: 10 -> 6; matrix products, arithmetic and copies ran while one was open for 25% -> 24% of each run, Pallas kernels for 7% -> 15%
where the time goes in v2:
time: 348 us; the launch traced here: 346 us
  waiting for transfers between devices  155 us (45%)
  matrix products  75.2 us (22%)
  Pallas kernels  52.4 us (15%)
  starting transfers between devices  35.1 us (10%)
  local copies, waits for them, and re-layouts  14.9 us (4%)
  between operations  10.9 us (3%)
    ppermute x1, waiting for transfers between devices, ring_projection(): behind = lax.ppermute(in_weight, 'ctx', backward)  58.4 us
    dot_general x24, matrix products, product(): jnp.dot(cols, block[:, field, :], preferred_element_type=jnp.float32)  58 us
    pallas_call x2, Pallas kernels, channel_filter(): pl.pallas_call(functools.partial(filter_kernel, term_count), grid=(tiles,...  52.4 us
    ppermute x2, waiting for transfers between devices, ring_step(): moved_ahead = lax.ppermute(ahead, 'ctx', forward)  44.8 us
    ppermute x2, waiting for transfers between devices, ring_step(): moved_behind = lax.ppermute(behind, 'ctx', backward)  31.3 us
    ppermute x6, starting transfers between devices, output_projection(): lax.ppermute(piece, 'tp', pairs)  19.8 us
    ppermute x1, waiting for transfers between devices, ring_projection(): last_ahead = lax.ppermute(ahead[:half], 'ctx', forward)  19.1 us
    dot_general x8, matrix products, output_projection(): jnp.dot(pieces[key], weights[key], preferred_element_type=jnp.float32)  17.2 us
  transfers between devices with their start and end apart: 19, of which 6 were waited for; matrix products, arithmetic and copies ran while one was open for 24% of the time, Pallas kernels for 15%

profile of v2, /device:TPU:1, one launch (start us, length us, event | category | flops | bytes accessed | tf_op | source)
XLA Modules:
  0.0 346.1 jit_solution(4810139442998080058)
XLA Ops:
  0.0 2.1 collective-permute-start.2
  2.1 7.0 %constant_dynamic-slice_fusion.2 = (bf16[1024,1024]{1,0:T(8,128)(2,1)}, bf16[1024,1024]{1,0:T(8,128)(2,1)}, bf16[1024,1024]{1,0:T(8,128)(2,1)}, bf16[1024,1024]{1,0:T(8,128)(2,1)}) fusion(bf16[1024,4096]{1,0:T(8,128)(2,1)} %param.15, s32[]{:T(128)S(6)} %select_n.119, s32[]{:T(128)S(6)} %select_n.117, s32[]{:T(128)S(6)} %select_n.116, s32[]{:T(128)S(6)} %select_n.118), kind=kLoop, calls=%fused_computation.154 | loop fusion | bytes 16777232 | tf_op jit(solution)/shard_map/dynamic_slice | solution.py:234
  9.2 2.5 collective-permute-start.6
  11.9 58.4 %collective-permute-done.2 = bf16[512,3,1024]{2,0,1:T(8,128)(2,1)} collective-permute-done((bf16[512,3,1024]{2,0,1:T(8,128)(2,1)}, bf16[512,3,1024]{2,0,1:T(8,128)(2,1)}, u32[]{:S(2)}, u32[]{:S(2)}) %collective-permute-start.2) | collective-permute-done | bytes 3145760 | tf_op jit(solution)/shard_map/ppermute | solution.py:182
  70.3 1.1 collective-permute-start.3
  71.7 4.2 %fusion.34 = f32[768,1024]{1,0:T(8,128)} fusion(bf16[512,3,1024]{2,0,1:T(8,128)(2,1)} %param.10, bf16[768,4096]{1,0:T(8,128)(2,1)} %param.9, s32[]{:T(128)S(6)} %select_n.108), kind=kOutput, calls=%fused_computation.50 | convolution fusion | flops 805306368 | bytes 4980740 | tf_op jit(solution)/shard_map/dot_general | solution.py:146
  83.9 2.6 fusion.30
  86.5 2.5 fusion.32
  89.0 2.2 fusion.9
  91.2 2.2 fusion.10
  93.5 2.2 fusion.11
  95.7 3.9 %add_add_fusion.3 = f32[768,1024]{1,0:T(8,128)} fusion(f32[768,1024]{1,0:T(8,128)S(1)} %fusion.30, f32[768,1024]{1,0:T(8,128)S(1)} %fusion.9, bf16[512,3,1024]{2,0,1:T(8,128)(2,1)} %collective-permute-done.2, bf16[768,4096]{1,0:T(8,128)(2,1)S(1)} %bitcast.122, s32[]{:T(128)S(6)} %select_n.115), kind=kOutput, calls=%fused_computation.4 | convolution fusion | flops 806879232 | bytes 11272196 | tf_op jit(solution)/shard_map/dot_general | solution.py:146
  99.6 4.1 %add_add_fusion.4 = f32[768,1024]{1,0:T(8,128)} fusion(f32[768,1024]{1,0:T(8,128)S(1)} %fusion.32, f32[768,1024]{1,0:T(8,128)S(1)} %fusion.10, bf16[512,3,1024]{2,0,1:T(8,128)(2,1)} %collective-permute-done.2, bf16[768,4096]{1,0:T(8,128)(2,1)S(1)} %bitcast.122, s32[]{:T(128)S(6)} %select_n.115), kind=kOutput, calls=%fused_computation.5 | convolution fusion | flops 806879232 | bytes 11272196 | tf_op jit(solution)/shard_map/dot_general | solution.py:146
  103.7 3.9 %add_add_fusion.5 = f32[768,1024]{1,0:T(8,128)} fusion(f32[768,1024]{1,0:T(8,128)S(1)} %copy-done.12, f32[768,1024]{1,0:T(8,128)S(1)} %fusion.11, bf16[512,3,1024]{2,0,1:T(8,128)(2,1)} %collective-permute-done.2, bf16[768,4096]{1,0:T(8,128)(2,1)S(1)} %bitcast.122, s32[]{:T(128)S(6)} %select_n.115), kind=kOutput, calls=%fused_computation.6 | convolution fusion | flops 806879232 | bytes 11272196 | tf_op jit(solution)/shard_map/dot_general | solution.py:146
  107.6 31.3 %collective-permute-done.3 = bf16[512,3,1024]{2,0,1:T(8,128)(2,1)} collective-permute-done((bf16[512,3,1024]{2,0,1:T(8,128)(2,1)}, bf16[512,3,1024]{2,0,1:T(8,128)(2,1)}, u32[]{:S(2)}, u32[]{:S(2)}) %collective-permute-start.3) | collective-permute-done | bytes 3145760 | tf_op jit(solution)/shard_map/ppermute | solution.py:175
  144.6 1.3 constant_dynamic-slice_fusion.1
  145.9 2.6 fusion.16
  148.6 2.5 fusion.22
  151.1 2.4 fusion.28
  153.4 2.4 add_add_fusion.refs_8_
  155.9 3.2 add_add_fusion.1.refs_4_
  159.2 3.0 add_add_fusion.2.refs_0_
  162.3 44.3 %collective-permute-done.7 = bf16[512,3,1024]{2,0,1:T(8,128)(2,1)} collective-permute-done((bf16[512,3,1024]{2,0,1:T(8,128)(2,1)}, bf16[512,3,1024]{2,0,1:T(8,128)(2,1)}, u32[]{:S(2)}, u32[]{:S(2)}) %collective-permute-start.7) | collective-permute-done | bytes 3145760 | tf_op jit(solution)/shard_map/while/body/eval_jaxpr/ppermute | solution.py:174
  206.6 1.5 slice.249
  208.1 1.1 collective-permute-start.9
  210.1 2.2 fusion.2.refs_9_
  212.3 3.0 fusion.5.refs_5_
  215.3 3.0 fusion.8.refs_1_
  218.3 1.0 fusion.1.refs_10_
  219.3 1.0 fusion.4.refs_6_
  220.3 1.0 fusion.7.refs_2_
  221.3 19.1 %collective-permute-done.9 = bf16[256,3,1024]{2,0,1:T(8,128)(2,1)S(1)} collective-permute-done((bf16[256,3,1024]{2,0,1:T(8,128)(2,1)S(1)}, bf16[256,3,1024]{2,0,1:T(8,128)(2,1)S(1)}, u32[]{:S(2)}, u32[]{:S(2)}) %collective-permute-start.9) | collective-permute-done | bytes 1572896 | tf_op jit(solution)/shard_map/ppermute | solution.py:194
  240.5 1.3 collective-permute-done.10
  242.0 1.0 fusion.refs_11_
  243.0 1.0 fusion.3.refs_7_
  246.8 2.1 collective-permute-start.11
  249.6 3.7 %collective-permute-start.15 = (bf16[3,136,512]{2,1,0:T(8,128)(2,1)}, bf16[3,136,512]{2,1,0:T(8,128)(2,1)S(1)}, u32[]{:S(2)}, u32[]{:S(2)}) collective-permute-start(bf16[3,136,512]{2,1,0:T(8,128)(2,1)} %pad_maximum_fusion.2), channel_id=1, source_target_pairs={{0,4},{4,8},{8,12},{12,16},{16,20},{20,24},{24,28},{1,5},{5,9},{9,... | collective-permute-start | bytes 1253384 | tf_op jit(solution)/shard_map/ppermute | solution.py:295
  255.9 26.2 %shard_map.91 = bf16[768,512]{1,0:T(8,128)(2,1)} custom-call(bf16[3,136,512]{2,1,0:T(8,128)(2,1)} %copy-done.21, f32[768,1024]{1,0:T(8,128)} %copy-done.2, f32[768,1024]{1,0:T(8,128)} %copy-done.5, f32[768,1024]{1,0:T(8,128)} %copy-done.8, f32[768,1024]{1,0:T(8,128)} %copy-done.11, f32[768,1024]{1,0:T(8,128)} %copy-done.1, f32[768,1024]{1,0:T(8,128)} %copy-done.4, ...), custom_call_target="tpu_custom_call" | custom-call | tf_op jit(solution)/shard_map/pallas_call | solution.py:105
  282.1 1.3 collective-permute-start.13
  284.1 26.2 %shard_map.92 = bf16[768,512]{1,0:T(8,128)(2,1)} custom-call(bf16[3,136,512]{2,1,0:T(8,128)(2,1)} %copy-done.20, f32[768,1024]{1,0:T(8,128)} %copy-done.2, f32[768,1024]{1,0:T(8,128)} %copy-done.5, f32[768,1024]{1,0:T(8,128)} %copy-done.8, f32[768,1024]{1,0:T(8,128)} %copy-done.11, f32[768,1024]{1,0:T(8,128)} %copy-done.1, f32[768,1024]{1,0:T(8,128)} %copy-done.4, ...), custom_call_target="tpu_custom_call" | custom-call | tf_op jit(solution)/shard_map/pallas_call | solution.py:105
  310.7 8.6 %collective-permute-start.12 = (bf16[768,512]{1,0:T(8,128)(2,1)S(1)}, bf16[768,512]{1,0:T(8,128)(2,1)S(1)}, u32[]{:S(2)}, u32[]{:S(2)}) collective-permute-start(bf16[768,512]{1,0:T(8,128)(2,1)S(1)} %copy-done.17), channel_id=1, source_target_pairs={{0,1},{1,0},{2,3},{3,2},{4,5},{5,4},{6,7},{7,6},{8,9},{9,8},{10,11... | collective-permute-start | bytes 2359304 | tf_op jit(solution)/shard_map/ppermute | solution.py:244
  321.8 9.1 %collective-permute-start.18 = (bf16[768,512]{1,0:T(8,128)(2,1)S(1)}, bf16[768,512]{1,0:T(8,128)(2,1)S(1)}, u32[]{:S(2)}, u32[]{:S(2)}) collective-permute-start(bf16[768,512]{1,0:T(8,128)(2,1)S(1)} %collective-permute-done.17), channel_id=1, source_target_pairs={{0,1},{1,0},{2,3},{3,2},{4,5},{5,4},{6,7},{7,6},{8,9},{9,8},{10,11... | collective-permute-start | bytes 2359304 | tf_op jit(solution)/shard_map/ppermute | solution.py:244
  330.9 2.2 fusion.37
  333.1 2.4 fusion.45
  335.5 2.2 fusion.39
  337.8 2.2 fusion.47
  340.0 2.2 fusion.43
  342.2 3.9 %add_convert_fusion = bf16[768,1024]{1,0:T(8,128)(2,1)} fusion(f32[768,1024]{1,0:T(8,128)S(1)} %fusion.37, f32[768,1024]{1,0:T(8,128)S(1)} %fusion.41, f32[768,1024]{1,0:T(8,128)S(1)} %fusion.39, f32[768,1024]{1,0:T(8,128)S(1)} %fusion.43, f32[768,1024]{1,0:T(8,128)S(1)} %fusion.45, f32[768,1024]{1,0:T(8,128)S(1)} %fusion.49, f32[768,1024]{1,0:T(8,128)S(1)} %fusion.47, ...), kind=kOutput, calls=%fused_computation | convolution fusion | flops 811597824 | bytes 25427968 | tf_op jit(solution)/shard_map/dot_general | solution.py:248
  (102 shorter events, 14.8 us)
Async XLA Ops:
  0.0 70.3 %collective-permute-start.2 = (bf16[512,3,1024]{2,0,1:T(8,128)(2,1)}, bf16[512,3,1024]{2,0,1:T(8,128)(2,1)}, u32[]{:S(2)}, u32[]{:S(2)}) collective-permute-start(bf16[512,3,1024]{2,0,1:T(8,128)(2,1)} %param.10), channel_id=1, source_target_pairs={{0,4},{8,0},{16,8},{24,16},{28,24},{20,28},{12,20},{4,12},{1,5},{9... | collective-permute-start | bytes 9437192 | tf_op jit(solution)/shard_map/ppermute | solution.py:182
  2.1 69.3 %collective-permute-start = (bf16[512,3,1024]{2,0,1:T(8,128)(2,1)}, bf16[512,3,1024]{2,0,1:T(8,128)(2,1)}, u32[]{:S(2)}, u32[]{:S(2)}) collective-permute-start(bf16[512,3,1024]{2,0,1:T(8,128)(2,1)} %param.10), channel_id=1, source_target_pairs={{0,8},{8,16},{16,24},{24,28},{28,20},{20,12},{12,4},{4,0},{1,9},{9... | collective-permute-start | bytes 9437192 | tf_op jit(solution)/shard_map/ppermute | solution.py:181
  9.2 66.8 %copy-start.25 = (s32[8]{0:T(128)S(1)}, s32[8]{0:T(128)}, u32[]{:S(2)}) copy-start(s32[8]{0:T(128)} %constant.118.clone) | copy-start | bytes 100
  9.2 72.7 %copy-start.23 = (s32[8]{0:T(128)S(1)}, s32[8]{0:T(128)}, u32[]{:S(2)}) copy-start(s32[8]{0:T(128)} %constant.117.clone) | copy-start | bytes 100
  9.2 98.4 %collective-permute-start.6 = (bf16[1024,1024]{1,0:T(8,128)(2,1)}, bf16[1024,1024]{1,0:T(8,128)(2,1)}, u32[]{:S(2)}, u32[]{:S(2)}) collective-permute-start(bf16[1024,1024]{1,0:T(8,128)(2,1)} %get-tuple-element.59), channel_id=1, source_target_pairs={{0,3},{1,2},{2,1},{3,0},{4,7},{5,6},{6,5},{7,4},{8,11},{9,10},{10,... | collective-permute-start | bytes 6291464 | tf_op jit(solution)/shard_map/ppermute | solution.py:235
  11.7 95.9 %collective-permute-start.4 = (bf16[1024,1024]{1,0:T(8,128)(2,1)}, bf16[1024,1024]{1,0:T(8,128)(2,1)}, u32[]{:S(2)}, u32[]{:S(2)}) collective-permute-start(bf16[1024,1024]{1,0:T(8,128)(2,1)} %get-tuple-element.60), channel_id=1, source_target_pairs={{0,1},{1,0},{2,3},{3,2},{4,5},{5,4},{6,7},{7,6},{8,9},{9,8},{10,11... | collective-permute-start | bytes 6291464 | tf_op jit(solution)/shard_map/ppermute | solution.py:235
  11.7 95.9 %collective-permute-start.5 = (bf16[1024,1024]{1,0:T(8,128)(2,1)}, bf16[1024,1024]{1,0:T(8,128)(2,1)}, u32[]{:S(2)}, u32[]{:S(2)}) collective-permute-start(bf16[1024,1024]{1,0:T(8,128)(2,1)} %get-tuple-element.62), channel_id=1, source_target_pairs={{0,2},{1,3},{2,0},{3,1},{4,6},{5,7},{6,4},{7,5},{8,10},{9,11},{10,... | collective-permute-start | bytes 6291464 | tf_op jit(solution)/shard_map/ppermute | solution.py:235
  70.3 68.7 %collective-permute-start.3 = (bf16[512,3,1024]{2,0,1:T(8,128)(2,1)}, bf16[512,3,1024]{2,0,1:T(8,128)(2,1)}, u32[]{:S(2)}, u32[]{:S(2)}) collective-permute-start(bf16[512,3,1024]{2,0,1:T(8,128)(2,1)} %collective-permute-done.2), channel_id=1, source_target_pairs={{0,4},{8,0},{16,8},{24,16},{28,24},{20,28},{12,20},{4,12},{1,5},{9... | collective-permute-start | bytes 9437192 | tf_op jit(solution)/shard_map/ppermute | solution.py:175
  71.4 68.1 %collective-permute-start.1 = (bf16[512,3,1024]{2,0,1:T(8,128)(2,1)}, bf16[512,3,1024]{2,0,1:T(8,128)(2,1)}, u32[]{:S(2)}, u32[]{:S(2)}) collective-permute-start(bf16[512,3,1024]{2,0,1:T(8,128)(2,1)} %collective-permute-done), channel_id=1, source_target_pairs={{0,8},{8,16},{16,24},{24,28},{28,20},{20,12},{12,4},{4,0},{1,9},{9... | collective-permute-start | bytes 9437192 | tf_op jit(solution)/shard_map/ppermute | solution.py:174
  71.7 17.3 %slice-start = ((s8[6291456]{0:T(1024)(128)(4,1)}), s8[2097152]{0:T(1024)(128)(4,1)S(1)}, s32[]{:S(2)}) async-start(s8[6291456]{0:T(1024)(128)(4,1)} %bitcast.121), calls=%async_computation | async-start | bytes 4194304
  83.9 5.1 %slice-start.1 = ((s8[6291456]{0:T(1024)(128)(4,1)}), s8[4194304]{0:T(1024)(128)(4,1)S(1)}, s32[]{:S(2)}) async-start(s8[6291456]{0:T(1024)(128)(4,1)} %bitcast.121), calls=%async_computation.1 | async-start | bytes 8388608
  99.6 4.1 %copy-start.12 = (f32[768,1024]{1,0:T(8,128)S(1)}, f32[768,1024]{1,0:T(8,128)}, u32[]{:S(2)}) copy-start(f32[768,1024]{1,0:T(8,128)} %fusion.34) | copy-start | bytes 9437188
  139.4 67.2 %collective-permute-start.7 = (bf16[512,3,1024]{2,0,1:T(8,128)(2,1)}, bf16[512,3,1024]{2,0,1:T(8,128)(2,1)}, u32[]{:S(2)}, u32[]{:S(2)}) collective-permute-start(bf16[512,3,1024]{2,0,1:T(8,128)(2,1)} %collective-permute-done.1), channel_id=1, source_target_pairs={{0,8},{8,16},{16,24},{24,28},{28,20},{20,12},{12,4},{4,0},{1,9},{9... | collective-permute-start | bytes 9437192 | tf_op jit(solution)/shard_map/while/body/eval_jaxpr/ppermute | solution.py:174
  140.1 69.1 %collective-permute-start.8 = (bf16[512,3,1024]{2,0,1:T(8,128)(2,1)}, bf16[512,3,1024]{2,0,1:T(8,128)(2,1)S(1)}, u32[]{:S(2)}, u32[]{:S(2)}) collective-permute-start(bf16[512,3,1024]{2,0,1:T(8,128)(2,1)} %collective-permute-done.3), channel_id=1, source_target_pairs={{0,4},{8,0},{16,8},{24,16},{28,24},{20,28},{12,20},{4,12},{1,5},{9... | collective-permute-start | bytes 9437192 | tf_op jit(solution)/shard_map/while/body/eval_jaxpr/ppermute | solution.py:175
  144.6 6.4 %slice-start.2 = ((s8[6291456]{0:T(1024)(128)(4,1)}), s8[4194304]{0:T(1024)(128)(4,1)S(1)}, s32[]{:S(2)}) async-start(s8[6291456]{0:T(1024)(128)(4,1)} %bitcast.123), calls=%async_computation.2 | async-start | bytes 8388608
  145.9 5.1 %slice-start.3 = ((s8[6291456]{0:T(1024)(128)(4,1)}), s8[2097152]{0:T(1024)(128)(4,1)S(1)}, s32[]{:S(2)}) async-start(s8[6291456]{0:T(1024)(128)(4,1)} %bitcast.123), calls=%async_computation.3 | async-start | bytes 4194304
  151.0 2.4 copy-start.13
  153.4 2.4 copy-start.14
  155.9 89.1 %copy-start = (f32[768,1024]{1,0:T(8,128)}, f32[768,1024]{1,0:T(8,128)S(1)}, u32[]{:S(2)}) copy-start(f32[768,1024]{1,0:T(8,128)S(1)} %add_add_fusion.refs_8_) | copy-start | bytes 9437188
  155.9 3.3 copy-start.15
  159.2 86.0 %copy-start.1 = (f32[768,1024]{1,0:T(8,128)}, f32[768,1024]{1,0:T(8,128)S(1)}, u32[]{:S(2)}) copy-start(f32[768,1024]{1,0:T(8,128)S(1)} %add_add_fusion.1.refs_4_) | copy-start | bytes 9437188
  162.2 83.0 %copy-start.2 = (f32[768,1024]{1,0:T(8,128)}, f32[768,1024]{1,0:T(8,128)S(1)}, u32[]{:S(2)}) copy-start(f32[768,1024]{1,0:T(8,128)S(1)} %add_add_fusion.2.refs_0_) | copy-start | bytes 9437188
  208.1 32.3 %collective-permute-start.9 = (bf16[256,3,1024]{2,0,1:T(8,128)(2,1)S(1)}, bf16[256,3,1024]{2,0,1:T(8,128)(2,1)S(1)}, u32[]{:S(2)}, u32[]{:S(2)}) collective-permute-start(bf16[256,3,1024]{2,0,1:T(8,128)(2,1)S(1)} %slice.249), channel_id=1, source_target_pairs={{0,8},{8,16},{16,24},{24,28},{28,20},{20,12},{12,4},{4,0},{1,9},{9... | collective-permute-start | bytes 4718600 | tf_op jit(solution)/shard_map/ppermute | solution.py:194
  209.3 32.5 %collective-permute-start.10 = (bf16[256,3,1024]{2,0,1:T(8,128)(2,1)S(1)}, bf16[256,3,1024]{2,0,1:T(8,128)(2,1)S(1)}, u32[]{:S(2)}, u32[]{:S(2)}) collective-permute-start(bf16[256,3,1024]{2,0,1:T(8,128)(2,1)S(1)} %slice.250), channel_id=1, source_target_pairs={{0,4},{8,0},{16,8},{24,16},{28,24},{20,28},{12,20},{4,12},{1,5},{9... | collective-permute-start | bytes 4718600 | tf_op jit(solution)/shard_map/ppermute | solution.py:195
  212.3 32.7 %copy-start.3 = (f32[768,1024]{1,0:T(8,128)}, f32[768,1024]{1,0:T(8,128)S(1)}, u32[]{:S(2)}) copy-start(f32[768,1024]{1,0:T(8,128)S(1)} %fusion.2.refs_9_) | copy-start | bytes 9437188
  215.3 30.0 %copy-start.4 = (f32[768,1024]{1,0:T(8,128)}, f32[768,1024]{1,0:T(8,128)S(1)}, u32[]{:S(2)}) copy-start(f32[768,1024]{1,0:T(8,128)S(1)} %fusion.5.refs_5_) | copy-start | bytes 9437188
  218.3 27.0 %copy-start.5 = (f32[768,1024]{1,0:T(8,128)}, f32[768,1024]{1,0:T(8,128)S(1)}, u32[]{:S(2)}) copy-start(f32[768,1024]{1,0:T(8,128)S(1)} %fusion.8.refs_1_) | copy-start | bytes 9437188
  219.3 25.7 %copy-start.6 = (f32[768,1024]{1,0:T(8,128)}, f32[768,1024]{1,0:T(8,128)S(1)}, u32[]{:S(2)}) copy-start(f32[768,1024]{1,0:T(8,128)S(1)} %fusion.1.refs_10_) | copy-start | bytes 9437188
  220.3 25.0 %copy-start.7 = (f32[768,1024]{1,0:T(8,128)}, f32[768,1024]{1,0:T(8,128)S(1)}, u32[]{:S(2)}) copy-start(f32[768,1024]{1,0:T(8,128)S(1)} %fusion.4.refs_6_) | copy-start | bytes 9437188
  221.3 24.0 %copy-start.8 = (f32[768,1024]{1,0:T(8,128)}, f32[768,1024]{1,0:T(8,128)S(1)}, u32[]{:S(2)}) copy-start(f32[768,1024]{1,0:T(8,128)S(1)} %fusion.7.refs_2_) | copy-start | bytes 9437188
  243.0 2.0 copy-start.9
  244.0 1.7 copy-start.10
  245.0 1.7 copy-start.11
  245.6 7.8 %copy-start.24 = (f32[1024]{0:T(1024)S(1)}, f32[1024]{0:T(1024)}, u32[]{:S(2)}) copy-start(f32[1024]{0:T(1024)} %param.13) | copy-start | bytes 12292
  245.6 7.8 %copy-start.19 = (f32[1024,128]{1,0:T(8,128)S(1)}, f32[1024,128]{1,0:T(8,128)}, u32[]{:S(2)}) copy-start(f32[1024,128]{1,0:T(8,128)} %param.12) | copy-start | bytes 1572868
  245.6 8.0 %copy-start.22 = (f32[3,1024,7]{1,2,0:T(8,128)S(1)}, f32[3,1024,7]{1,2,0:T(8,128)}, u32[]{:S(2)}) copy-start(f32[3,1024,7]{1,2,0:T(8,128)} %param.11) | copy-start | bytes 258052
  246.8 8.4 %collective-permute-start.11 = (bf16[3,136,512]{2,1,0:T(8,128)(2,1)S(1)}, bf16[3,136,512]{2,1,0:T(8,128)(2,1)S(1)}, u32[]{:S(2)}, u32[]{:S(2)}) collective-permute-start(bf16[3,136,512]{2,1,0:T(8,128)(2,1)S(1)} %pad_maximum_fusion.1), channel_id=1, source_target_pairs={{0,4},{4,8},{8,12},{12,16},{16,20},{20,24},{24,28},{1,5},{5,9},{9,... | collective-permute-start | bytes 1253384 | tf_op jit(solution)/shard_map/ppermute | solution.py:295
  249.6 33.7 %collective-permute-start.15 = (bf16[3,136,512]{2,1,0:T(8,128)(2,1)}, bf16[3,136,512]{2,1,0:T(8,128)(2,1)S(1)}, u32[]{:S(2)}, u32[]{:S(2)}) collective-permute-start(bf16[3,136,512]{2,1,0:T(8,128)(2,1)} %pad_maximum_fusion.2), channel_id=1, source_target_pairs={{0,4},{4,8},{8,12},{12,16},{16,20},{20,24},{24,28},{1,5},{5,9},{9,... | collective-permute-start | bytes 1253384 | tf_op jit(solution)/shard_map/ppermute | solution.py:295
  282.1 28.6 %copy-start.17 = (bf16[768,512]{1,0:T(8,128)(2,1)S(1)}, bf16[768,512]{1,0:T(8,128)(2,1)}, u32[]{:S(2)}) copy-start(bf16[768,512]{1,0:T(8,128)(2,1)} %shard_map.91) | copy-start | bytes 2359300
  282.1 37.1 %copy-start.16 = (bf16[1024,1024]{1,0:T(8,128)(2,1)S(1)}, bf16[1024,1024]{1,0:T(8,128)(2,1)}, u32[]{:S(2)}) copy-start(bf16[1024,1024]{1,0:T(8,128)(2,1)} %get-tuple-element.49) | copy-start | bytes 6291460
  282.1 39.1 %collective-permute-start.13 = (bf16[768,512]{1,0:T(8,128)(2,1)}, bf16[768,512]{1,0:T(8,128)(2,1)}, u32[]{:S(2)}, u32[]{:S(2)}) collective-permute-start(bf16[768,512]{1,0:T(8,128)(2,1)} %shard_map.91), channel_id=1, source_target_pairs={{0,2},{1,3},{2,0},{3,1},{4,6},{5,7},{6,4},{7,5},{8,10},{9,11},{10,... | collective-permute-start | bytes 2359304 | tf_op jit(solution)/shard_map/ppermute | solution.py:244
  283.4 0.8 copy-start.20
  310.3 9.9 %copy-start.18 = (bf16[768,512]{1,0:T(8,128)(2,1)S(1)}, bf16[768,512]{1,0:T(8,128)(2,1)}, u32[]{:S(2)}) copy-start(bf16[768,512]{1,0:T(8,128)(2,1)} %shard_map.92) | copy-start | bytes 2359300
  310.3 11.4 %collective-permute-start.17 = (bf16[768,512]{1,0:T(8,128)(2,1)}, bf16[768,512]{1,0:T(8,128)(2,1)S(1)}, u32[]{:S(2)}, u32[]{:S(2)}) collective-permute-start(bf16[768,512]{1,0:T(8,128)(2,1)} %shard_map.92), channel_id=1, source_target_pairs={{0,2},{1,3},{2,0},{3,1},{4,6},{5,7},{6,4},{7,5},{8,10},{9,11},{10,... | collective-permute-start | bytes 2359304 | tf_op jit(solution)/shard_map/ppermute | solution.py:244
  310.7 27.1 %collective-permute-start.12 = (bf16[768,512]{1,0:T(8,128)(2,1)S(1)}, bf16[768,512]{1,0:T(8,128)(2,1)S(1)}, u32[]{:S(2)}, u32[]{:S(2)}) collective-permute-start(bf16[768,512]{1,0:T(8,128)(2,1)S(1)} %copy-done.17), channel_id=1, source_target_pairs={{0,1},{1,0},{2,3},{3,2},{4,5},{5,4},{6,7},{7,6},{8,9},{9,8},{10,11... | collective-permute-start | bytes 2359304 | tf_op jit(solution)/shard_map/ppermute | solution.py:244
  319.2 16.3 %collective-permute-start.16 = (bf16[768,512]{1,0:T(8,128)(2,1)}, bf16[768,512]{1,0:T(8,128)(2,1)S(1)}, u32[]{:S(2)}, u32[]{:S(2)}) collective-permute-start(bf16[768,512]{1,0:T(8,128)(2,1)} %shard_map.92), channel_id=1, source_target_pairs={{0,1},{1,0},{2,3},{3,2},{4,5},{5,4},{6,7},{7,6},{8,9},{9,8},{10,11... | collective-permute-start | bytes 2359304 | tf_op jit(solution)/shard_map/ppermute | solution.py:244
  321.2 18.8 %collective-permute-start.14 = (bf16[768,512]{1,0:T(8,128)(2,1)}, bf16[768,512]{1,0:T(8,128)(2,1)S(1)}, u32[]{:S(2)}, u32[]{:S(2)}) collective-permute-start(bf16[768,512]{1,0:T(8,128)(2,1)} %collective-permute-done.13), channel_id=1, source_target_pairs={{0,1},{1,0},{2,3},{3,2},{4,5},{5,4},{6,7},{7,6},{8,9},{9,8},{10,11... | collective-permute-start | bytes 2359304 | tf_op jit(solution)/shard_map/ppermute | solution.py:244
  321.8 20.4 %collective-permute-start.18 = (bf16[768,512]{1,0:T(8,128)(2,1)S(1)}, bf16[768,512]{1,0:T(8,128)(2,1)S(1)}, u32[]{:S(2)}, u32[]{:S(2)}) collective-permute-start(bf16[768,512]{1,0:T(8,128)(2,1)S(1)} %collective-permute-done.17), channel_id=1, source_target_pairs={{0,1},{1,0},{2,3},{3,2},{4,5},{5,4},{6,7},{7,6},{8,9},{9,8},{10,11... | collective-permute-start | bytes 2359304 | tf_op jit(solution)/shard_map/ppermute | solution.py:244
  (1 other events, 0.7 us)

commit v3 on v2

--- a/solution.py
+++ b/solution.py
@@ -95,18 +95,18 @@
 
 def channel_filter(halo, fields, taps, medium, skip, first, tiles):
     term_count = len(fields[0])
-    local = fields[0][0].shape[0]
+    local = fields[0][0][0].shape[0]
     ext = local + HALO
     channels = tiles * LANES
 
-    def field_spec(field):
-        return pl.BlockSpec((local, LANES), lambda t: (0, first + t))
+    def field_spec(shift):
+        return pl.BlockSpec((local, LANES), lambda t: (0, shift + t))
 
     return pl.pallas_call(
         functools.partial(filter_kernel, term_count),
         grid=(tiles,),
         in_specs=[pl.BlockSpec((3, HALO, LANES), lambda t: (0, 0, t))]
-        + [field_spec(0)] * (3 * term_count)
+        + [field_spec(shift) for field in fields for _, shift in field]
         + [
             pl.BlockSpec((taps.shape[0], LANES), lambda t: (0, first + t)),
             pl.BlockSpec((medium.shape[0], LANES), lambda t: (0, first + t)),
@@ -120,7 +120,7 @@
             pltpu.VMEM((8, ext, LANES), jnp.float32),
             pltpu.VMEM((local, LANES), jnp.float32),
         ],
-    )(halo, *[term for field in fields for term in field], taps, medium, skip)
+    )(halo, *[term for field in fields for term, _ in field], taps, medium, skip)
 
 def ring_order(count):
     if count % 2:
@@ -128,7 +128,7 @@
     return list(range(0, count, 2)) + list(range(count - 1, 0, -2))
 
 
-def ring_projection(tokens, in_weight, riders):
+def ring_projection(tokens, in_weight, riders, parts):
     count = lax.axis_size("ctx")
     rows = in_weight.shape[0]
     order = ring_order(count)
@@ -177,7 +177,7 @@
         return (moved_ahead, moved_behind, total)
 
     if full_steps == 0:
-        return tuple((part,) for part in total), riders
+        return tuple(((part, None),) for part in total), riders, None
     ahead = lax.ppermute(in_weight, "ctx", forward)
     behind = lax.ppermute(in_weight, "ctx", backward)
     carry = (ahead, behind, total)
@@ -205,14 +205,20 @@
             axis=1,
         )
         block = jnp.concatenate([last_ahead, last_behind], axis=0)
-        last_terms = product(cols, block)
-        terms = tuple(zip(total, first_terms, second_terms, last_terms))
+        terms = tuple(
+            tuple((term, None) for term in group)
+            for group in zip(total, first_terms, second_terms)
+        )
+        return terms, riders, (cols, block)
     else:
         from_behind_full, from_ahead_full = sources(full_steps)
         first_terms = partial(ahead, from_behind_full, 0, rows)
         second_terms = partial(behind, from_ahead_full, 0, rows)
-        terms = tuple(zip(total, first_terms, second_terms))
-    return terms, riders
+        terms = tuple(
+            tuple((term, None) for term in group)
+            for group in zip(total, first_terms, second_terms)
+        )
+    return terms, riders, None
 
 
 def tp_bits(count):
@@ -272,7 +278,6 @@
     ctx_count = lax.axis_size("ctx")
     medium_count = medium_taps.shape[1]
     short_count = short_taps.shape[2]
-    features, weights = ring_projection(tokens, in_weight, spread_weights(out_weight))
     lag_values = lax.broadcasted_iota(jnp.float32, (1, medium_count), 1)
     filters = medium_taps * jnp.exp(-medium_decay[:, None] * lag_values)
     taps = jnp.pad(
@@ -282,18 +287,42 @@
     parts = 2 if tiles % 2 == 0 else 1
     share = tiles // parts
     medium = jnp.transpose(filters)
+    features, weights, last = ring_projection(tokens, in_weight, spread_weights(out_weight), parts)
+    tail = None
     skip = skip_gain.reshape(1, channel_count)
     total = None
     for part in range(parts):
         cols = slice(part * share * LANES, (part + 1) * share * LANES)
+        chosen = tuple(tuple((term, part * share) for term, _ in field) for field in features)
+        if last is not None:
+            cols_in, block = last
+            if tail is not None:
+                cols_in, block, _ = lax.optimization_barrier((cols_in, block, tail))
+            chosen = tuple(
+                field
+                + (
+                    (
+                        jnp.dot(
+                            cols_in,
+                            block[:, index, cols],
+                            preferred_element_type=jnp.float32,
+                        ),
+                        0,
+                    ),
+                )
+                for index, field in enumerate(chosen)
+            )
         tail = jnp.stack(
             [
-                sum(term[row_count - HALO :, cols] for term in field).astype(jnp.bfloat16)
-                for field in features
+                sum(
+                    term[row_count - HALO :, cols] if shift else term[row_count - HALO :, : cols.stop - cols.start]
+                    for term, shift in field
+                ).astype(jnp.bfloat16)
+                for field in chosen
             ]
         )
         halo = lax.ppermute(tail, "ctx", [(k, k + 1) for k in range(ctx_count - 1)])
-        gated = channel_filter(halo, features, taps, medium, skip, part * share, share)
+        gated = channel_filter(halo, chosen, taps, medium, skip, part * share, share)
         rows = slice(part * share * LANES, (part + 1) * share * LANES)
         piece = output_projection(gated, tuple(w[rows] for w in weights))
         total = piece if total is None else total + piece

time: 348 us -> 347 us (level)
  starting transfers between devices: 35.1 us -> 29.7 us
  waiting for transfers between devices: 155 us -> 159 us
    ppermute x6, starting transfers between devices: 19.8 us -> 14.6 us  [output_projection(): lax.ppermute(piece, 'tp', pairs)]
    ppermute x6, waiting for transfers between devices: 0.02 us -> 3.82 us  [output_projection(): lax.ppermute(piece, 'tp', pairs)]
    dot_general x24 -> x21, matrix products: 58 us -> 55.1 us  [product(): jnp.dot(cols, block[:, field, :], preferred_element_type=jnp.float32)]
  transfers between devices with their start and end apart: 19 -> 19, of which waited for: 6 -> 7; matrix products, arithmetic and copies ran while one was open for 24% -> 25% of each run, Pallas kernels for 15% -> 15%
where the time goes in v3:
time: 347 us; the launch traced here: 346 us
  waiting for transfers between devices  159 us (46%)
  matrix products  76.8 us (22%)
  Pallas kernels  52.4 us (15%)
  starting transfers between devices  29.7 us (9%)
  local copies, waits for them, and re-layouts  14.2 us (4%)
  between operations  11.3 us (3%)
    ppermute x1, waiting for transfers between devices, ring_projection(): behind = lax.ppermute(in_weight, 'ctx', backward)  58.5 us
    dot_general x21, matrix products, product(): jnp.dot(cols, block[:, field, :], preferred_element_type=jnp.float32)  55.1 us
    pallas_call x2, Pallas kernels, channel_filter(): pl.pallas_call(functools.partial(filter_kernel, term_count), grid=(tiles,...  52.4 us
    ppermute x2, waiting for transfers between devices, ring_step(): moved_ahead = lax.ppermute(ahead, 'ctx', forward)  44.7 us
    ppermute x2, waiting for transfers between devices, ring_step(): moved_behind = lax.ppermute(behind, 'ctx', backward)  31.3 us
    ppermute x1, waiting for transfers between devices, ring_projection(): last_ahead = lax.ppermute(ahead[:half], 'ctx', forward)  19.3 us
    dot_general x8, matrix products, output_projection(): jnp.dot(pieces[key], weights[key], preferred_element_type=jnp.float32)  18.3 us
    ppermute x6, starting transfers between devices, output_projection(): lax.ppermute(piece, 'tp', pairs)  14.6 us
  transfers between devices with their start and end apart: 19, of which 7 were waited for; matrix products, arithmetic and copies ran while one was open for 25% of the time, Pallas kernels for 15%

profile of v3, /device:TPU:1, one launch (start us, length us, event | category | flops | bytes accessed | tf_op | source)
XLA Modules:
  0.0 345.6 jit_solution(6032611714262997441)
XLA Ops:
  0.0 2.1 collective-permute-start.2
  2.1 6.9 %constant_dynamic-slice_fusion.2 = (bf16[1024,1024]{1,0:T(8,128)(2,1)}, bf16[1024,1024]{1,0:T(8,128)(2,1)}, bf16[1024,1024]{1,0:T(8,128)(2,1)}, bf16[1024,1024]{1,0:T(8,128)(2,1)}) fusion(bf16[1024,4096]{1,0:T(8,128)(2,1)} %param.15, s32[]{:T(128)S(6)} %select_n.119, s32[]{:T(128)S(6)} %select_n.117, s32[]{:T(128)S(6)} %select_n.116, s32[]{:T(128)S(6)} %select_n.118), kind=kLoop, calls=%fused_computation.163 | loop fusion | bytes 16777232 | tf_op jit(solution)/shard_map/dynamic_slice | solution.py:240
  9.1 2.5 collective-permute-start.6
  11.8 58.5 %collective-permute-done.2 = bf16[512,3,1024]{2,0,1:T(8,128)(2,1)} collective-permute-done((bf16[512,3,1024]{2,0,1:T(8,128)(2,1)}, bf16[512,3,1024]{2,0,1:T(8,128)(2,1)}, u32[]{:S(2)}, u32[]{:S(2)}) %collective-permute-start.2) | collective-permute-done | bytes 3145760 | tf_op jit(solution)/shard_map/ppermute | solution.py:182
  70.3 1.1 collective-permute-start.3
  71.7 4.2 %fusion.31 = f32[768,1024]{1,0:T(8,128)} fusion(bf16[512,3,1024]{2,0,1:T(8,128)(2,1)} %param.10, bf16[768,4096]{1,0:T(8,128)(2,1)} %param.9, s32[]{:T(128)S(6)} %select_n.108), kind=kOutput, calls=%fused_computation.44 | convolution fusion | flops 805306368 | bytes 4980740 | tf_op jit(solution)/shard_map/dot_general | solution.py:146
  83.9 2.6 fusion.27
  86.5 2.5 fusion.29
  89.0 2.2 fusion.6
  91.2 2.2 fusion.7
  93.4 2.2 fusion.8
  95.7 4.0 %add_add_fusion.3 = f32[768,1024]{1,0:T(8,128)} fusion(f32[768,1024]{1,0:T(8,128)S(1)} %fusion.27, f32[768,1024]{1,0:T(8,128)S(1)} %fusion.6, bf16[512,3,1024]{2,0,1:T(8,128)(2,1)} %collective-permute-done.2, bf16[768,4096]{1,0:T(8,128)(2,1)S(1)} %bitcast.134, s32[]{:T(128)S(6)} %select_n.115), kind=kOutput, calls=%fused_computation.4 | convolution fusion | flops 806879232 | bytes 11272196 | tf_op jit(solution)/shard_map/dot_general | solution.py:146
  99.6 4.1 %add_add_fusion.4 = f32[768,1024]{1,0:T(8,128)} fusion(f32[768,1024]{1,0:T(8,128)S(1)} %fusion.29, f32[768,1024]{1,0:T(8,128)S(1)} %fusion.7, bf16[512,3,1024]{2,0,1:T(8,128)(2,1)} %collective-permute-done.2, bf16[768,4096]{1,0:T(8,128)(2,1)S(1)} %bitcast.134, s32[]{:T(128)S(6)} %select_n.115), kind=kOutput, calls=%fused_computation.5 | convolution fusion | flops 806879232 | bytes 11272196 | tf_op jit(solution)/shard_map/dot_general | solution.py:146
  103.7 3.9 %add_add_fusion.5 = f32[768,1024]{1,0:T(8,128)} fusion(f32[768,1024]{1,0:T(8,128)S(1)} %copy-done.9, f32[768,1024]{1,0:T(8,128)S(1)} %fusion.8, bf16[512,3,1024]{2,0,1:T(8,128)(2,1)} %collective-permute-done.2, bf16[768,4096]{1,0:T(8,128)(2,1)S(1)} %bitcast.134, s32[]{:T(128)S(6)} %select_n.115), kind=kOutput, calls=%fused_computation.6 | convolution fusion | flops 806879232 | bytes 11272196 | tf_op jit(solution)/shard_map/dot_general | solution.py:146
  107.6 31.3 %collective-permute-done.3 = bf16[512,3,1024]{2,0,1:T(8,128)(2,1)} collective-permute-done((bf16[512,3,1024]{2,0,1:T(8,128)(2,1)}, bf16[512,3,1024]{2,0,1:T(8,128)(2,1)}, u32[]{:S(2)}, u32[]{:S(2)}) %collective-permute-start.3) | collective-permute-done | bytes 3145760 | tf_op jit(solution)/shard_map/ppermute | solution.py:175
  144.9 1.2 constant_dynamic-slice_fusion.1
  146.1 2.6 fusion.13
  148.7 2.5 fusion.19
  151.2 2.4 fusion.25
  153.6 2.4 add_add_fusion.refs_8_
  156.1 3.2 add_add_fusion.1.refs_4_
  159.4 3.0 add_add_fusion.2.refs_0_
  162.4 44.2 %collective-permute-done.7 = bf16[512,3,1024]{2,0,1:T(8,128)(2,1)} collective-permute-done((bf16[512,3,1024]{2,0,1:T(8,128)(2,1)}, bf16[512,3,1024]{2,0,1:T(8,128)(2,1)}, u32[]{:S(2)}, u32[]{:S(2)}) %collective-permute-start.7) | collective-permute-done | bytes 3145760 | tf_op jit(solution)/shard_map/while/body/eval_jaxpr/ppermute | solution.py:174
  206.6 1.5 slice.261
  208.1 1.1 collective-permute-start.9
  209.8 2.2 fusion.1.refs_9_
  212.1 3.0 fusion.3.refs_5_
  215.1 3.0 fusion.5.refs_1_
  218.1 1.0 fusion.refs_10_
  219.1 1.0 fusion.2.refs_6_
  220.1 1.0 fusion.4.refs_2_
  221.1 19.3 %collective-permute-done.9 = bf16[256,3,1024]{2,0,1:T(8,128)(2,1)S(1)} collective-permute-done((bf16[256,3,1024]{2,0,1:T(8,128)(2,1)S(1)}, bf16[256,3,1024]{2,0,1:T(8,128)(2,1)S(1)}, u32[]{:S(2)}, u32[]{:S(2)}) %collective-permute-start.9) | collective-permute-done | bytes 1572896 | tf_op jit(solution)/shard_map/ppermute | solution.py:194
  240.5 1.1 collective-permute-done.10
  244.2 2.4 collective-permute-start.11
  249.7 3.4 collective-permute-start.15
  255.7 26.2 %shard_map.91 = bf16[768,512]{1,0:T(8,128)(2,1)} custom-call(bf16[3,136,512]{2,1,0:T(8,128)(2,1)} %copy-done.23, f32[768,1024]{1,0:T(8,128)} %copy-done.2, f32[768,1024]{1,0:T(8,128)} %copy-done.5, f32[768,1024]{1,0:T(8,128)} %copy-done.8, f32[768,512]{1,0:T(8,128)} %copy-done.20, f32[768,1024]{1,0:T(8,128)} %copy-done.1, f32[768,1024]{1,0:T(8,128)} %copy-done.4, ...), custom_call_target="tpu_custom_call" | custom-call | tf_op jit(solution)/shard_map/pallas_call | solution.py:105
  281.9 1.3 collective-permute-start.13
  283.9 26.2 %shard_map.92 = bf16[768,512]{1,0:T(8,128)(2,1)} custom-call(bf16[3,136,512]{2,1,0:T(8,128)(2,1)} %copy-done.22, f32[768,1024]{1,0:T(8,128)} %copy-done.2, f32[768,1024]{1,0:T(8,128)} %copy-done.5, f32[768,1024]{1,0:T(8,128)} %copy-done.8, f32[768,512]{1,0:T(8,128)} %copy-done.16, f32[768,1024]{1,0:T(8,128)} %copy-done.1, f32[768,1024]{1,0:T(8,128)} %copy-done.4, ...), custom_call_target="tpu_custom_call" | custom-call | tf_op jit(solution)/shard_map/pallas_call | solution.py:105
  310.5 5.9 %collective-permute-start.12 = (bf16[768,512]{1,0:T(8,128)(2,1)S(1)}, bf16[768,512]{1,0:T(8,128)(2,1)S(1)}, u32[]{:S(2)}, u32[]{:S(2)}) collective-permute-start(bf16[768,512]{1,0:T(8,128)(2,1)S(1)} %copy-done.17), channel_id=1, source_target_pairs={{0,1},{1,0},{2,3},{3,2},{4,5},{5,4},{6,7},{7,6},{8,9},{9,8},{10,11... | collective-permute-start | bytes 2359304 | tf_op jit(solution)/shard_map/ppermute | solution.py:250
  316.3 2.1 fusion.38
  320.0 3.8 %collective-permute-done.17 = bf16[768,512]{1,0:T(8,128)(2,1)S(1)} collective-permute-done((bf16[768,512]{1,0:T(8,128)(2,1)}, bf16[768,512]{1,0:T(8,128)(2,1)S(1)}, u32[]{:S(2)}, u32[]{:S(2)}) %collective-permute-start.17) | collective-permute-done | bytes 786464 | tf_op jit(solution)/shard_map/ppermute | solution.py:250
  323.8 6.5 %collective-permute-start.18 = (bf16[768,512]{1,0:T(8,128)(2,1)S(1)}, bf16[768,512]{1,0:T(8,128)(2,1)S(1)}, u32[]{:S(2)}, u32[]{:S(2)}) collective-permute-start(bf16[768,512]{1,0:T(8,128)(2,1)S(1)} %collective-permute-done.17), channel_id=1, source_target_pairs={{0,1},{1,0},{2,3},{3,2},{4,5},{5,4},{6,7},{7,6},{8,9},{9,8},{10,11... | collective-permute-start | bytes 2359304 | tf_op jit(solution)/shard_map/ppermute | solution.py:250
  330.4 2.2 fusion.34
  332.6 2.4 fusion.42
  335.0 2.2 fusion.36
  337.2 2.2 fusion.44
  339.5 2.2 fusion.40
  341.7 3.9 %add_convert_fusion = bf16[768,1024]{1,0:T(8,128)(2,1)} fusion(f32[768,1024]{1,0:T(8,128)S(1)} %fusion.34, f32[768,1024]{1,0:T(8,128)S(1)} %fusion.38, f32[768,1024]{1,0:T(8,128)S(1)} %fusion.36, f32[768,1024]{1,0:T(8,128)S(1)} %fusion.40, f32[768,1024]{1,0:T(8,128)S(1)} %fusion.42, f32[768,1024]{1,0:T(8,128)S(1)} %fusion.46, f32[768,1024]{1,0:T(8,128)S(1)} %fusion.44, ...), kind=kOutput, calls=%fused_computation | convolution fusion | flops 811597824 | bytes 25427968 | tf_op jit(solution)/shard_map/dot_general | solution.py:254
  (113 shorter events, 15.5 us)
Async XLA Ops:
  0.0 70.3 %collective-permute-start.2 = (bf16[512,3,1024]{2,0,1:T(8,128)(2,1)}, bf16[512,3,1024]{2,0,1:T(8,128)(2,1)}, u32[]{:S(2)}, u32[]{:S(2)}) collective-permute-start(bf16[512,3,1024]{2,0,1:T(8,128)(2,1)} %param.10), channel_id=1, source_target_pairs={{0,4},{8,0},{16,8},{24,16},{28,24},{20,28},{12,20},{4,12},{1,5},{9... | collective-permute-start | bytes 9437192 | tf_op jit(solution)/shard_map/ppermute | solution.py:182
  2.1 69.3 %collective-permute-start = (bf16[512,3,1024]{2,0,1:T(8,128)(2,1)}, bf16[512,3,1024]{2,0,1:T(8,128)(2,1)}, u32[]{:S(2)}, u32[]{:S(2)}) collective-permute-start(bf16[512,3,1024]{2,0,1:T(8,128)(2,1)} %param.10), channel_id=1, source_target_pairs={{0,8},{8,16},{16,24},{24,28},{28,20},{20,12},{12,4},{4,0},{1,9},{9... | collective-permute-start | bytes 9437192 | tf_op jit(solution)/shard_map/ppermute | solution.py:181
  9.1 66.9 %copy-start.27 = (s32[8]{0:T(128)S(1)}, s32[8]{0:T(128)}, u32[]{:S(2)}) copy-start(s32[8]{0:T(128)} %constant.118.clone) | copy-start | bytes 100
  9.1 72.8 %copy-start.25 = (s32[8]{0:T(128)S(1)}, s32[8]{0:T(128)}, u32[]{:S(2)}) copy-start(s32[8]{0:T(128)} %constant.117.clone) | copy-start | bytes 100
  9.1 98.6 %collective-permute-start.6 = (bf16[1024,1024]{1,0:T(8,128)(2,1)}, bf16[1024,1024]{1,0:T(8,128)(2,1)}, u32[]{:S(2)}, u32[]{:S(2)}) collective-permute-start(bf16[1024,1024]{1,0:T(8,128)(2,1)} %get-tuple-element.57), channel_id=1, source_target_pairs={{0,3},{1,2},{2,1},{3,0},{4,7},{5,6},{6,5},{7,4},{8,11},{9,10},{10,... | collective-permute-start | bytes 6291464 | tf_op jit(solution)/shard_map/ppermute | solution.py:241
  11.6 96.1 %collective-permute-start.4 = (bf16[1024,1024]{1,0:T(8,128)(2,1)}, bf16[1024,1024]{1,0:T(8,128)(2,1)}, u32[]{:S(2)}, u32[]{:S(2)}) collective-permute-start(bf16[1024,1024]{1,0:T(8,128)(2,1)} %get-tuple-element.58), channel_id=1, source_target_pairs={{0,1},{1,0},{2,3},{3,2},{4,5},{5,4},{6,7},{7,6},{8,9},{9,8},{10,11... | collective-permute-start | bytes 6291464 | tf_op jit(solution)/shard_map/ppermute | solution.py:241
  11.6 96.1 %collective-permute-start.5 = (bf16[1024,1024]{1,0:T(8,128)(2,1)}, bf16[1024,1024]{1,0:T(8,128)(2,1)}, u32[]{:S(2)}, u32[]{:S(2)}) collective-permute-start(bf16[1024,1024]{1,0:T(8,128)(2,1)} %get-tuple-element.60), channel_id=1, source_target_pairs={{0,2},{1,3},{2,0},{3,1},{4,6},{5,7},{6,4},{7,5},{8,10},{9,11},{10,... | collective-permute-start | bytes 6291464 | tf_op jit(solution)/shard_map/ppermute | solution.py:241
  70.3 68.7 %collective-permute-start.3 = (bf16[512,3,1024]{2,0,1:T(8,128)(2,1)}, bf16[512,3,1024]{2,0,1:T(8,128)(2,1)}, u32[]{:S(2)}, u32[]{:S(2)}) collective-permute-start(bf16[512,3,1024]{2,0,1:T(8,128)(2,1)} %collective-permute-done.2), channel_id=1, source_target_pairs={{0,4},{8,0},{16,8},{24,16},{28,24},{20,28},{12,20},{4,12},{1,5},{9... | collective-permute-start | bytes 9437192 | tf_op jit(solution)/shard_map/ppermute | solution.py:175
  71.4 68.1 %collective-permute-start.1 = (bf16[512,3,1024]{2,0,1:T(8,128)(2,1)}, bf16[512,3,1024]{2,0,1:T(8,128)(2,1)}, u32[]{:S(2)}, u32[]{:S(2)}) collective-permute-start(bf16[512,3,1024]{2,0,1:T(8,128)(2,1)} %collective-permute-done), channel_id=1, source_target_pairs={{0,8},{8,16},{16,24},{24,28},{28,20},{20,12},{12,4},{4,0},{1,9},{9... | collective-permute-start | bytes 9437192 | tf_op jit(solution)/shard_map/ppermute | solution.py:174
  71.7 17.2 %slice-start = ((s8[6291456]{0:T(1024)(128)(4,1)}), s8[2097152]{0:T(1024)(128)(4,1)S(1)}, s32[]{:S(2)}) async-start(s8[6291456]{0:T(1024)(128)(4,1)} %bitcast.133), calls=%async_computation | async-start | bytes 4194304
  83.9 5.1 %slice-start.1 = ((s8[6291456]{0:T(1024)(128)(4,1)}), s8[4194304]{0:T(1024)(128)(4,1)S(1)}, s32[]{:S(2)}) async-start(s8[6291456]{0:T(1024)(128)(4,1)} %bitcast.133), calls=%async_computation.1 | async-start | bytes 8388608
  99.6 4.1 %copy-start.9 = (f32[768,1024]{1,0:T(8,128)S(1)}, f32[768,1024]{1,0:T(8,128)}, u32[]{:S(2)}) copy-start(f32[768,1024]{1,0:T(8,128)} %fusion.31) | copy-start | bytes 9437188
  139.4 67.2 %collective-permute-start.7 = (bf16[512,3,1024]{2,0,1:T(8,128)(2,1)}, bf16[512,3,1024]{2,0,1:T(8,128)(2,1)}, u32[]{:S(2)}, u32[]{:S(2)}) collective-permute-start(bf16[512,3,1024]{2,0,1:T(8,128)(2,1)} %collective-permute-done.1), channel_id=1, source_target_pairs={{0,8},{8,16},{16,24},{24,28},{28,20},{20,12},{12,4},{4,0},{1,9},{9... | collective-permute-start | bytes 9437192 | tf_op jit(solution)/shard_map/while/body/eval_jaxpr/ppermute | solution.py:174
  140.1 69.1 %collective-permute-start.8 = (bf16[512,3,1024]{2,0,1:T(8,128)(2,1)}, bf16[512,3,1024]{2,0,1:T(8,128)(2,1)S(1)}, u32[]{:S(2)}, u32[]{:S(2)}) collective-permute-start(bf16[512,3,1024]{2,0,1:T(8,128)(2,1)} %collective-permute-done.3), channel_id=1, source_target_pairs={{0,4},{8,0},{16,8},{24,16},{28,24},{20,28},{12,20},{4,12},{1,5},{9... | collective-permute-start | bytes 9437192 | tf_op jit(solution)/shard_map/while/body/eval_jaxpr/ppermute | solution.py:175
  146.0 5.2 %slice-start.2 = ((s8[6291456]{0:T(1024)(128)(4,1)}), s8[4194304]{0:T(1024)(128)(4,1)S(1)}, s32[]{:S(2)}) async-start(s8[6291456]{0:T(1024)(128)(4,1)} %bitcast.135), calls=%async_computation.2 | async-start | bytes 8388608
  146.1 5.1 %slice-start.3 = ((s8[6291456]{0:T(1024)(128)(4,1)}), s8[2097152]{0:T(1024)(128)(4,1)S(1)}, s32[]{:S(2)}) async-start(s8[6291456]{0:T(1024)(128)(4,1)} %bitcast.135), calls=%async_computation.3 | async-start | bytes 4194304
  151.2 2.4 copy-start.10
  153.6 2.4 copy-start.11
  156.1 92.3 %copy-start = (f32[768,1024]{1,0:T(8,128)}, f32[768,1024]{1,0:T(8,128)S(1)}, u32[]{:S(2)}) copy-start(f32[768,1024]{1,0:T(8,128)S(1)} %add_add_fusion.refs_8_) | copy-start | bytes 9437188
  156.1 3.3 copy-start.12
  159.4 89.2 %copy-start.1 = (f32[768,1024]{1,0:T(8,128)}, f32[768,1024]{1,0:T(8,128)S(1)}, u32[]{:S(2)}) copy-start(f32[768,1024]{1,0:T(8,128)S(1)} %add_add_fusion.1.refs_4_) | copy-start | bytes 9437188
  162.4 86.0 %copy-start.2 = (f32[768,1024]{1,0:T(8,128)}, f32[768,1024]{1,0:T(8,128)S(1)}, u32[]{:S(2)}) copy-start(f32[768,1024]{1,0:T(8,128)S(1)} %add_add_fusion.2.refs_0_) | copy-start | bytes 9437188
  208.1 32.3 %collective-permute-start.9 = (bf16[256,3,1024]{2,0,1:T(8,128)(2,1)S(1)}, bf16[256,3,1024]{2,0,1:T(8,128)(2,1)S(1)}, u32[]{:S(2)}, u32[]{:S(2)}) collective-permute-start(bf16[256,3,1024]{2,0,1:T(8,128)(2,1)S(1)} %slice.261), channel_id=1, source_target_pairs={{0,8},{8,16},{16,24},{24,28},{28,20},{20,12},{12,4},{4,0},{1,9},{9... | collective-permute-start | bytes 4718600 | tf_op jit(solution)/shard_map/ppermute | solution.py:194
  209.3 32.3 %collective-permute-start.10 = (bf16[256,3,1024]{2,0,1:T(8,128)(2,1)S(1)}, bf16[256,3,1024]{2,0,1:T(8,128)(2,1)S(1)}, u32[]{:S(2)}, u32[]{:S(2)}) collective-permute-start(bf16[256,3,1024]{2,0,1:T(8,128)(2,1)S(1)} %slice.262), channel_id=1, source_target_pairs={{0,4},{8,0},{16,8},{24,16},{28,24},{20,28},{12,20},{4,12},{1,5},{9... | collective-permute-start | bytes 4718600 | tf_op jit(solution)/shard_map/ppermute | solution.py:195
  212.0 36.3 %copy-start.3 = (f32[768,1024]{1,0:T(8,128)}, f32[768,1024]{1,0:T(8,128)S(1)}, u32[]{:S(2)}) copy-start(f32[768,1024]{1,0:T(8,128)S(1)} %fusion.1.refs_9_) | copy-start | bytes 9437188
  215.0 33.6 %copy-start.4 = (f32[768,1024]{1,0:T(8,128)}, f32[768,1024]{1,0:T(8,128)S(1)}, u32[]{:S(2)}) copy-start(f32[768,1024]{1,0:T(8,128)S(1)} %fusion.3.refs_5_) | copy-start | bytes 9437188
  218.1 30.4 %copy-start.5 = (f32[768,1024]{1,0:T(8,128)}, f32[768,1024]{1,0:T(8,128)S(1)}, u32[]{:S(2)}) copy-start(f32[768,1024]{1,0:T(8,128)S(1)} %fusion.5.refs_1_) | copy-start | bytes 9437188
  219.1 29.3 %copy-start.6 = (f32[768,1024]{1,0:T(8,128)}, f32[768,1024]{1,0:T(8,128)S(1)}, u32[]{:S(2)}) copy-start(f32[768,1024]{1,0:T(8,128)S(1)} %fusion.refs_10_) | copy-start | bytes 9437188
  220.1 28.6 %copy-start.7 = (f32[768,1024]{1,0:T(8,128)}, f32[768,1024]{1,0:T(8,128)S(1)}, u32[]{:S(2)}) copy-start(f32[768,1024]{1,0:T(8,128)S(1)} %fusion.2.refs_6_) | copy-start | bytes 9437188
  221.1 27.4 %copy-start.8 = (f32[768,1024]{1,0:T(8,128)}, f32[768,1024]{1,0:T(8,128)S(1)}, u32[]{:S(2)}) copy-start(f32[768,1024]{1,0:T(8,128)S(1)} %fusion.4.refs_2_) | copy-start | bytes 9437188
  242.3 1.3 copy-start.18
  242.9 1.2 copy-start.19
  243.5 3.0 copy-start.20
  244.2 10.7 %collective-permute-start.11 = (bf16[3,136,512]{2,1,0:T(8,128)(2,1)S(1)}, bf16[3,136,512]{2,1,0:T(8,128)(2,1)S(1)}, u32[]{:S(2)}, u32[]{:S(2)}) collective-permute-start(bf16[3,136,512]{2,1,0:T(8,128)(2,1)S(1)} %pad_maximum_fusion.1), channel_id=1, source_target_pairs={{0,4},{4,8},{8,12},{12,16},{16,20},{20,24},{24,28},{1,5},{5,9},{9,... | collective-permute-start | bytes 1253384 | tf_op jit(solution)/shard_map/ppermute | solution.py:324
  247.1 1.4 copy-start.14
  247.7 5.4 %copy-start.26 = (f32[1024]{0:T(1024)S(1)}, f32[1024]{0:T(1024)}, u32[]{:S(2)}) copy-start(f32[1024]{0:T(1024)} %param.13) | copy-start | bytes 12292
  247.7 5.4 %copy-start.21 = (f32[1024,128]{1,0:T(8,128)S(1)}, f32[1024,128]{1,0:T(8,128)}, u32[]{:S(2)}) copy-start(f32[1024,128]{1,0:T(8,128)} %param.12) | copy-start | bytes 1572868
  248.3 1.3 copy-start.16
  248.3 5.0 %copy-start.24 = (f32[3,1024,7]{1,2,0:T(8,128)S(1)}, f32[3,1024,7]{1,2,0:T(8,128)}, u32[]{:S(2)}) copy-start(f32[3,1024,7]{1,2,0:T(8,128)} %param.11) | copy-start | bytes 258052
  249.7 33.5 %collective-permute-start.15 = (bf16[3,136,512]{2,1,0:T(8,128)(2,1)}, bf16[3,136,512]{2,1,0:T(8,128)(2,1)S(1)}, u32[]{:S(2)}, u32[]{:S(2)}) collective-permute-start(bf16[3,136,512]{2,1,0:T(8,128)(2,1)} %pad_maximum_fusion.2), channel_id=1, source_target_pairs={{0,4},{4,8},{8,12},{12,16},{16,20},{20,24},{24,28},{1,5},{5,9},{9,... | collective-permute-start | bytes 1253384 | tf_op jit(solution)/shard_map/ppermute | solution.py:324
  281.8 28.6 %copy-start.17 = (bf16[768,512]{1,0:T(8,128)(2,1)S(1)}, bf16[768,512]{1,0:T(8,128)(2,1)}, u32[]{:S(2)}) copy-start(bf16[768,512]{1,0:T(8,128)(2,1)} %shard_map.91) | copy-start | bytes 2359300
  281.8 34.5 %copy-start.13 = (bf16[1024,1024]{1,0:T(8,128)(2,1)S(1)}, bf16[1024,1024]{1,0:T(8,128)(2,1)}, u32[]{:S(2)}) copy-start(bf16[1024,1024]{1,0:T(8,128)(2,1)} %get-tuple-element.51) | copy-start | bytes 6291460
  281.9 37.6 %collective-permute-start.13 = (bf16[768,512]{1,0:T(8,128)(2,1)}, bf16[768,512]{1,0:T(8,128)(2,1)}, u32[]{:S(2)}, u32[]{:S(2)}) collective-permute-start(bf16[768,512]{1,0:T(8,128)(2,1)} %shard_map.91), channel_id=1, source_target_pairs={{0,2},{1,3},{2,0},{3,1},{4,6},{5,7},{6,4},{7,5},{8,10},{9,11},{10,... | collective-permute-start | bytes 2359304 | tf_op jit(solution)/shard_map/ppermute | solution.py:250
  310.1 13.7 %collective-permute-start.17 = (bf16[768,512]{1,0:T(8,128)(2,1)}, bf16[768,512]{1,0:T(8,128)(2,1)S(1)}, u32[]{:S(2)}, u32[]{:S(2)}) collective-permute-start(bf16[768,512]{1,0:T(8,128)(2,1)} %shard_map.92), channel_id=1, source_target_pairs={{0,2},{1,3},{2,0},{3,1},{4,6},{5,7},{6,4},{7,5},{8,10},{9,11},{10,... | collective-permute-start | bytes 2359304 | tf_op jit(solution)/shard_map/ppermute | solution.py:250
  310.5 26.8 %collective-permute-start.12 = (bf16[768,512]{1,0:T(8,128)(2,1)S(1)}, bf16[768,512]{1,0:T(8,128)(2,1)S(1)}, u32[]{:S(2)}, u32[]{:S(2)}) collective-permute-start(bf16[768,512]{1,0:T(8,128)(2,1)S(1)} %copy-done.17), channel_id=1, source_target_pairs={{0,1},{1,0},{2,3},{3,2},{4,5},{5,4},{6,7},{7,6},{8,9},{9,8},{10,11... | collective-permute-start | bytes 2359304 | tf_op jit(solution)/shard_map/ppermute | solution.py:250
  316.3 18.7 %collective-permute-start.16 = (bf16[768,512]{1,0:T(8,128)(2,1)}, bf16[768,512]{1,0:T(8,128)(2,1)S(1)}, u32[]{:S(2)}, u32[]{:S(2)}) collective-permute-start(bf16[768,512]{1,0:T(8,128)(2,1)} %shard_map.92), channel_id=1, source_target_pairs={{0,1},{1,0},{2,3},{3,2},{4,5},{5,4},{6,7},{7,6},{8,9},{9,8},{10,11... | collective-permute-start | bytes 2359304 | tf_op jit(solution)/shard_map/ppermute | solution.py:250
  319.4 20.0 %collective-permute-start.14 = (bf16[768,512]{1,0:T(8,128)(2,1)}, bf16[768,512]{1,0:T(8,128)(2,1)S(1)}, u32[]{:S(2)}, u32[]{:S(2)}) collective-permute-start(bf16[768,512]{1,0:T(8,128)(2,1)} %collective-permute-done.13), channel_id=1, source_target_pairs={{0,1},{1,0},{2,3},{3,2},{4,5},{5,4},{6,7},{7,6},{8,9},{9,8},{10,11... | collective-permute-start | bytes 2359304 | tf_op jit(solution)/shard_map/ppermute | solution.py:250
  323.8 17.8 %collective-permute-start.18 = (bf16[768,512]{1,0:T(8,128)(2,1)S(1)}, bf16[768,512]{1,0:T(8,128)(2,1)S(1)}, u32[]{:S(2)}, u32[]{:S(2)}) collective-permute-start(bf16[768,512]{1,0:T(8,128)(2,1)S(1)} %collective-permute-done.17), channel_id=1, source_target_pairs={{0,1},{1,0},{2,3},{3,2},{4,5},{5,4},{6,7},{7,6},{8,9},{9,8},{10,11... | collective-permute-start | bytes 2359304 | tf_op jit(solution)/shard_map/ppermute | solution.py:250
  (3 other events, 2.7 us)

commit v4 on v3

--- a/solution.py
+++ b/solution.py
@@ -284,16 +284,18 @@
         jnp.transpose(short_taps, (0, 2, 1)), ((0, 0), (0, 8 - short_count), (0, 0))
     ).reshape(3 * 8, channel_count)
     tiles = channel_count // LANES
-    parts = 2 if tiles % 2 == 0 else 1
-    share = tiles // parts
+    split = (tiles * 5 + 7) // 8
+    bounds = [0, split, tiles] if 0 < split < tiles else [0, tiles]
+    parts = len(bounds) - 1
     medium = jnp.transpose(filters)
     features, weights, last = ring_projection(tokens, in_weight, spread_weights(out_weight), parts)
     tail = None
     skip = skip_gain.reshape(1, channel_count)
     total = None
     for part in range(parts):
-        cols = slice(part * share * LANES, (part + 1) * share * LANES)
-        chosen = tuple(tuple((term, part * share) for term, _ in field) for field in features)
+        first, share = bounds[part], bounds[part + 1] - bounds[part]
+        cols = slice(first * LANES, (first + share) * LANES)
+        chosen = tuple(tuple((term, first) for term, _ in field) for field in features)
         if last is not None:
             cols_in, block = last
             if tail is not None:
@@ -322,9 +324,8 @@
             ]
         )
         halo = lax.ppermute(tail, "ctx", [(k, k + 1) for k in range(ctx_count - 1)])
-        gated = channel_filter(halo, chosen, taps, medium, skip, part * share, share)
-        rows = slice(part * share * LANES, (part + 1) * share * LANES)
-        piece = output_projection(gated, tuple(w[rows] for w in weights))
+        gated = channel_filter(halo, chosen, taps, medium, skip, first, share)
+        piece = output_projection(gated, tuple(w[cols] for w in weights))
         total = piece if total is None else total + piece
     return total.astype(jnp.bfloat16)
 

time: 347 us -> 363 us (1.046)
  waiting for transfers between devices: 159 us -> 177 us
  starting transfers between devices: 29.7 us -> 24.4 us
    ppermute x6, waiting for transfers between devices: 3.82 us -> 18.2 us  [output_projection(): lax.ppermute(piece, 'tp', pairs)]
    ppermute x2, waiting for transfers between devices: 0.01 us -> 5.69 us  [per_device(): halo = lax.ppermute(tail, 'ctx', [(k, k + 1) for k in range(ctx_count - 1)])]
    ppermute x6, starting transfers between devices: 14.6 us -> 9.09 us  [output_projection(): lax.ppermute(piece, 'tp', pairs)]
  transfers between devices with their start and end apart: 19 -> 19, of which waited for: 7 -> 8; matrix products, arithmetic and copies ran while one was open for 25% -> 24% of each run, Pallas kernels for 15% -> 15%
where the time goes in v4:
time: 363 us; the launch traced here: 360 us
  waiting for transfers between devices  177 us (49%)
  matrix products  77.8 us (21%)
  Pallas kernels  52.4 us (14%)
  starting transfers between devices  24.4 us (7%)
  local copies, waits for them, and re-layouts  15.1 us (4%)
  between operations  11.1 us (3%)
    ppermute x1, waiting for transfers between devices, ring_projection(): behind = lax.ppermute(in_weight, 'ctx', backward)  58.4 us
    dot_general x21, matrix products, product(): jnp.dot(cols, block[:, field, :], preferred_element_type=jnp.float32)  55.1 us
    pallas_call x2, Pallas kernels, channel_filter(): pl.pallas_call(functools.partial(filter_kernel, term_count), grid=(tiles,...  52.4 us
    ppermute x2, waiting for transfers between devices, ring_step(): moved_ahead = lax.ppermute(ahead, 'ctx', forward)  42.7 us
    ppermute x2, waiting for transfers between devices, ring_step(): moved_behind = lax.ppermute(behind, 'ctx', backward)  31.3 us
    ppermute x1, waiting for transfers between devices, ring_projection(): last_ahead = lax.ppermute(ahead[:half], 'ctx', forward)  19.1 us
    dot_general x8, matrix products, output_projection(): jnp.dot(pieces[key], weights[key], preferred_element_type=jnp.float32)  18.6 us
    ppermute x6, waiting for transfers between devices, output_projection(): lax.ppermute(piece, 'tp', pairs)  18.2 us
  transfers between devices with their start and end apart: 19, of which 8 were waited for; matrix products, arithmetic and copies ran while one was open for 24% of the time, Pallas kernels for 15%

profile of v4, /device:TPU:1, one launch (start us, length us, event | category | flops | bytes accessed | tf_op | source)
XLA Modules:
  0.0 360.2 jit_solution(1983323066989531959)
XLA Ops:
  0.0 2.1 collective-permute-start.2
  2.1 7.0 %constant_dynamic-slice_fusion.2 = (bf16[1024,1024]{1,0:T(8,128)(2,1)}, bf16[1024,1024]{1,0:T(8,128)(2,1)}, bf16[1024,1024]{1,0:T(8,128)(2,1)}, bf16[1024,1024]{1,0:T(8,128)(2,1)}) fusion(bf16[1024,4096]{1,0:T(8,128)(2,1)} %param.15, s32[]{:T(128)S(6)} %select_n.119, s32[]{:T(128)S(6)} %select_n.117, s32[]{:T(128)S(6)} %select_n.116, s32[]{:T(128)S(6)} %select_n.118), kind=kLoop, calls=%fused_computation.163 | loop fusion | bytes 16777232 | tf_op jit(solution)/shard_map/dynamic_slice | solution.py:240
  9.1 2.5 collective-permute-start.6
  11.8 58.4 %collective-permute-done.2 = bf16[512,3,1024]{2,0,1:T(8,128)(2,1)} collective-permute-done((bf16[512,3,1024]{2,0,1:T(8,128)(2,1)}, bf16[512,3,1024]{2,0,1:T(8,128)(2,1)}, u32[]{:S(2)}, u32[]{:S(2)}) %collective-permute-start.2) | collective-permute-done | bytes 3145760 | tf_op jit(solution)/shard_map/ppermute | solution.py:182
  70.3 1.1 collective-permute-start.3
  71.7 4.2 %fusion.39 = f32[768,1024]{1,0:T(8,128)} fusion(bf16[512,3,1024]{2,0,1:T(8,128)(2,1)} %param.10, bf16[768,4096]{1,0:T(8,128)(2,1)} %param.9, s32[]{:T(128)S(6)} %select_n.108), kind=kOutput, calls=%fused_computation.52 | convolution fusion | flops 805306368 | bytes 4980740 | tf_op jit(solution)/shard_map/dot_general | solution.py:146
  83.9 2.6 fusion.35
  86.5 2.5 fusion.37
  89.0 2.2 fusion.14
  91.2 2.2 fusion.15
  93.4 2.2 fusion.16
  95.6 3.9 %add_add_fusion.3 = f32[768,1024]{1,0:T(8,128)} fusion(f32[768,1024]{1,0:T(8,128)S(1)} %fusion.35, f32[768,1024]{1,0:T(8,128)S(1)} %fusion.14, bf16[512,3,1024]{2,0,1:T(8,128)(2,1)} %collective-permute-done.2, bf16[768,4096]{1,0:T(8,128)(2,1)S(1)} %bitcast.134, s32[]{:T(128)S(6)} %select_n.115), kind=kOutput, calls=%fused_computation.4 | convolution fusion | flops 806879232 | bytes 11272196 | tf_op jit(solution)/shard_map/dot_general | solution.py:146
  99.6 4.1 %add_add_fusion.4 = f32[768,1024]{1,0:T(8,128)} fusion(f32[768,1024]{1,0:T(8,128)S(1)} %fusion.37, f32[768,1024]{1,0:T(8,128)S(1)} %fusion.15, bf16[512,3,1024]{2,0,1:T(8,128)(2,1)} %collective-permute-done.2, bf16[768,4096]{1,0:T(8,128)(2,1)S(1)} %bitcast.134, s32[]{:T(128)S(6)} %select_n.115), kind=kOutput, calls=%fused_computation.5 | convolution fusion | flops 806879232 | bytes 11272196 | tf_op jit(solution)/shard_map/dot_general | solution.py:146
  103.7 3.9 %add_add_fusion.5 = f32[768,1024]{1,0:T(8,128)} fusion(f32[768,1024]{1,0:T(8,128)S(1)} %copy-done.9, f32[768,1024]{1,0:T(8,128)S(1)} %fusion.16, bf16[512,3,1024]{2,0,1:T(8,128)(2,1)} %collective-permute-done.2, bf16[768,4096]{1,0:T(8,128)(2,1)S(1)} %bitcast.134, s32[]{:T(128)S(6)} %select_n.115), kind=kOutput, calls=%fused_computation.6 | convolution fusion | flops 806879232 | bytes 11272196 | tf_op jit(solution)/shard_map/dot_general | solution.py:146
  107.6 31.3 %collective-permute-done.3 = bf16[512,3,1024]{2,0,1:T(8,128)(2,1)} collective-permute-done((bf16[512,3,1024]{2,0,1:T(8,128)(2,1)}, bf16[512,3,1024]{2,0,1:T(8,128)(2,1)}, u32[]{:S(2)}, u32[]{:S(2)}) %collective-permute-start.3) | collective-permute-done | bytes 3145760 | tf_op jit(solution)/shard_map/ppermute | solution.py:175
  144.8 2.1 copy.10
  146.8 1.2 constant_dynamic-slice_fusion.1
  148.1 2.6 fusion.21
  150.7 2.5 fusion.27
  153.2 2.4 fusion.33
  155.6 2.4 add_add_fusion.refs_8_
  158.1 3.2 add_add_fusion.1.refs_4_
  161.4 3.0 add_add_fusion.2.refs_0_
  164.4 42.2 %collective-permute-done.7 = bf16[512,3,1024]{2,0,1:T(8,128)(2,1)} collective-permute-done((bf16[512,3,1024]{2,0,1:T(8,128)(2,1)}, bf16[512,3,1024]{2,0,1:T(8,128)(2,1)}, u32[]{:S(2)}, u32[]{:S(2)}) %collective-permute-start.7) | collective-permute-done | bytes 3145760 | tf_op jit(solution)/shard_map/while/body/eval_jaxpr/ppermute | solution.py:174
  206.6 1.5 slice.261
  208.1 1.1 collective-permute-start.9
  210.1 2.2 fusion.9.refs_9_
  212.3 3.0 fusion.11.refs_5_
  215.3 3.0 fusion.13.refs_1_
  218.3 1.0 fusion.8.refs_10_
  220.3 1.0 fusion.12.refs_2_
  221.3 19.1 %collective-permute-done.9 = bf16[256,3,1024]{2,0,1:T(8,128)(2,1)S(1)} collective-permute-done((bf16[256,3,1024]{2,0,1:T(8,128)(2,1)S(1)}, bf16[256,3,1024]{2,0,1:T(8,128)(2,1)S(1)}, u32[]{:S(2)}, u32[]{:S(2)}) %collective-permute-start.9) | collective-permute-done | bytes 1572896 | tf_op jit(solution)/shard_map/ppermute | solution.py:194
  240.5 1.3 collective-permute-done.10
  245.8 2.8 collective-permute-start.11
  250.8 3.0 collective-permute-start.15
  255.4 5.7 %collective-permute-done.15.halo = bf16[3,136,384]{2,1,0:T(8,128)(2,1)S(1)} collective-permute-done((bf16[3,136,384]{2,1,0:T(8,128)(2,1)S(1)}, bf16[3,136,384]{2,1,0:T(8,128)(2,1)S(1)}, u32[]{:S(2)}, u32[]{:S(2)}) %collective-permute-start.15) | collective-permute-done | bytes 313376 | tf_op jit(solution)/shard_map/ppermute | solution.py:326
  261.8 20.4 %shard_map.92 = bf16[768,384]{1,0:T(8,128)(2,1)} custom-call(bf16[3,136,384]{2,1,0:T(8,128)(2,1)} %copy-done.23, f32[768,1024]{1,0:T(8,128)} %copy-done.2, f32[768,1024]{1,0:T(8,128)} %copy-done.5, f32[768,1024]{1,0:T(8,128)} %copy-done.8, f32[768,384]{1,0:T(8,128)} %copy-done.18, f32[768,1024]{1,0:T(8,128)} %copy-done.1, f32[768,1024]{1,0:T(8,128)} %copy-done.4, ...), custom_call_target="tpu_custom_call" | custom-call | tf_op jit(solution)/shard_map/pallas_call | solution.py:105
  282.2 1.3 collective-permute-start.17
  283.5 6.1 %collective-permute-start.16 = (bf16[768,384]{1,0:T(8,128)(2,1)}, bf16[768,384]{1,0:T(8,128)(2,1)}, u32[]{:S(2)}, u32[]{:S(2)}) collective-permute-start(bf16[768,384]{1,0:T(8,128)(2,1)} %shard_map.92), channel_id=1, source_target_pairs={{0,1},{1,0},{2,3},{3,2},{4,5},{5,4},{6,7},{7,6},{8,9},{9,8},{10,11... | collective-permute-start | bytes 1769480 | tf_op jit(solution)/shard_map/ppermute | solution.py:250
  289.5 31.9 %shard_map.91 = bf16[768,640]{1,0:T(8,128)(2,1)} custom-call(bf16[3,136,640]{2,1,0:T(8,128)(2,1)} %collective-permute-done.11.halo, f32[768,1024]{1,0:T(8,128)} %copy-done.2, f32[768,1024]{1,0:T(8,128)} %copy-done.5, f32[768,1024]{1,0:T(8,128)} %copy-done.8, f32[768,640]{1,0:T(8,128)} %copy-done.14, f32[768,1024]{1,0:T(8,128)} %copy-done.1, ...), custom_call_target="tpu_custom_call" | custom-call | tf_op jit(solution)/shard_map/pallas_call | solution.py:105
  323.3 1.4 fusion.6
  324.9 2.1 fusion.51
  327.0 18.2 %collective-permute-done.13 = bf16[768,640]{1,0:T(8,128)(2,1)S(1)} collective-permute-done((bf16[768,640]{1,0:T(8,128)(2,1)}, bf16[768,640]{1,0:T(8,128)(2,1)S(1)}, u32[]{:S(2)}, u32[]{:S(2)}) %collective-permute-start.13) | collective-permute-done | bytes 983072 | tf_op jit(solution)/shard_map/ppermute | solution.py:250
  346.0 2.3 fusion.53
  348.3 2.7 fusion.2
  351.0 2.7 fusion.4
  353.7 2.7 fusion
  356.4 3.8 %add_convert_fusion = bf16[768,1024]{1,0:T(8,128)(2,1)} fusion(f32[768,1024]{1,0:T(8,128)S(1)} %fusion.51, f32[768,1024]{1,0:T(8,128)S(1)} %fusion.55, f32[768,1024]{1,0:T(8,128)S(1)} %fusion.53, f32[768,1024]{1,0:T(8,128)S(1)} %fusion, f32[768,1024]{1,0:T(8,128)S(1)} %fusion.2, f32[768,1024]{1,0:T(8,128)S(1)} %fusion.6, f32[768,1024]{1,0:T(8,128)S(1)} %fusion.4, ...), kind=kOutput, calls=%fused_computation | convolution fusion | flops 610271232 | bytes 24969216 | tf_op jit(solution)/shard_map/dot_general | solution.py:254
  (113 shorter events, 17.0 us)
Async XLA Ops:
  0.0 70.3 %collective-permute-start.2 = (bf16[512,3,1024]{2,0,1:T(8,128)(2,1)}, bf16[512,3,1024]{2,0,1:T(8,128)(2,1)}, u32[]{:S(2)}, u32[]{:S(2)}) collective-permute-start(bf16[512,3,1024]{2,0,1:T(8,128)(2,1)} %param.10), channel_id=1, source_target_pairs={{0,4},{8,0},{16,8},{24,16},{28,24},{20,28},{12,20},{4,12},{1,5},{9... | collective-permute-start | bytes 9437192 | tf_op jit(solution)/shard_map/ppermute | solution.py:182
  2.1 69.3 %collective-permute-start = (bf16[512,3,1024]{2,0,1:T(8,128)(2,1)}, bf16[512,3,1024]{2,0,1:T(8,128)(2,1)}, u32[]{:S(2)}, u32[]{:S(2)}) collective-permute-start(bf16[512,3,1024]{2,0,1:T(8,128)(2,1)} %param.10), channel_id=1, source_target_pairs={{0,8},{8,16},{16,24},{24,28},{28,20},{20,12},{12,4},{4,0},{1,9},{9... | collective-permute-start | bytes 9437192 | tf_op jit(solution)/shard_map/ppermute | solution.py:181
  9.1 66.9 %copy-start.27 = (s32[8]{0:T(128)S(1)}, s32[8]{0:T(128)}, u32[]{:S(2)}) copy-start(s32[8]{0:T(128)} %constant.118.clone) | copy-start | bytes 100
  9.1 72.8 %copy-start.25 = (s32[8]{0:T(128)S(1)}, s32[8]{0:T(128)}, u32[]{:S(2)}) copy-start(s32[8]{0:T(128)} %constant.117.clone) | copy-start | bytes 100
  9.1 98.5 %collective-permute-start.6 = (bf16[1024,1024]{1,0:T(8,128)(2,1)}, bf16[1024,1024]{1,0:T(8,128)(2,1)}, u32[]{:S(2)}, u32[]{:S(2)}) collective-permute-start(bf16[1024,1024]{1,0:T(8,128)(2,1)} %get-tuple-element.57), channel_id=1, source_target_pairs={{0,3},{1,2},{2,1},{3,0},{4,7},{5,6},{6,5},{7,4},{8,11},{9,10},{10,... | collective-permute-start | bytes 6291464 | tf_op jit(solution)/shard_map/ppermute | solution.py:241
  11.6 96.0 %collective-permute-start.4 = (bf16[1024,1024]{1,0:T(8,128)(2,1)}, bf16[1024,1024]{1,0:T(8,128)(2,1)}, u32[]{:S(2)}, u32[]{:S(2)}) collective-permute-start(bf16[1024,1024]{1,0:T(8,128)(2,1)} %get-tuple-element.58), channel_id=1, source_target_pairs={{0,1},{1,0},{2,3},{3,2},{4,5},{5,4},{6,7},{7,6},{8,9},{9,8},{10,11... | collective-permute-start | bytes 6291464 | tf_op jit(solution)/shard_map/ppermute | solution.py:241
  11.6 96.0 %collective-permute-start.5 = (bf16[1024,1024]{1,0:T(8,128)(2,1)}, bf16[1024,1024]{1,0:T(8,128)(2,1)}, u32[]{:S(2)}, u32[]{:S(2)}) collective-permute-start(bf16[1024,1024]{1,0:T(8,128)(2,1)} %get-tuple-element.60), channel_id=1, source_target_pairs={{0,2},{1,3},{2,0},{3,1},{4,6},{5,7},{6,4},{7,5},{8,10},{9,11},{10,... | collective-permute-start | bytes 6291464 | tf_op jit(solution)/shard_map/ppermute | solution.py:241
  70.3 68.7 %collective-permute-start.3 = (bf16[512,3,1024]{2,0,1:T(8,128)(2,1)}, bf16[512,3,1024]{2,0,1:T(8,128)(2,1)}, u32[]{:S(2)}, u32[]{:S(2)}) collective-permute-start(bf16[512,3,1024]{2,0,1:T(8,128)(2,1)} %collective-permute-done.2), channel_id=1, source_target_pairs={{0,4},{8,0},{16,8},{24,16},{28,24},{20,28},{12,20},{4,12},{1,5},{9... | collective-permute-start | bytes 9437192 | tf_op jit(solution)/shard_map/ppermute | solution.py:175
  71.4 68.1 %collective-permute-start.1 = (bf16[512,3,1024]{2,0,1:T(8,128)(2,1)}, bf16[512,3,1024]{2,0,1:T(8,128)(2,1)}, u32[]{:S(2)}, u32[]{:S(2)}) collective-permute-start(bf16[512,3,1024]{2,0,1:T(8,128)(2,1)} %collective-permute-done), channel_id=1, source_target_pairs={{0,8},{8,16},{16,24},{24,28},{28,20},{20,12},{12,4},{4,0},{1,9},{9... | collective-permute-start | bytes 9437192 | tf_op jit(solution)/shard_map/ppermute | solution.py:174
  71.7 17.2 %slice-start = ((s8[6291456]{0:T(1024)(128)(4,1)}), s8[2097152]{0:T(1024)(128)(4,1)S(1)}, s32[]{:S(2)}) async-start(s8[6291456]{0:T(1024)(128)(4,1)} %bitcast.133), calls=%async_computation | async-start | bytes 4194304
  83.9 5.1 %slice-start.1 = ((s8[6291456]{0:T(1024)(128)(4,1)}), s8[4194304]{0:T(1024)(128)(4,1)S(1)}, s32[]{:S(2)}) async-start(s8[6291456]{0:T(1024)(128)(4,1)} %bitcast.133), calls=%async_computation.1 | async-start | bytes 8388608
  99.6 4.1 %copy-start.9 = (f32[768,1024]{1,0:T(8,128)S(1)}, f32[768,1024]{1,0:T(8,128)}, u32[]{:S(2)}) copy-start(f32[768,1024]{1,0:T(8,128)} %fusion.39) | copy-start | bytes 9437188
  103.7 41.1 %copy-start.26 = (f32[1024]{0:T(1024)S(1)}, f32[1024]{0:T(1024)}, u32[]{:S(2)}) copy-start(f32[1024]{0:T(1024)} %param.13) | copy-start | bytes 12292
  139.4 67.2 %collective-permute-start.7 = (bf16[512,3,1024]{2,0,1:T(8,128)(2,1)}, bf16[512,3,1024]{2,0,1:T(8,128)(2,1)}, u32[]{:S(2)}, u32[]{:S(2)}) collective-permute-start(bf16[512,3,1024]{2,0,1:T(8,128)(2,1)} %collective-permute-done.1), channel_id=1, source_target_pairs={{0,8},{8,16},{16,24},{24,28},{28,20},{20,12},{12,4},{4,0},{1,9},{9... | collective-permute-start | bytes 9437192 | tf_op jit(solution)/shard_map/while/body/eval_jaxpr/ppermute | solution.py:174
  140.1 69.1 %collective-permute-start.8 = (bf16[512,3,1024]{2,0,1:T(8,128)(2,1)}, bf16[512,3,1024]{2,0,1:T(8,128)(2,1)S(1)}, u32[]{:S(2)}, u32[]{:S(2)}) collective-permute-start(bf16[512,3,1024]{2,0,1:T(8,128)(2,1)} %collective-permute-done.3), channel_id=1, source_target_pairs={{0,4},{8,0},{16,8},{24,16},{28,24},{20,28},{12,20},{4,12},{1,5},{9... | collective-permute-start | bytes 9437192 | tf_op jit(solution)/shard_map/while/body/eval_jaxpr/ppermute | solution.py:175
  148.0 5.2 %slice-start.2 = ((s8[6291456]{0:T(1024)(128)(4,1)}), s8[4194304]{0:T(1024)(128)(4,1)S(1)}, s32[]{:S(2)}) async-start(s8[6291456]{0:T(1024)(128)(4,1)} %bitcast.135), calls=%async_computation.2 | async-start | bytes 8388608
  148.1 5.1 %slice-start.3 = ((s8[6291456]{0:T(1024)(128)(4,1)}), s8[2097152]{0:T(1024)(128)(4,1)S(1)}, s32[]{:S(2)}) async-start(s8[6291456]{0:T(1024)(128)(4,1)} %bitcast.135), calls=%async_computation.3 | async-start | bytes 4194304
  153.2 2.4 copy-start.10
  155.6 2.4 copy-start.11
  158.0 92.4 %copy-start = (f32[768,1024]{1,0:T(8,128)}, f32[768,1024]{1,0:T(8,128)S(1)}, u32[]{:S(2)}) copy-start(f32[768,1024]{1,0:T(8,128)S(1)} %add_add_fusion.refs_8_) | copy-start | bytes 9437188
  158.0 3.3 copy-start.12
  161.4 89.3 %copy-start.1 = (f32[768,1024]{1,0:T(8,128)}, f32[768,1024]{1,0:T(8,128)S(1)}, u32[]{:S(2)}) copy-start(f32[768,1024]{1,0:T(8,128)S(1)} %add_add_fusion.1.refs_4_) | copy-start | bytes 9437188
  164.4 86.1 %copy-start.2 = (f32[768,1024]{1,0:T(8,128)}, f32[768,1024]{1,0:T(8,128)S(1)}, u32[]{:S(2)}) copy-start(f32[768,1024]{1,0:T(8,128)S(1)} %add_add_fusion.2.refs_0_) | copy-start | bytes 9437188
  208.1 32.3 %collective-permute-start.9 = (bf16[256,3,1024]{2,0,1:T(8,128)(2,1)S(1)}, bf16[256,3,1024]{2,0,1:T(8,128)(2,1)S(1)}, u32[]{:S(2)}, u32[]{:S(2)}) collective-permute-start(bf16[256,3,1024]{2,0,1:T(8,128)(2,1)S(1)} %slice.261), channel_id=1, source_target_pairs={{0,8},{8,16},{16,24},{24,28},{28,20},{20,12},{12,4},{4,0},{1,9},{9... | collective-permute-start | bytes 4718600 | tf_op jit(solution)/shard_map/ppermute | solution.py:194
  209.3 32.5 %collective-permute-start.10 = (bf16[256,3,1024]{2,0,1:T(8,128)(2,1)S(1)}, bf16[256,3,1024]{2,0,1:T(8,128)(2,1)S(1)}, u32[]{:S(2)}, u32[]{:S(2)}) collective-permute-start(bf16[256,3,1024]{2,0,1:T(8,128)(2,1)S(1)} %slice.262), channel_id=1, source_target_pairs={{0,4},{8,0},{16,8},{24,16},{28,24},{20,28},{12,20},{4,12},{1,5},{9... | collective-permute-start | bytes 4718600 | tf_op jit(solution)/shard_map/ppermute | solution.py:195
  212.3 38.2 %copy-start.3 = (f32[768,1024]{1,0:T(8,128)}, f32[768,1024]{1,0:T(8,128)S(1)}, u32[]{:S(2)}) copy-start(f32[768,1024]{1,0:T(8,128)S(1)} %fusion.9.refs_9_) | copy-start | bytes 9437188
  215.3 35.4 %copy-start.4 = (f32[768,1024]{1,0:T(8,128)}, f32[768,1024]{1,0:T(8,128)S(1)}, u32[]{:S(2)}) copy-start(f32[768,1024]{1,0:T(8,128)S(1)} %fusion.11.refs_5_) | copy-start | bytes 9437188
  218.3 32.3 %copy-start.5 = (f32[768,1024]{1,0:T(8,128)}, f32[768,1024]{1,0:T(8,128)S(1)}, u32[]{:S(2)}) copy-start(f32[768,1024]{1,0:T(8,128)S(1)} %fusion.13.refs_1_) | copy-start | bytes 9437188
  219.3 31.1 %copy-start.6 = (f32[768,1024]{1,0:T(8,128)}, f32[768,1024]{1,0:T(8,128)S(1)}, u32[]{:S(2)}) copy-start(f32[768,1024]{1,0:T(8,128)S(1)} %fusion.8.refs_10_) | copy-start | bytes 9437188
  220.3 30.4 %copy-start.7 = (f32[768,1024]{1,0:T(8,128)}, f32[768,1024]{1,0:T(8,128)S(1)}, u32[]{:S(2)}) copy-start(f32[768,1024]{1,0:T(8,128)S(1)} %fusion.10.refs_6_) | copy-start | bytes 9437188
  221.3 29.2 %copy-start.8 = (f32[768,1024]{1,0:T(8,128)}, f32[768,1024]{1,0:T(8,128)S(1)}, u32[]{:S(2)}) copy-start(f32[768,1024]{1,0:T(8,128)S(1)} %fusion.12.refs_2_) | copy-start | bytes 9437188
  242.8 1.6 copy-start.15
  244.4 4.9 %copy-start.14 = (f32[768,640]{1,0:T(8,128)}, f32[768,640]{1,0:T(8,128)S(1)}, u32[]{:S(2)}) copy-start(f32[768,640]{1,0:T(8,128)S(1)} %fusion.59.refs_3_) | copy-start | bytes 5898244
  245.8 43.7 %collective-permute-start.11 = (bf16[3,136,640]{2,1,0:T(8,128)(2,1)}, bf16[3,136,640]{2,1,0:T(8,128)(2,1)}, u32[]{:S(2)}, u32[]{:S(2)}) collective-permute-start(bf16[3,136,640]{2,1,0:T(8,128)(2,1)} %pad_maximum_fusion.1), channel_id=1, source_target_pairs={{0,4},{4,8},{8,12},{12,16},{16,20},{20,24},{24,28},{1,5},{5,9},{9,... | collective-permute-start | bytes 1566728 | tf_op jit(solution)/shard_map/ppermute | solution.py:326
  249.2 1.5 copy-start.16
  249.8 5.5 %copy-start.17 = (f32[768,384]{1,0:T(8,128)}, f32[768,384]{1,0:T(8,128)S(1)}, u32[]{:S(2)}) copy-start(f32[768,384]{1,0:T(8,128)S(1)} %fusion.83.refs_7_) | copy-start | bytes 3538948
  249.8 4.0 %copy-start.24 = (f32[3,1024,7]{1,2,0:T(8,128)S(1)}, f32[3,1024,7]{1,2,0:T(8,128)}, u32[]{:S(2)}) copy-start(f32[3,1024,7]{1,2,0:T(8,128)} %param.11) | copy-start | bytes 258052
  249.8 4.6 %copy-start.21 = (f32[1024,128]{0,1:T(8,128)S(1)}, f32[1024,128]{0,1:T(8,128)}, u32[]{:S(2)}) copy-start(f32[1024,128]{0,1:T(8,128)} %copy.10) | copy-start | bytes 1572868
  250.4 10.6 %copy-start.18 = (f32[768,384]{1,0:T(8,128)}, f32[768,384]{1,0:T(8,128)S(1)}, u32[]{:S(2)}) copy-start(f32[768,384]{1,0:T(8,128)S(1)} %fusion.85.refs_3_) | copy-start | bytes 3538948
  250.8 10.2 %collective-permute-start.15 = (bf16[3,136,384]{2,1,0:T(8,128)(2,1)S(1)}, bf16[3,136,384]{2,1,0:T(8,128)(2,1)S(1)}, u32[]{:S(2)}, u32[]{:S(2)}) collective-permute-start(bf16[3,136,384]{2,1,0:T(8,128)(2,1)S(1)} %pad_maximum_fusion.2), channel_id=1, source_target_pairs={{0,4},{4,8},{8,12},{12,16},{16,20},{20,24},{24,28},{1,5},{5,9},{9,... | collective-permute-start | bytes 940040 | tf_op jit(solution)/shard_map/ppermute | solution.py:326
  282.2 39.7 %copy-start.19 = (bf16[1024,1024]{1,0:T(8,128)(2,1)S(1)}, bf16[1024,1024]{1,0:T(8,128)(2,1)}, u32[]{:S(2)}) copy-start(bf16[1024,1024]{1,0:T(8,128)(2,1)} %get-tuple-element.51) | copy-start | bytes 6291460
  282.2 39.6 %copy-start.20 = (bf16[768,384]{1,0:T(8,128)(2,1)S(1)}, bf16[768,384]{1,0:T(8,128)(2,1)}, u32[]{:S(2)}) copy-start(bf16[768,384]{1,0:T(8,128)(2,1)} %shard_map.92) | copy-start | bytes 1769476
  282.2 42.5 %collective-permute-start.17 = (bf16[768,384]{1,0:T(8,128)(2,1)}, bf16[768,384]{1,0:T(8,128)(2,1)S(1)}, u32[]{:S(2)}, u32[]{:S(2)}) collective-permute-start(bf16[768,384]{1,0:T(8,128)(2,1)} %shard_map.92), channel_id=1, source_target_pairs={{0,2},{1,3},{2,0},{3,1},{4,6},{5,7},{6,4},{7,5},{8,10},{9,11},{10,... | collective-permute-start | bytes 1769480 | tf_op jit(solution)/shard_map/ppermute | solution.py:250
  283.5 62.5 %collective-permute-start.16 = (bf16[768,384]{1,0:T(8,128)(2,1)}, bf16[768,384]{1,0:T(8,128)(2,1)}, u32[]{:S(2)}, u32[]{:S(2)}) collective-permute-start(bf16[768,384]{1,0:T(8,128)(2,1)} %shard_map.92), channel_id=1, source_target_pairs={{0,1},{1,0},{2,3},{3,2},{4,5},{5,4},{6,7},{7,6},{8,9},{9,8},{10,11... | collective-permute-start | bytes 1769480 | tf_op jit(solution)/shard_map/ppermute | solution.py:250
  321.5 23.7 %collective-permute-start.13 = (bf16[768,640]{1,0:T(8,128)(2,1)}, bf16[768,640]{1,0:T(8,128)(2,1)S(1)}, u32[]{:S(2)}, u32[]{:S(2)}) collective-permute-start(bf16[768,640]{1,0:T(8,128)(2,1)} %shard_map.91), channel_id=1, source_target_pairs={{0,2},{1,3},{2,0},{3,1},{4,6},{5,7},{6,4},{7,5},{8,10},{9,11},{10,... | collective-permute-start | bytes 2949128 | tf_op jit(solution)/shard_map/ppermute | solution.py:250
  322.8 28.1 %collective-permute-start.12 = (bf16[768,640]{1,0:T(8,128)(2,1)S(1)}, bf16[768,640]{1,0:T(8,128)(2,1)S(1)}, u32[]{:S(2)}, u32[]{:S(2)}) collective-permute-start(bf16[768,640]{1,0:T(8,128)(2,1)S(1)} %copy-done.22), channel_id=1, source_target_pairs={{0,1},{1,0},{2,3},{3,2},{4,5},{5,4},{6,7},{7,6},{8,9},{9,8},{10,11... | collective-permute-start | bytes 2949128 | tf_op jit(solution)/shard_map/ppermute | solution.py:250
  324.7 31.7 %collective-permute-start.18 = (bf16[768,384]{1,0:T(8,128)(2,1)S(1)}, bf16[768,384]{1,0:T(8,128)(2,1)S(1)}, u32[]{:S(2)}, u32[]{:S(2)}) collective-permute-start(bf16[768,384]{1,0:T(8,128)(2,1)S(1)} %collective-permute-done.17), channel_id=1, source_target_pairs={{0,1},{1,0},{2,3},{3,2},{4,5},{5,4},{6,7},{7,6},{8,9},{9,8},{10,11... | collective-permute-start | bytes 1769480 | tf_op jit(solution)/shard_map/ppermute | solution.py:250
  345.2 8.5 %collective-permute-start.14 = (bf16[768,640]{1,0:T(8,128)(2,1)S(1)}, bf16[768,640]{1,0:T(8,128)(2,1)S(1)}, u32[]{:S(2)}, u32[]{:S(2)}) collective-permute-start(bf16[768,640]{1,0:T(8,128)(2,1)S(1)} %collective-permute-done.13), channel_id=1, source_target_pairs={{0,1},{1,0},{2,3},{3,2},{4,5},{5,4},{6,7},{7,6},{8,9},{9,8},{10,11... | collective-permute-start | bytes 2949128 | tf_op jit(solution)/shard_map/ppermute | solution.py:250
  (3 other events, 3.3 us)

commit v5 on v3

--- a/solution.py
+++ b/solution.py
@@ -77,16 +77,19 @@
     def chunk_body(index, carry):
         row = pl.multiple_of(index * CHUNK, CHUNK)
         at = pl.multiple_of(row + HALO, 8)
-        total = skip[...] * prod[pl.ds(at, CHUNK), :]
-        groups = medium.shape[0] // 8
+        total = (skip[...] * prod[pl.ds(at, CHUNK), :]).reshape(CHUNK // 8, 8, LANES)
+        groups = medium.shape[0] // 64
         reach = 8 * (groups - 1)
         start = pl.multiple_of(at - reach, 8)
         for shift in range(8):
             window = shifted[shift, pl.ds(start, CHUNK + reach), :]
             for group in range(groups):
                 offset = reach - 8 * group
-                weight = medium[pl.ds(8 * group + shift, 1), :]
-                total = total + weight * window[offset : offset + CHUNK]
+                lag = 8 * group + shift
+                weight = medium[8 * lag : 8 * lag + 8, :]
+                part = window[offset : offset + CHUNK].reshape(CHUNK // 8, 8, LANES)
+                total = total + weight[None] * part
+        total = total.reshape(CHUNK, LANES)
         out[pl.ds(row, CHUNK), :] = (smooth_q[pl.ds(row, CHUNK), :] * total).astype(out.dtype)
         return carry
 
@@ -286,7 +289,7 @@
     tiles = channel_count // LANES
     parts = 2 if tiles % 2 == 0 else 1
     share = tiles // parts
-    medium = jnp.transpose(filters)
+    medium = jnp.repeat(jnp.transpose(filters), 8, axis=0)
     features, weights, last = ring_projection(tokens, in_weight, spread_weights(out_weight), parts)
     tail = None
     skip = skip_gain.reshape(1, channel_count)

time: 347 us -> 349 us (level)
  local copies, waits for them, and re-layouts: 14.2 us -> 18.7 us
  waiting for transfers between devices: 159 us -> 155 us
    ppermute x2, waiting for transfers between devices: 44.7 us -> 40.7 us  [ring_step(): moved_ahead = lax.ppermute(ahead, 'ctx', forward)]
  transfers between devices with their start and end apart: 19 -> 19, of which waited for: 7 -> 7; matrix products, arithmetic and copies ran while one was open for 25% -> 26% of each run, Pallas kernels for 15% -> 15%
where the time goes in v5:
time: 349 us; the launch traced here: 348 us
  waiting for transfers between devices  155 us (44%)
  matrix products  76.9 us (22%)
  Pallas kernels  52.9 us (15%)
  starting transfers between devices  29.9 us (9%)
  local copies, waits for them, and re-layouts  18.7 us (5%)
  between operations  11.1 us (3%)
  other arithmetic  3.65 us (1%)
    ppermute x1, waiting for transfers between devices, ring_projection(): behind = lax.ppermute(in_weight, 'ctx', backward)  58.5 us
    dot_general x21, matrix products, product(): jnp.dot(cols, block[:, field, :], preferred_element_type=jnp.float32)  55.2 us
    pallas_call x2, Pallas kernels, channel_filter(): pl.pallas_call(functools.partial(filter_kernel, term_count), grid=(tiles,...  52.9 us
    ppermute x2, waiting for transfers between devices, ring_step(): moved_ahead = lax.ppermute(ahead, 'ctx', forward)  40.7 us
    ppermute x2, waiting for transfers between devices, ring_step(): moved_behind = lax.ppermute(behind, 'ctx', backward)  31.2 us
    ppermute x1, waiting for transfers between devices, ring_projection(): last_ahead = lax.ppermute(ahead[:half], 'ctx', forward)  19.1 us
    dot_general x8, matrix products, output_projection(): jnp.dot(pieces[key], weights[key], preferred_element_type=jnp.float32)  18.3 us
    ppermute x6, starting transfers between devices, output_projection(): lax.ppermute(piece, 'tp', pairs)  14.6 us
  transfers between devices with their start and end apart: 19, of which 7 were waited for; matrix products, arithmetic and copies ran while one was open for 26% of the time, Pallas kernels for 15%

profile of v5, /device:TPU:1, one launch (start us, length us, event | category | flops | bytes accessed | tf_op | source)
XLA Modules:
  0.0 347.8 jit_solution(13522088458090467434)
XLA Ops:
  0.0 2.1 collective-permute-start.2
  2.1 7.0 %constant_dynamic-slice_fusion.2 = (bf16[1024,1024]{1,0:T(8,128)(2,1)}, bf16[1024,1024]{1,0:T(8,128)(2,1)}, bf16[1024,1024]{1,0:T(8,128)(2,1)}, bf16[1024,1024]{1,0:T(8,128)(2,1)}) fusion(bf16[1024,4096]{1,0:T(8,128)(2,1)} %param.15, s32[]{:T(128)S(6)} %select_n.119, s32[]{:T(128)S(6)} %select_n.117, s32[]{:T(128)S(6)} %select_n.116, s32[]{:T(128)S(6)} %select_n.118), kind=kLoop, calls=%fused_computation.164 | loop fusion | bytes 16777232 | tf_op jit(solution)/shard_map/dynamic_slice | solution.py:243
  9.1 2.5 collective-permute-start.6
  11.8 58.5 %collective-permute-done.2 = bf16[512,3,1024]{2,0,1:T(8,128)(2,1)} collective-permute-done((bf16[512,3,1024]{2,0,1:T(8,128)(2,1)}, bf16[512,3,1024]{2,0,1:T(8,128)(2,1)}, u32[]{:S(2)}, u32[]{:S(2)}) %collective-permute-start.2) | collective-permute-done | bytes 3145760 | tf_op jit(solution)/shard_map/ppermute | solution.py:185
  70.3 1.1 collective-permute-start.3
  71.7 4.3 %fusion.31 = f32[768,1024]{1,0:T(8,128)} fusion(bf16[512,3,1024]{2,0,1:T(8,128)(2,1)} %param.10, bf16[768,4096]{1,0:T(8,128)(2,1)} %param.9, s32[]{:T(128)S(6)} %select_n.108), kind=kOutput, calls=%fused_computation.45 | convolution fusion | flops 805306368 | bytes 4980740 | tf_op jit(solution)/shard_map/dot_general | solution.py:149
  84.0 2.6 fusion.27
  86.6 2.5 fusion.29
  89.1 2.2 fusion.6
  91.3 2.2 fusion.7
  93.5 2.2 fusion.8
  95.7 3.9 %add_add_fusion.3 = f32[768,1024]{1,0:T(8,128)} fusion(f32[768,1024]{1,0:T(8,128)S(1)} %fusion.27, f32[768,1024]{1,0:T(8,128)S(1)} %fusion.6, bf16[512,3,1024]{2,0,1:T(8,128)(2,1)} %collective-permute-done.2, bf16[768,4096]{1,0:T(8,128)(2,1)S(1)} %bitcast.136, s32[]{:T(128)S(6)} %select_n.115), kind=kOutput, calls=%fused_computation.4 | convolution fusion | flops 806879232 | bytes 11272196 | tf_op jit(solution)/shard_map/dot_general | solution.py:149
  99.6 4.1 %add_add_fusion.4 = f32[768,1024]{1,0:T(8,128)} fusion(f32[768,1024]{1,0:T(8,128)S(1)} %fusion.29, f32[768,1024]{1,0:T(8,128)S(1)} %fusion.7, bf16[512,3,1024]{2,0,1:T(8,128)(2,1)} %collective-permute-done.2, bf16[768,4096]{1,0:T(8,128)(2,1)S(1)} %bitcast.136, s32[]{:T(128)S(6)} %select_n.115), kind=kOutput, calls=%fused_computation.5 | convolution fusion | flops 806879232 | bytes 11272196 | tf_op jit(solution)/shard_map/dot_general | solution.py:149
  103.7 4.0 %add_add_fusion.5 = f32[768,1024]{1,0:T(8,128)} fusion(f32[768,1024]{1,0:T(8,128)S(1)} %copy-done.9, f32[768,1024]{1,0:T(8,128)S(1)} %fusion.8, bf16[512,3,1024]{2,0,1:T(8,128)(2,1)} %collective-permute-done.2, bf16[768,4096]{1,0:T(8,128)(2,1)S(1)} %bitcast.136, s32[]{:T(128)S(6)} %select_n.115), kind=kOutput, calls=%fused_computation.6 | convolution fusion | flops 806879232 | bytes 11272196 | tf_op jit(solution)/shard_map/dot_general | solution.py:149
  107.7 31.2 %collective-permute-done.3 = bf16[512,3,1024]{2,0,1:T(8,128)(2,1)} collective-permute-done((bf16[512,3,1024]{2,0,1:T(8,128)(2,1)}, bf16[512,3,1024]{2,0,1:T(8,128)(2,1)}, u32[]{:S(2)}, u32[]{:S(2)}) %collective-permute-start.3) | collective-permute-done | bytes 3145760 | tf_op jit(solution)/shard_map/ppermute | solution.py:178
  144.7 2.0 multiply_bitcast_fusion
  146.8 2.1 copy.10
  148.8 1.2 constant_dynamic-slice_fusion.1
  150.1 2.6 fusion.13
  152.7 2.5 fusion.19
  155.2 2.4 fusion.25
  157.6 2.4 add_add_fusion.refs_8_
  160.0 3.2 add_add_fusion.1.refs_4_
  163.4 3.0 add_add_fusion.2.refs_0_
  166.4 40.2 %collective-permute-done.7 = bf16[512,3,1024]{2,0,1:T(8,128)(2,1)} collective-permute-done((bf16[512,3,1024]{2,0,1:T(8,128)(2,1)}, bf16[512,3,1024]{2,0,1:T(8,128)(2,1)}, u32[]{:S(2)}, u32[]{:S(2)}) %collective-permute-start.7) | collective-permute-done | bytes 3145760 | tf_op jit(solution)/shard_map/while/body/eval_jaxpr/ppermute | solution.py:177
  206.6 1.5 slice.261
  208.1 1.1 collective-permute-start.9
  210.1 2.2 fusion.1.refs_9_
  212.3 3.0 fusion.3.refs_5_
  215.3 3.0 fusion.5.refs_1_
  221.3 19.1 %collective-permute-done.9 = bf16[256,3,1024]{2,0,1:T(8,128)(2,1)S(1)} collective-permute-done((bf16[256,3,1024]{2,0,1:T(8,128)(2,1)S(1)}, bf16[256,3,1024]{2,0,1:T(8,128)(2,1)S(1)}, u32[]{:S(2)}, u32[]{:S(2)}) %collective-permute-start.9) | collective-permute-done | bytes 1572896 | tf_op jit(solution)/shard_map/ppermute | solution.py:197
  240.5 1.3 collective-permute-done.10
  244.4 2.1 collective-permute-start.11
  249.6 3.7 %collective-permute-start.15 = (bf16[3,136,512]{2,1,0:T(8,128)(2,1)}, bf16[3,136,512]{2,1,0:T(8,128)(2,1)S(1)}, u32[]{:S(2)}, u32[]{:S(2)}) collective-permute-start(bf16[3,136,512]{2,1,0:T(8,128)(2,1)} %pad_maximum_fusion.2), channel_id=1, source_target_pairs={{0,4},{4,8},{8,12},{12,16},{16,20},{20,24},{24,28},{1,5},{5,9},{9,... | collective-permute-start | bytes 1253384 | tf_op jit(solution)/shard_map/ppermute | solution.py:327
  254.0 2.5 broadcast_bitcast_fusion.refs_13_
  257.3 26.4 %shard_map.91 = bf16[768,512]{1,0:T(8,128)(2,1)} custom-call(bf16[3,136,512]{2,1,0:T(8,128)(2,1)} %copy-done.23, f32[768,1024]{1,0:T(8,128)} %copy-done.2, f32[768,1024]{1,0:T(8,128)} %copy-done.5, f32[768,1024]{1,0:T(8,128)} %copy-done.8, f32[768,512]{1,0:T(8,128)} %copy-done.20, f32[768,1024]{1,0:T(8,128)} %copy-done.1, f32[768,1024]{1,0:T(8,128)} %copy-done.4, ...), custom_call_target="tpu_custom_call" | custom-call | tf_op jit(solution)/shard_map/pallas_call | solution.py:108
  283.8 1.3 collective-permute-start.13
  285.8 26.5 %shard_map.92 = bf16[768,512]{1,0:T(8,128)(2,1)} custom-call(bf16[3,136,512]{2,1,0:T(8,128)(2,1)} %copy-done.22, f32[768,1024]{1,0:T(8,128)} %copy-done.2, f32[768,1024]{1,0:T(8,128)} %copy-done.5, f32[768,1024]{1,0:T(8,128)} %copy-done.8, f32[768,512]{1,0:T(8,128)} %copy-done.16, f32[768,1024]{1,0:T(8,128)} %copy-done.1, f32[768,1024]{1,0:T(8,128)} %copy-done.4, ...), custom_call_target="tpu_custom_call" | custom-call | tf_op jit(solution)/shard_map/pallas_call | solution.py:108
  312.6 5.9 %collective-permute-start.12 = (bf16[768,512]{1,0:T(8,128)(2,1)S(1)}, bf16[768,512]{1,0:T(8,128)(2,1)S(1)}, u32[]{:S(2)}, u32[]{:S(2)}) collective-permute-start(bf16[768,512]{1,0:T(8,128)(2,1)S(1)} %copy-done.17), channel_id=1, source_target_pairs={{0,1},{1,0},{2,3},{3,2},{4,5},{5,4},{6,7},{7,6},{8,9},{9,8},{10,11... | collective-permute-start | bytes 2359304 | tf_op jit(solution)/shard_map/ppermute | solution.py:253
  318.5 2.1 fusion.38
  322.2 3.8 %collective-permute-done.17 = bf16[768,512]{1,0:T(8,128)(2,1)S(1)} collective-permute-done((bf16[768,512]{1,0:T(8,128)(2,1)}, bf16[768,512]{1,0:T(8,128)(2,1)S(1)}, u32[]{:S(2)}, u32[]{:S(2)}) %collective-permute-start.17) | collective-permute-done | bytes 786464 | tf_op jit(solution)/shard_map/ppermute | solution.py:253
  326.0 6.5 %collective-permute-start.18 = (bf16[768,512]{1,0:T(8,128)(2,1)S(1)}, bf16[768,512]{1,0:T(8,128)(2,1)S(1)}, u32[]{:S(2)}, u32[]{:S(2)}) collective-permute-start(bf16[768,512]{1,0:T(8,128)(2,1)S(1)} %collective-permute-done.17), channel_id=1, source_target_pairs={{0,1},{1,0},{2,3},{3,2},{4,5},{5,4},{6,7},{7,6},{8,9},{9,8},{10,11... | collective-permute-start | bytes 2359304 | tf_op jit(solution)/shard_map/ppermute | solution.py:253
  332.5 2.2 fusion.34
  334.7 2.4 fusion.42
  337.2 2.2 fusion.36
  339.4 2.2 fusion.44
  341.6 2.2 fusion.40
  343.8 3.9 %add_convert_fusion = bf16[768,1024]{1,0:T(8,128)(2,1)} fusion(f32[768,1024]{1,0:T(8,128)S(1)} %fusion.34, f32[768,1024]{1,0:T(8,128)S(1)} %fusion.38, f32[768,1024]{1,0:T(8,128)S(1)} %fusion.36, f32[768,1024]{1,0:T(8,128)S(1)} %fusion.40, f32[768,1024]{1,0:T(8,128)S(1)} %fusion.42, f32[768,1024]{1,0:T(8,128)S(1)} %fusion.46, f32[768,1024]{1,0:T(8,128)S(1)} %fusion.44, ...), kind=kOutput, calls=%fused_computation | convolution fusion | flops 811597824 | bytes 25427968 | tf_op jit(solution)/shard_map/dot_general | solution.py:257
  (114 shorter events, 17.7 us)
Async XLA Ops:
  0.0 70.3 %collective-permute-start.2 = (bf16[512,3,1024]{2,0,1:T(8,128)(2,1)}, bf16[512,3,1024]{2,0,1:T(8,128)(2,1)}, u32[]{:S(2)}, u32[]{:S(2)}) collective-permute-start(bf16[512,3,1024]{2,0,1:T(8,128)(2,1)} %param.10), channel_id=1, source_target_pairs={{0,4},{8,0},{16,8},{24,16},{28,24},{20,28},{12,20},{4,12},{1,5},{9... | collective-permute-start | bytes 9437192 | tf_op jit(solution)/shard_map/ppermute | solution.py:185
  2.1 69.3 %collective-permute-start = (bf16[512,3,1024]{2,0,1:T(8,128)(2,1)}, bf16[512,3,1024]{2,0,1:T(8,128)(2,1)}, u32[]{:S(2)}, u32[]{:S(2)}) collective-permute-start(bf16[512,3,1024]{2,0,1:T(8,128)(2,1)} %param.10), channel_id=1, source_target_pairs={{0,8},{8,16},{16,24},{24,28},{28,20},{20,12},{12,4},{4,0},{1,9},{9... | collective-permute-start | bytes 9437192 | tf_op jit(solution)/shard_map/ppermute | solution.py:184
  9.1 66.9 %copy-start.27 = (s32[8]{0:T(128)S(1)}, s32[8]{0:T(128)}, u32[]{:S(2)}) copy-start(s32[8]{0:T(128)} %constant.118.clone) | copy-start | bytes 100
  9.1 72.8 %copy-start.25 = (s32[8]{0:T(128)S(1)}, s32[8]{0:T(128)}, u32[]{:S(2)}) copy-start(s32[8]{0:T(128)} %constant.117.clone) | copy-start | bytes 100
  9.1 98.6 %collective-permute-start.6 = (bf16[1024,1024]{1,0:T(8,128)(2,1)}, bf16[1024,1024]{1,0:T(8,128)(2,1)}, u32[]{:S(2)}, u32[]{:S(2)}) collective-permute-start(bf16[1024,1024]{1,0:T(8,128)(2,1)} %get-tuple-element.57), channel_id=1, source_target_pairs={{0,3},{1,2},{2,1},{3,0},{4,7},{5,6},{6,5},{7,4},{8,11},{9,10},{10,... | collective-permute-start | bytes 6291464 | tf_op jit(solution)/shard_map/ppermute | solution.py:244
  11.6 96.1 %collective-permute-start.4 = (bf16[1024,1024]{1,0:T(8,128)(2,1)}, bf16[1024,1024]{1,0:T(8,128)(2,1)}, u32[]{:S(2)}, u32[]{:S(2)}) collective-permute-start(bf16[1024,1024]{1,0:T(8,128)(2,1)} %get-tuple-element.58), channel_id=1, source_target_pairs={{0,1},{1,0},{2,3},{3,2},{4,5},{5,4},{6,7},{7,6},{8,9},{9,8},{10,11... | collective-permute-start | bytes 6291464 | tf_op jit(solution)/shard_map/ppermute | solution.py:244
  11.6 96.1 %collective-permute-start.5 = (bf16[1024,1024]{1,0:T(8,128)(2,1)}, bf16[1024,1024]{1,0:T(8,128)(2,1)}, u32[]{:S(2)}, u32[]{:S(2)}) collective-permute-start(bf16[1024,1024]{1,0:T(8,128)(2,1)} %get-tuple-element.60), channel_id=1, source_target_pairs={{0,2},{1,3},{2,0},{3,1},{4,6},{5,7},{6,4},{7,5},{8,10},{9,11},{10,... | collective-permute-start | bytes 6291464 | tf_op jit(solution)/shard_map/ppermute | solution.py:244
  70.3 68.7 %collective-permute-start.3 = (bf16[512,3,1024]{2,0,1:T(8,128)(2,1)}, bf16[512,3,1024]{2,0,1:T(8,128)(2,1)}, u32[]{:S(2)}, u32[]{:S(2)}) collective-permute-start(bf16[512,3,1024]{2,0,1:T(8,128)(2,1)} %collective-permute-done.2), channel_id=1, source_target_pairs={{0,4},{8,0},{16,8},{24,16},{28,24},{20,28},{12,20},{4,12},{1,5},{9... | collective-permute-start | bytes 9437192 | tf_op jit(solution)/shard_map/ppermute | solution.py:178
  71.4 68.1 %collective-permute-start.1 = (bf16[512,3,1024]{2,0,1:T(8,128)(2,1)}, bf16[512,3,1024]{2,0,1:T(8,128)(2,1)}, u32[]{:S(2)}, u32[]{:S(2)}) collective-permute-start(bf16[512,3,1024]{2,0,1:T(8,128)(2,1)} %collective-permute-done), channel_id=1, source_target_pairs={{0,8},{8,16},{16,24},{24,28},{28,20},{20,12},{12,4},{4,0},{1,9},{9... | collective-permute-start | bytes 9437192 | tf_op jit(solution)/shard_map/ppermute | solution.py:177
  71.7 17.3 %slice-start = ((s8[6291456]{0:T(1024)(128)(4,1)}), s8[2097152]{0:T(1024)(128)(4,1)S(1)}, s32[]{:S(2)}) async-start(s8[6291456]{0:T(1024)(128)(4,1)} %bitcast.135), calls=%async_computation | async-start | bytes 4194304
  84.0 5.1 %slice-start.1 = ((s8[6291456]{0:T(1024)(128)(4,1)}), s8[4194304]{0:T(1024)(128)(4,1)S(1)}, s32[]{:S(2)}) async-start(s8[6291456]{0:T(1024)(128)(4,1)} %bitcast.135), calls=%async_computation.1 | async-start | bytes 8388608
  99.6 4.1 %copy-start.9 = (f32[768,1024]{1,0:T(8,128)S(1)}, f32[768,1024]{1,0:T(8,128)}, u32[]{:S(2)}) copy-start(f32[768,1024]{1,0:T(8,128)} %fusion.31) | copy-start | bytes 9437188
  103.7 41.0 %copy-start.26 = (f32[1024]{0:T(1024)S(1)}, f32[1024]{0:T(1024)}, u32[]{:S(2)}) copy-start(f32[1024]{0:T(1024)} %param.13) | copy-start | bytes 12292
  139.4 67.2 %collective-permute-start.7 = (bf16[512,3,1024]{2,0,1:T(8,128)(2,1)}, bf16[512,3,1024]{2,0,1:T(8,128)(2,1)}, u32[]{:S(2)}, u32[]{:S(2)}) collective-permute-start(bf16[512,3,1024]{2,0,1:T(8,128)(2,1)} %collective-permute-done.1), channel_id=1, source_target_pairs={{0,8},{8,16},{16,24},{24,28},{28,20},{20,12},{12,4},{4,0},{1,9},{9... | collective-permute-start | bytes 9437192 | tf_op jit(solution)/shard_map/while/body/eval_jaxpr/ppermute | solution.py:177
  140.1 69.1 %collective-permute-start.8 = (bf16[512,3,1024]{2,0,1:T(8,128)(2,1)}, bf16[512,3,1024]{2,0,1:T(8,128)(2,1)S(1)}, u32[]{:S(2)}, u32[]{:S(2)}) collective-permute-start(bf16[512,3,1024]{2,0,1:T(8,128)(2,1)} %collective-permute-done.3), channel_id=1, source_target_pairs={{0,4},{8,0},{16,8},{24,16},{28,24},{20,28},{12,20},{4,12},{1,5},{9... | collective-permute-start | bytes 9437192 | tf_op jit(solution)/shard_map/while/body/eval_jaxpr/ppermute | solution.py:178
  150.0 5.2 %slice-start.2 = ((s8[6291456]{0:T(1024)(128)(4,1)}), s8[4194304]{0:T(1024)(128)(4,1)S(1)}, s32[]{:S(2)}) async-start(s8[6291456]{0:T(1024)(128)(4,1)} %bitcast.137), calls=%async_computation.2 | async-start | bytes 8388608
  150.1 5.1 %slice-start.3 = ((s8[6291456]{0:T(1024)(128)(4,1)}), s8[2097152]{0:T(1024)(128)(4,1)S(1)}, s32[]{:S(2)}) async-start(s8[6291456]{0:T(1024)(128)(4,1)} %bitcast.137), calls=%async_computation.3 | async-start | bytes 4194304
  155.2 2.4 copy-start.10
  157.6 2.4 copy-start.11
  160.0 88.2 %copy-start = (f32[768,1024]{1,0:T(8,128)}, f32[768,1024]{1,0:T(8,128)S(1)}, u32[]{:S(2)}) copy-start(f32[768,1024]{1,0:T(8,128)S(1)} %add_add_fusion.refs_8_) | copy-start | bytes 9437188
  160.0 3.3 copy-start.12
  163.4 85.1 %copy-start.1 = (f32[768,1024]{1,0:T(8,128)}, f32[768,1024]{1,0:T(8,128)S(1)}, u32[]{:S(2)}) copy-start(f32[768,1024]{1,0:T(8,128)S(1)} %add_add_fusion.1.refs_4_) | copy-start | bytes 9437188
  166.4 82.0 %copy-start.2 = (f32[768,1024]{1,0:T(8,128)}, f32[768,1024]{1,0:T(8,128)S(1)}, u32[]{:S(2)}) copy-start(f32[768,1024]{1,0:T(8,128)S(1)} %add_add_fusion.2.refs_0_) | copy-start | bytes 9437188
  208.1 32.3 %collective-permute-start.9 = (bf16[256,3,1024]{2,0,1:T(8,128)(2,1)S(1)}, bf16[256,3,1024]{2,0,1:T(8,128)(2,1)S(1)}, u32[]{:S(2)}, u32[]{:S(2)}) collective-permute-start(bf16[256,3,1024]{2,0,1:T(8,128)(2,1)S(1)} %slice.261), channel_id=1, source_target_pairs={{0,8},{8,16},{16,24},{24,28},{28,20},{20,12},{12,4},{4,0},{1,9},{9... | collective-permute-start | bytes 4718600 | tf_op jit(solution)/shard_map/ppermute | solution.py:197
  209.3 32.5 %collective-permute-start.10 = (bf16[256,3,1024]{2,0,1:T(8,128)(2,1)S(1)}, bf16[256,3,1024]{2,0,1:T(8,128)(2,1)S(1)}, u32[]{:S(2)}, u32[]{:S(2)}) collective-permute-start(bf16[256,3,1024]{2,0,1:T(8,128)(2,1)S(1)} %slice.262), channel_id=1, source_target_pairs={{0,4},{8,0},{16,8},{24,16},{28,24},{20,28},{12,20},{4,12},{1,5},{9... | collective-permute-start | bytes 4718600 | tf_op jit(solution)/shard_map/ppermute | solution.py:198
  212.3 36.0 %copy-start.3 = (f32[768,1024]{1,0:T(8,128)}, f32[768,1024]{1,0:T(8,128)S(1)}, u32[]{:S(2)}) copy-start(f32[768,1024]{1,0:T(8,128)S(1)} %fusion.1.refs_9_) | copy-start | bytes 9437188
  215.3 33.3 %copy-start.4 = (f32[768,1024]{1,0:T(8,128)}, f32[768,1024]{1,0:T(8,128)S(1)}, u32[]{:S(2)}) copy-start(f32[768,1024]{1,0:T(8,128)S(1)} %fusion.3.refs_5_) | copy-start | bytes 9437188
  218.3 30.1 %copy-start.5 = (f32[768,1024]{1,0:T(8,128)}, f32[768,1024]{1,0:T(8,128)S(1)}, u32[]{:S(2)}) copy-start(f32[768,1024]{1,0:T(8,128)S(1)} %fusion.5.refs_1_) | copy-start | bytes 9437188
  219.3 28.9 %copy-start.6 = (f32[768,1024]{1,0:T(8,128)}, f32[768,1024]{1,0:T(8,128)S(1)}, u32[]{:S(2)}) copy-start(f32[768,1024]{1,0:T(8,128)S(1)} %fusion.refs_10_) | copy-start | bytes 9437188
  220.3 28.2 %copy-start.7 = (f32[768,1024]{1,0:T(8,128)}, f32[768,1024]{1,0:T(8,128)S(1)}, u32[]{:S(2)}) copy-start(f32[768,1024]{1,0:T(8,128)S(1)} %fusion.2.refs_6_) | copy-start | bytes 9437188
  221.3 27.1 %copy-start.8 = (f32[768,1024]{1,0:T(8,128)}, f32[768,1024]{1,0:T(8,128)S(1)}, u32[]{:S(2)}) copy-start(f32[768,1024]{1,0:T(8,128)S(1)} %fusion.4.refs_2_) | copy-start | bytes 9437188
  242.6 1.3 copy-start.18
  243.7 2.7 copy-start.20
  244.4 12.2 %collective-permute-start.11 = (bf16[3,136,512]{2,1,0:T(8,128)(2,1)S(1)}, bf16[3,136,512]{2,1,0:T(8,128)(2,1)S(1)}, u32[]{:S(2)}, u32[]{:S(2)}) collective-permute-start(bf16[3,136,512]{2,1,0:T(8,128)(2,1)S(1)} %pad_maximum_fusion.1), channel_id=1, source_target_pairs={{0,4},{4,8},{8,12},{12,16},{16,20},{20,24},{24,28},{1,5},{5,9},{9,... | collective-permute-start | bytes 1253384 | tf_op jit(solution)/shard_map/ppermute | solution.py:327
  247.0 1.4 copy-start.14
  247.6 1.2 copy-start.15
  247.6 5.7 %copy-start.24 = (f32[3,1024,7]{1,2,0:T(8,128)S(1)}, f32[3,1024,7]{1,2,0:T(8,128)}, u32[]{:S(2)}) copy-start(f32[3,1024,7]{1,2,0:T(8,128)} %param.11) | copy-start | bytes 258052
  247.6 6.4 %copy-start.21 = (f32[128,1024]{1,0:T(8,128)S(1)}, f32[128,1024]{1,0:T(8,128)}, u32[]{:S(2)}) copy-start(f32[128,1024]{1,0:T(8,128)} %copy.10) | copy-start | bytes 1572868
  248.2 1.4 copy-start.16
  249.6 35.4 %collective-permute-start.15 = (bf16[3,136,512]{2,1,0:T(8,128)(2,1)}, bf16[3,136,512]{2,1,0:T(8,128)(2,1)S(1)}, u32[]{:S(2)}, u32[]{:S(2)}) collective-permute-start(bf16[3,136,512]{2,1,0:T(8,128)(2,1)} %pad_maximum_fusion.2), channel_id=1, source_target_pairs={{0,4},{4,8},{8,12},{12,16},{16,20},{20,24},{24,28},{1,5},{5,9},{9,... | collective-permute-start | bytes 1253384 | tf_op jit(solution)/shard_map/ppermute | solution.py:327
  283.7 28.9 %copy-start.17 = (bf16[768,512]{1,0:T(8,128)(2,1)S(1)}, bf16[768,512]{1,0:T(8,128)(2,1)}, u32[]{:S(2)}) copy-start(bf16[768,512]{1,0:T(8,128)(2,1)} %shard_map.91) | copy-start | bytes 2359300
  283.7 34.7 %copy-start.13 = (bf16[1024,1024]{1,0:T(8,128)(2,1)S(1)}, bf16[1024,1024]{1,0:T(8,128)(2,1)}, u32[]{:S(2)}) copy-start(bf16[1024,1024]{1,0:T(8,128)(2,1)} %get-tuple-element.51) | copy-start | bytes 6291460
  283.8 37.8 %collective-permute-start.13 = (bf16[768,512]{1,0:T(8,128)(2,1)}, bf16[768,512]{1,0:T(8,128)(2,1)}, u32[]{:S(2)}, u32[]{:S(2)}) collective-permute-start(bf16[768,512]{1,0:T(8,128)(2,1)} %shard_map.91), channel_id=1, source_target_pairs={{0,2},{1,3},{2,0},{3,1},{4,6},{5,7},{6,4},{7,5},{8,10},{9,11},{10,... | collective-permute-start | bytes 2359304 | tf_op jit(solution)/shard_map/ppermute | solution.py:253
  312.3 13.7 %collective-permute-start.17 = (bf16[768,512]{1,0:T(8,128)(2,1)}, bf16[768,512]{1,0:T(8,128)(2,1)S(1)}, u32[]{:S(2)}, u32[]{:S(2)}) collective-permute-start(bf16[768,512]{1,0:T(8,128)(2,1)} %shard_map.92), channel_id=1, source_target_pairs={{0,2},{1,3},{2,0},{3,1},{4,6},{5,7},{6,4},{7,5},{8,10},{9,11},{10,... | collective-permute-start | bytes 2359304 | tf_op jit(solution)/shard_map/ppermute | solution.py:253
  312.6 26.8 %collective-permute-start.12 = (bf16[768,512]{1,0:T(8,128)(2,1)S(1)}, bf16[768,512]{1,0:T(8,128)(2,1)S(1)}, u32[]{:S(2)}, u32[]{:S(2)}) collective-permute-start(bf16[768,512]{1,0:T(8,128)(2,1)S(1)} %copy-done.17), channel_id=1, source_target_pairs={{0,1},{1,0},{2,3},{3,2},{4,5},{5,4},{6,7},{7,6},{8,9},{9,8},{10,11... | collective-permute-start | bytes 2359304 | tf_op jit(solution)/shard_map/ppermute | solution.py:253
  318.5 18.7 %collective-permute-start.16 = (bf16[768,512]{1,0:T(8,128)(2,1)}, bf16[768,512]{1,0:T(8,128)(2,1)S(1)}, u32[]{:S(2)}, u32[]{:S(2)}) collective-permute-start(bf16[768,512]{1,0:T(8,128)(2,1)} %shard_map.92), channel_id=1, source_target_pairs={{0,1},{1,0},{2,3},{3,2},{4,5},{5,4},{6,7},{7,6},{8,9},{9,8},{10,11... | collective-permute-start | bytes 2359304 | tf_op jit(solution)/shard_map/ppermute | solution.py:253
  321.6 20.0 %collective-permute-start.14 = (bf16[768,512]{1,0:T(8,128)(2,1)}, bf16[768,512]{1,0:T(8,128)(2,1)S(1)}, u32[]{:S(2)}, u32[]{:S(2)}) collective-permute-start(bf16[768,512]{1,0:T(8,128)(2,1)} %collective-permute-done.13), channel_id=1, source_target_pairs={{0,1},{1,0},{2,3},{3,2},{4,5},{5,4},{6,7},{7,6},{8,9},{9,8},{10,11... | collective-permute-start | bytes 2359304 | tf_op jit(solution)/shard_map/ppermute | solution.py:253
  326.0 17.8 %collective-permute-start.18 = (bf16[768,512]{1,0:T(8,128)(2,1)S(1)}, bf16[768,512]{1,0:T(8,128)(2,1)S(1)}, u32[]{:S(2)}, u32[]{:S(2)}) collective-permute-start(bf16[768,512]{1,0:T(8,128)(2,1)S(1)} %collective-permute-done.17), channel_id=1, source_target_pairs={{0,1},{1,0},{2,3},{3,2},{4,5},{5,4},{6,7},{7,6},{8,9},{9,8},{10,11... | collective-permute-start | bytes 2359304 | tf_op jit(solution)/shard_map/ppermute | solution.py:253
  (3 other events, 2.7 us)

commit v6 on v3

--- a/solution.py
+++ b/solution.py
@@ -242,14 +242,16 @@
     return tuple(weights)
 
 
-def output_projection(gated, weights):
+def output_projection(gated, weights, earlier):
     count = lax.axis_size("tp")
     pieces = {0: gated}
     for bit in reversed(tp_bits(count)):
         pairs = [(k, k ^ bit) for k in range(count)]
         moved = {key ^ bit: lax.ppermute(piece, "tp", pairs) for key, piece in pieces.items()}
+        if earlier is not None:
+            moved, earlier = lax.optimization_barrier((moved, earlier))
         pieces.update(moved)
-    total = None
+    total = earlier
     for key in sorted(pieces):
         part = jnp.dot(pieces[key], weights[key], preferred_element_type=jnp.float32)
         total = part if total is None else total + part
@@ -324,8 +326,7 @@
         halo = lax.ppermute(tail, "ctx", [(k, k + 1) for k in range(ctx_count - 1)])
         gated = channel_filter(halo, chosen, taps, medium, skip, part * share, share)
         rows = slice(part * share * LANES, (part + 1) * share * LANES)
-        piece = output_projection(gated, tuple(w[rows] for w in weights))
-        total = piece if total is None else total + piece
+        total = output_projection(gated, tuple(w[rows] for w in weights), total)
     return total.astype(jnp.bfloat16)
 
 def solution(mesh):

time: 347 us -> 349 us (level)
  starting transfers between devices: 29.7 us -> 35.7 us
  waiting for transfers between devices: 159 us -> 154 us
    ppermute x6, starting transfers between devices: 14.6 us -> 19.7 us  [output_projection(): lax.ppermute(piece, 'tp', pairs)]
    ppermute x6, waiting for transfers between devices: 3.82 us -> 0.02 us  [output_projection(): lax.ppermute(piece, 'tp', pairs)]
    ppermute x2, waiting for transfers between devices: 44.7 us -> 40.9 us  [ring_step(): moved_ahead = lax.ppermute(ahead, 'ctx', forward)]
  transfers between devices with their start and end apart: 19 -> 19, of which waited for: 7 -> 7; matrix products, arithmetic and copies ran while one was open for 25% -> 24% of each run, Pallas kernels for 15% -> 8%
where the time goes in v6:
time: 349 us; the launch traced here: 348 us
  waiting for transfers between devices  154 us (44%)
  matrix products  76.4 us (22%)
  Pallas kernels  52.4 us (15%)
  starting transfers between devices  35.7 us (10%)
  local copies, waits for them, and re-layouts  16 us (5%)
  between operations  11.2 us (3%)
    ppermute x1, waiting for transfers between devices, ring_projection(): behind = lax.ppermute(in_weight, 'ctx', backward)  58.4 us
    dot_general x21, matrix products, product(): jnp.dot(cols, block[:, field, :], preferred_element_type=jnp.float32)  55.6 us
    pallas_call x2, Pallas kernels, channel_filter(): pl.pallas_call(functools.partial(filter_kernel, term_count), grid=(tiles,...  52.4 us
    ppermute x2, waiting for transfers between devices, ring_step(): moved_ahead = lax.ppermute(ahead, 'ctx', forward)  40.9 us
    ppermute x2, waiting for transfers between devices, ring_step(): moved_behind = lax.ppermute(behind, 'ctx', backward)  31.1 us
    ppermute x6, starting transfers between devices, output_projection(): lax.ppermute(piece, 'tp', pairs)  19.7 us
    ppermute x1, waiting for transfers between devices, ring_projection(): last_ahead = lax.ppermute(ahead[:half], 'ctx', forward)  19.1 us
    dot_general x8, matrix products, output_projection(): jnp.dot(pieces[key], weights[key], preferred_element_type=jnp.float32)  17.3 us
  transfers between devices with their start and end apart: 19, of which 7 were waited for; matrix products, arithmetic and copies ran while one was open for 24% of the time, Pallas kernels for 8%

profile of v6, /device:TPU:1, one launch (start us, length us, event | category | flops | bytes accessed | tf_op | source)
XLA Modules:
  0.0 348.1 jit_solution(10706943250770790157)
XLA Ops:
  0.0 2.1 collective-permute-start.2
  2.1 7.1 %constant_dynamic-slice_fusion.2 = (bf16[1024,1024]{1,0:T(8,128)(2,1)}, bf16[1024,1024]{1,0:T(8,128)(2,1)}, bf16[1024,1024]{1,0:T(8,128)(2,1)}, bf16[1024,1024]{1,0:T(8,128)(2,1)}) fusion(bf16[1024,4096]{1,0:T(8,128)(2,1)} %param.15, s32[]{:T(128)S(6)} %select_n.119, s32[]{:T(128)S(6)} %select_n.117, s32[]{:T(128)S(6)} %select_n.116, s32[]{:T(128)S(6)} %select_n.118), kind=kLoop, calls=%fused_computation.164 | loop fusion | bytes 16777232 | tf_op jit(solution)/shard_map/dynamic_slice | solution.py:240
  9.2 2.5 collective-permute-start.6
  11.9 58.4 %collective-permute-done.2 = bf16[512,3,1024]{2,0,1:T(8,128)(2,1)} collective-permute-done((bf16[512,3,1024]{2,0,1:T(8,128)(2,1)}, bf16[512,3,1024]{2,0,1:T(8,128)(2,1)}, u32[]{:S(2)}, u32[]{:S(2)}) %collective-permute-start.2) | collective-permute-done | bytes 3145760 | tf_op jit(solution)/shard_map/ppermute | solution.py:182
  70.3 1.1 collective-permute-start.3
  71.7 4.3 %fusion.31 = f32[768,1024]{1,0:T(8,128)} fusion(bf16[512,3,1024]{2,0,1:T(8,128)(2,1)} %param.10, bf16[768,4096]{1,0:T(8,128)(2,1)} %param.9, s32[]{:T(128)S(6)} %select_n.108), kind=kOutput, calls=%fused_computation.45 | convolution fusion | flops 805306368 | bytes 4980740 | tf_op jit(solution)/shard_map/dot_general | solution.py:146
  84.0 2.6 fusion.27
  86.7 2.5 fusion.29
  89.1 2.2 fusion.6
  91.4 2.2 fusion.7
  93.6 2.2 fusion.8
  95.8 4.0 %add_add_fusion.4 = f32[768,1024]{1,0:T(8,128)} fusion(f32[768,1024]{1,0:T(8,128)S(1)} %fusion.27, f32[768,1024]{1,0:T(8,128)S(1)} %fusion.6, bf16[512,3,1024]{2,0,1:T(8,128)(2,1)} %collective-permute-done.2, bf16[768,4096]{1,0:T(8,128)(2,1)S(1)} %bitcast.134, s32[]{:T(128)S(6)} %select_n.115), kind=kOutput, calls=%fused_computation.5 | convolution fusion | flops 806879232 | bytes 11272196 | tf_op jit(solution)/shard_map/dot_general | solution.py:146
  99.8 4.0 %add_add_fusion.5 = f32[768,1024]{1,0:T(8,128)} fusion(f32[768,1024]{1,0:T(8,128)S(1)} %fusion.29, f32[768,1024]{1,0:T(8,128)S(1)} %fusion.7, bf16[512,3,1024]{2,0,1:T(8,128)(2,1)} %collective-permute-done.2, bf16[768,4096]{1,0:T(8,128)(2,1)S(1)} %bitcast.134, s32[]{:T(128)S(6)} %select_n.115), kind=kOutput, calls=%fused_computation.6 | convolution fusion | flops 806879232 | bytes 11272196 | tf_op jit(solution)/shard_map/dot_general | solution.py:146
  103.8 4.0 %add_add_fusion.6 = f32[768,1024]{1,0:T(8,128)} fusion(f32[768,1024]{1,0:T(8,128)S(1)} %copy-done.9, f32[768,1024]{1,0:T(8,128)S(1)} %fusion.8, bf16[512,3,1024]{2,0,1:T(8,128)(2,1)} %collective-permute-done.2, bf16[768,4096]{1,0:T(8,128)(2,1)S(1)} %bitcast.134, s32[]{:T(128)S(6)} %select_n.115), kind=kOutput, calls=%fused_computation.7 | convolution fusion | flops 806879232 | bytes 11272196 | tf_op jit(solution)/shard_map/dot_general | solution.py:146
  107.9 31.1 %collective-permute-done.3 = bf16[512,3,1024]{2,0,1:T(8,128)(2,1)} collective-permute-done((bf16[512,3,1024]{2,0,1:T(8,128)(2,1)}, bf16[512,3,1024]{2,0,1:T(8,128)(2,1)}, u32[]{:S(2)}, u32[]{:S(2)}) %collective-permute-start.3) | collective-permute-done | bytes 3145760 | tf_op jit(solution)/shard_map/ppermute | solution.py:175
  144.7 2.0 copy.10
  147.4 1.2 constant_dynamic-slice_fusion.1
  149.6 2.9 fusion.13
  152.5 2.5 fusion.19
  155.0 2.4 fusion.25
  157.4 2.4 add_add_fusion.1.refs_8_
  159.8 3.2 add_add_fusion.2.refs_4_
  163.2 3.0 add_add_fusion.3.refs_0_
  166.2 40.4 %collective-permute-done.7 = bf16[512,3,1024]{2,0,1:T(8,128)(2,1)} collective-permute-done((bf16[512,3,1024]{2,0,1:T(8,128)(2,1)}, bf16[512,3,1024]{2,0,1:T(8,128)(2,1)}, u32[]{:S(2)}, u32[]{:S(2)}) %collective-permute-start.7) | collective-permute-done | bytes 3145760 | tf_op jit(solution)/shard_map/while/body/eval_jaxpr/ppermute | solution.py:174
  206.6 1.5 slice.261
  208.1 1.1 collective-permute-start.9
  210.1 2.2 fusion.1.refs_9_
  212.3 3.0 fusion.3.refs_5_
  215.3 3.0 fusion.5.refs_1_
  218.3 1.0 fusion.refs_10_
  221.3 19.1 %collective-permute-done.9 = bf16[256,3,1024]{2,0,1:T(8,128)(2,1)S(1)} collective-permute-done((bf16[256,3,1024]{2,0,1:T(8,128)(2,1)S(1)}, bf16[256,3,1024]{2,0,1:T(8,128)(2,1)S(1)}, u32[]{:S(2)}, u32[]{:S(2)}) %collective-permute-start.9) | collective-permute-done | bytes 1572896 | tf_op jit(solution)/shard_map/ppermute | solution.py:194
  240.5 1.3 collective-permute-done.10
  244.3 2.1 collective-permute-start.14
  248.4 2.9 collective-permute-done.14.halo
  252.1 26.2 %shard_map.92 = bf16[768,512]{1,0:T(8,128)(2,1)} custom-call(bf16[3,136,512]{2,1,0:T(8,128)(2,1)} %copy-done.24, f32[768,1024]{1,0:T(8,128)} %copy-done.2, f32[768,1024]{1,0:T(8,128)} %copy-done.5, f32[768,1024]{1,0:T(8,128)} %copy-done.8, f32[768,512]{1,0:T(8,128)} %copy-done.21, f32[768,1024]{1,0:T(8,128)} %copy-done.1, f32[768,1024]{1,0:T(8,128)} %copy-done.4, ...), custom_call_target="tpu_custom_call" | custom-call | tf_op jit(solution)/shard_map/pallas_call | solution.py:105
  278.3 1.3 collective-permute-start.16
  279.6 1.2 fusion.102
  280.9 4.4 %collective-permute-start.11 = (bf16[3,136,512]{2,1,0:T(8,128)(2,1)S(1)}, bf16[3,136,512]{2,1,0:T(8,128)(2,1)S(1)}, u32[]{:S(2)}, u32[]{:S(2)}) collective-permute-start(bf16[3,136,512]{2,1,0:T(8,128)(2,1)S(1)} %pad_maximum_fusion.2), channel_id=1, source_target_pairs={{0,4},{4,8},{8,12},{12,16},{16,20},{20,24},{24,28},{1,5},{5,9},{9,... | collective-permute-start | bytes 1253384 | tf_op jit(solution)/shard_map/ppermute | solution.py:326
  285.2 6.6 %collective-permute-start.15 = (bf16[768,512]{1,0:T(8,128)(2,1)}, bf16[768,512]{1,0:T(8,128)(2,1)}, u32[]{:S(2)}, u32[]{:S(2)}) collective-permute-start(bf16[768,512]{1,0:T(8,128)(2,1)} %shard_map.92), channel_id=1, source_target_pairs={{0,1},{1,0},{2,3},{3,2},{4,5},{5,4},{6,7},{7,6},{8,9},{9,8},{10,11... | collective-permute-start | bytes 2359304 | tf_op jit(solution)/shard_map/ppermute | solution.py:250
  292.6 26.2 %shard_map.91 = bf16[768,512]{1,0:T(8,128)(2,1)} custom-call(bf16[3,136,512]{2,1,0:T(8,128)(2,1)} %copy-done.23, f32[768,1024]{1,0:T(8,128)} %copy-done.2, f32[768,1024]{1,0:T(8,128)} %copy-done.5, f32[768,1024]{1,0:T(8,128)} %copy-done.8, f32[768,512]{1,0:T(8,128)} %copy-done.15, f32[768,1024]{1,0:T(8,128)} %copy-done.1, f32[768,1024]{1,0:T(8,128)} %copy-done.4, ...), custom_call_target="tpu_custom_call" | custom-call | tf_op jit(solution)/shard_map/pallas_call | solution.py:105
  319.2 5.5 %collective-permute-start.12 = (bf16[768,512]{1,0:T(8,128)(2,1)}, bf16[768,512]{1,0:T(8,128)(2,1)S(1)}, u32[]{:S(2)}, u32[]{:S(2)}) collective-permute-start(bf16[768,512]{1,0:T(8,128)(2,1)} %shard_map.91), channel_id=1, source_target_pairs={{0,1},{1,0},{2,3},{3,2},{4,5},{5,4},{6,7},{7,6},{8,9},{9,8},{10,11... | collective-permute-start | bytes 2359304 | tf_op jit(solution)/shard_map/ppermute | solution.py:250
  325.7 2.4 fusion.44
  328.1 2.4 fusion.46
  330.6 2.5 add_add_fusion
  333.1 6.0 %collective-permute-start.18 = (bf16[768,512]{1,0:T(8,128)(2,1)S(1)}, bf16[768,512]{1,0:T(8,128)(2,1)S(1)}, u32[]{:S(2)}, u32[]{:S(2)}) collective-permute-start(bf16[768,512]{1,0:T(8,128)(2,1)S(1)} %collective-permute-done.13), channel_id=1, source_target_pairs={{0,1},{1,0},{2,3},{3,2},{4,5},{5,4},{6,7},{7,6},{8,9},{9,8},{10,11... | collective-permute-start | bytes 2359304 | tf_op jit(solution)/shard_map/ppermute | solution.py:250
  340.1 2.2 fusion.37
  342.3 2.2 fusion.39
  344.6 3.5 %add_convert_fusion = bf16[768,1024]{1,0:T(8,128)(2,1)} fusion(f32[768,1024]{1,0:T(8,128)S(1)} %fusion.37, f32[768,1024]{1,0:T(8,128)S(1)} %fusion.39, f32[768,1024]{1,0:T(8,128)S(1)} %add_add_fusion, f32[768,1024]{1,0:T(8,128)S(1)} %fusion.41, bf16[768,512]{1,0:T(8,128)(2,1)S(1)} %collective-permute-done.18, bf16[1024,1024]{1,0:T(8,128)(2,1)} %collective-permute-done.6), kind=kOutput, calls=%fused_computation | convolution fusion | flops 809238528 | bytes 15990784 | tf_op jit(solution)/shard_map/dot_general | solution.py:256
  (115 shorter events, 16.9 us)
Async XLA Ops:
  0.0 70.3 %collective-permute-start.2 = (bf16[512,3,1024]{2,0,1:T(8,128)(2,1)}, bf16[512,3,1024]{2,0,1:T(8,128)(2,1)}, u32[]{:S(2)}, u32[]{:S(2)}) collective-permute-start(bf16[512,3,1024]{2,0,1:T(8,128)(2,1)} %param.10), channel_id=1, source_target_pairs={{0,4},{8,0},{16,8},{24,16},{28,24},{20,28},{12,20},{4,12},{1,5},{9... | collective-permute-start | bytes 9437192 | tf_op jit(solution)/shard_map/ppermute | solution.py:182
  2.1 69.3 %collective-permute-start = (bf16[512,3,1024]{2,0,1:T(8,128)(2,1)}, bf16[512,3,1024]{2,0,1:T(8,128)(2,1)}, u32[]{:S(2)}, u32[]{:S(2)}) collective-permute-start(bf16[512,3,1024]{2,0,1:T(8,128)(2,1)} %param.10), channel_id=1, source_target_pairs={{0,8},{8,16},{16,24},{24,28},{28,20},{20,12},{12,4},{4,0},{1,9},{9... | collective-permute-start | bytes 9437192 | tf_op jit(solution)/shard_map/ppermute | solution.py:181
  9.2 66.9 %copy-start.28 = (s32[8]{0:T(128)S(1)}, s32[8]{0:T(128)}, u32[]{:S(2)}) copy-start(s32[8]{0:T(128)} %constant.118.clone) | copy-start | bytes 100
  9.2 72.8 %copy-start.26 = (s32[8]{0:T(128)S(1)}, s32[8]{0:T(128)}, u32[]{:S(2)}) copy-start(s32[8]{0:T(128)} %constant.117.clone) | copy-start | bytes 100
  9.2 98.6 %collective-permute-start.6 = (bf16[1024,1024]{1,0:T(8,128)(2,1)}, bf16[1024,1024]{1,0:T(8,128)(2,1)}, u32[]{:S(2)}, u32[]{:S(2)}) collective-permute-start(bf16[1024,1024]{1,0:T(8,128)(2,1)} %get-tuple-element.67), channel_id=1, source_target_pairs={{0,3},{1,2},{2,1},{3,0},{4,7},{5,6},{6,5},{7,4},{8,11},{9,10},{10,... | collective-permute-start | bytes 6291464 | tf_op jit(solution)/shard_map/ppermute | solution.py:241
  11.7 96.1 %collective-permute-start.4 = (bf16[1024,1024]{1,0:T(8,128)(2,1)}, bf16[1024,1024]{1,0:T(8,128)(2,1)}, u32[]{:S(2)}, u32[]{:S(2)}) collective-permute-start(bf16[1024,1024]{1,0:T(8,128)(2,1)} %get-tuple-element.68), channel_id=1, source_target_pairs={{0,1},{1,0},{2,3},{3,2},{4,5},{5,4},{6,7},{7,6},{8,9},{9,8},{10,11... | collective-permute-start | bytes 6291464 | tf_op jit(solution)/shard_map/ppermute | solution.py:241
  11.7 96.1 %collective-permute-start.5 = (bf16[1024,1024]{1,0:T(8,128)(2,1)}, bf16[1024,1024]{1,0:T(8,128)(2,1)}, u32[]{:S(2)}, u32[]{:S(2)}) collective-permute-start(bf16[1024,1024]{1,0:T(8,128)(2,1)} %get-tuple-element.70), channel_id=1, source_target_pairs={{0,2},{1,3},{2,0},{3,1},{4,6},{5,7},{6,4},{7,5},{8,10},{9,11},{10,... | collective-permute-start | bytes 6291464 | tf_op jit(solution)/shard_map/ppermute | solution.py:241
  70.3 68.7 %collective-permute-start.3 = (bf16[512,3,1024]{2,0,1:T(8,128)(2,1)}, bf16[512,3,1024]{2,0,1:T(8,128)(2,1)}, u32[]{:S(2)}, u32[]{:S(2)}) collective-permute-start(bf16[512,3,1024]{2,0,1:T(8,128)(2,1)} %collective-permute-done.2), channel_id=1, source_target_pairs={{0,4},{8,0},{16,8},{24,16},{28,24},{20,28},{12,20},{4,12},{1,5},{9... | collective-permute-start | bytes 9437192 | tf_op jit(solution)/shard_map/ppermute | solution.py:175
  71.4 68.1 %collective-permute-start.1 = (bf16[512,3,1024]{2,0,1:T(8,128)(2,1)}, bf16[512,3,1024]{2,0,1:T(8,128)(2,1)}, u32[]{:S(2)}, u32[]{:S(2)}) collective-permute-start(bf16[512,3,1024]{2,0,1:T(8,128)(2,1)} %collective-permute-done), channel_id=1, source_target_pairs={{0,8},{8,16},{16,24},{24,28},{28,20},{20,12},{12,4},{4,0},{1,9},{9... | collective-permute-start | bytes 9437192 | tf_op jit(solution)/shard_map/ppermute | solution.py:174
  71.7 17.4 %slice-start = ((s8[6291456]{0:T(1024)(128)(4,1)}), s8[2097152]{0:T(1024)(128)(4,1)S(1)}, s32[]{:S(2)}) async-start(s8[6291456]{0:T(1024)(128)(4,1)} %bitcast.133), calls=%async_computation | async-start | bytes 4194304
  84.0 5.1 %slice-start.1 = ((s8[6291456]{0:T(1024)(128)(4,1)}), s8[4194304]{0:T(1024)(128)(4,1)S(1)}, s32[]{:S(2)}) async-start(s8[6291456]{0:T(1024)(128)(4,1)} %bitcast.133), calls=%async_computation.1 | async-start | bytes 8388608
  99.8 4.0 %copy-start.9 = (f32[768,1024]{1,0:T(8,128)S(1)}, f32[768,1024]{1,0:T(8,128)}, u32[]{:S(2)}) copy-start(f32[768,1024]{1,0:T(8,128)} %fusion.31) | copy-start | bytes 9437188
  103.8 40.9 %copy-start.27 = (f32[1024]{0:T(1024)S(1)}, f32[1024]{0:T(1024)}, u32[]{:S(2)}) copy-start(f32[1024]{0:T(1024)} %param.13) | copy-start | bytes 12292
  103.8 43.0 %copy-start.25 = (f32[3,1024,7]{1,2,0:T(8,128)S(1)}, f32[3,1024,7]{1,2,0:T(8,128)}, u32[]{:S(2)}) copy-start(f32[3,1024,7]{1,2,0:T(8,128)} %param.11) | copy-start | bytes 258052
  139.4 67.2 %collective-permute-start.7 = (bf16[512,3,1024]{2,0,1:T(8,128)(2,1)}, bf16[512,3,1024]{2,0,1:T(8,128)(2,1)}, u32[]{:S(2)}, u32[]{:S(2)}) collective-permute-start(bf16[512,3,1024]{2,0,1:T(8,128)(2,1)} %collective-permute-done.1), channel_id=1, source_target_pairs={{0,8},{8,16},{16,24},{24,28},{28,20},{20,12},{12,4},{4,0},{1,9},{9... | collective-permute-start | bytes 9437192 | tf_op jit(solution)/shard_map/while/body/eval_jaxpr/ppermute | solution.py:174
  140.1 69.1 %collective-permute-start.8 = (bf16[512,3,1024]{2,0,1:T(8,128)(2,1)}, bf16[512,3,1024]{2,0,1:T(8,128)(2,1)S(1)}, u32[]{:S(2)}, u32[]{:S(2)}) collective-permute-start(bf16[512,3,1024]{2,0,1:T(8,128)(2,1)} %collective-permute-done.3), channel_id=1, source_target_pairs={{0,4},{8,0},{16,8},{24,16},{28,24},{20,28},{12,20},{4,12},{1,5},{9... | collective-permute-start | bytes 9437192 | tf_op jit(solution)/shard_map/while/body/eval_jaxpr/ppermute | solution.py:175
  146.8 1.9 copy-start.22
  148.6 6.4 %slice-start.2 = ((s8[6291456]{0:T(1024)(128)(4,1)}), s8[4194304]{0:T(1024)(128)(4,1)S(1)}, s32[]{:S(2)}) async-start(s8[6291456]{0:T(1024)(128)(4,1)} %bitcast.135), calls=%async_computation.2 | async-start | bytes 8388608
  149.6 5.4 %slice-start.3 = ((s8[6291456]{0:T(1024)(128)(4,1)}), s8[2097152]{0:T(1024)(128)(4,1)S(1)}, s32[]{:S(2)}) async-start(s8[6291456]{0:T(1024)(128)(4,1)} %bitcast.135), calls=%async_computation.3 | async-start | bytes 4194304
  155.0 2.4 copy-start.10
  157.4 2.4 copy-start.11
  159.8 87.7 %copy-start = (f32[768,1024]{1,0:T(8,128)}, f32[768,1024]{1,0:T(8,128)S(1)}, u32[]{:S(2)}) copy-start(f32[768,1024]{1,0:T(8,128)S(1)} %add_add_fusion.1.refs_8_) | copy-start | bytes 9437188
  159.8 3.3 copy-start.12
  163.2 80.7 %copy-start.1 = (f32[768,1024]{1,0:T(8,128)}, f32[768,1024]{1,0:T(8,128)S(1)}, u32[]{:S(2)}) copy-start(f32[768,1024]{1,0:T(8,128)S(1)} %add_add_fusion.2.refs_4_) | copy-start | bytes 9437188
  166.2 81.5 %copy-start.2 = (f32[768,1024]{1,0:T(8,128)}, f32[768,1024]{1,0:T(8,128)S(1)}, u32[]{:S(2)}) copy-start(f32[768,1024]{1,0:T(8,128)S(1)} %add_add_fusion.3.refs_0_) | copy-start | bytes 9437188
  208.1 32.3 %collective-permute-start.9 = (bf16[256,3,1024]{2,0,1:T(8,128)(2,1)S(1)}, bf16[256,3,1024]{2,0,1:T(8,128)(2,1)S(1)}, u32[]{:S(2)}, u32[]{:S(2)}) collective-permute-start(bf16[256,3,1024]{2,0,1:T(8,128)(2,1)S(1)} %slice.261), channel_id=1, source_target_pairs={{0,8},{8,16},{16,24},{24,28},{28,20},{20,12},{12,4},{4,0},{1,9},{9... | collective-permute-start | bytes 4718600 | tf_op jit(solution)/shard_map/ppermute | solution.py:194
  209.3 32.5 %collective-permute-start.10 = (bf16[256,3,1024]{2,0,1:T(8,128)(2,1)S(1)}, bf16[256,3,1024]{2,0,1:T(8,128)(2,1)S(1)}, u32[]{:S(2)}, u32[]{:S(2)}) collective-permute-start(bf16[256,3,1024]{2,0,1:T(8,128)(2,1)S(1)} %slice.262), channel_id=1, source_target_pairs={{0,4},{8,0},{16,8},{24,16},{28,24},{20,28},{12,20},{4,12},{1,5},{9... | collective-permute-start | bytes 4718600 | tf_op jit(solution)/shard_map/ppermute | solution.py:195
  212.3 35.3 %copy-start.3 = (f32[768,1024]{1,0:T(8,128)}, f32[768,1024]{1,0:T(8,128)S(1)}, u32[]{:S(2)}) copy-start(f32[768,1024]{1,0:T(8,128)S(1)} %fusion.1.refs_9_) | copy-start | bytes 9437188
  215.3 28.6 %copy-start.4 = (f32[768,1024]{1,0:T(8,128)}, f32[768,1024]{1,0:T(8,128)S(1)}, u32[]{:S(2)}) copy-start(f32[768,1024]{1,0:T(8,128)S(1)} %fusion.3.refs_5_) | copy-start | bytes 9437188
  218.3 29.4 %copy-start.5 = (f32[768,1024]{1,0:T(8,128)}, f32[768,1024]{1,0:T(8,128)S(1)}, u32[]{:S(2)}) copy-start(f32[768,1024]{1,0:T(8,128)S(1)} %fusion.5.refs_1_) | copy-start | bytes 9437188
  219.3 28.3 %copy-start.6 = (f32[768,1024]{1,0:T(8,128)}, f32[768,1024]{1,0:T(8,128)S(1)}, u32[]{:S(2)}) copy-start(f32[768,1024]{1,0:T(8,128)S(1)} %fusion.refs_10_) | copy-start | bytes 9437188
  220.3 23.6 %copy-start.7 = (f32[768,1024]{1,0:T(8,128)}, f32[768,1024]{1,0:T(8,128)S(1)}, u32[]{:S(2)}) copy-start(f32[768,1024]{1,0:T(8,128)S(1)} %fusion.2.refs_6_) | copy-start | bytes 9437188
  221.3 26.4 %copy-start.8 = (f32[768,1024]{1,0:T(8,128)}, f32[768,1024]{1,0:T(8,128)S(1)}, u32[]{:S(2)}) copy-start(f32[768,1024]{1,0:T(8,128)S(1)} %fusion.4.refs_2_) | copy-start | bytes 9437188
  243.7 3.2 copy-start.21
  244.3 7.0 %collective-permute-start.14 = (bf16[3,136,512]{2,1,0:T(8,128)(2,1)S(1)}, bf16[3,136,512]{2,1,0:T(8,128)(2,1)S(1)}, u32[]{:S(2)}, u32[]{:S(2)}) collective-permute-start(bf16[3,136,512]{2,1,0:T(8,128)(2,1)S(1)} %pad_maximum_fusion.1), channel_id=1, source_target_pairs={{0,4},{4,8},{8,12},{12,16},{16,20},{20,24},{24,28},{1,5},{5,9},{9,... | collective-permute-start | bytes 1253384 | tf_op jit(solution)/shard_map/ppermute | solution.py:326
  247.0 1.5 copy-start.14
  247.6 3.7 %copy-start.15 = (f32[768,512]{1,0:T(8,128)}, f32[768,512]{1,0:T(8,128)S(1)}, u32[]{:S(2)}) copy-start(f32[768,512]{1,0:T(8,128)S(1)} %fusion.87.refs_3_) | copy-start | bytes 4718596
  248.4 31.1 %copy-start.16 = (f32[768,512]{1,0:T(8,128)}, f32[768,512]{1,0:T(8,128)S(1)}, u32[]{:S(2)}) copy-start(f32[768,512]{1,0:T(8,128)S(1)} %fusion.85.refs_7_) | copy-start | bytes 4718596
  278.3 46.4 %collective-permute-start.16 = (bf16[768,512]{1,0:T(8,128)(2,1)}, bf16[768,512]{1,0:T(8,128)(2,1)}, u32[]{:S(2)}, u32[]{:S(2)}) collective-permute-start(bf16[768,512]{1,0:T(8,128)(2,1)} %shard_map.92), channel_id=1, source_target_pairs={{0,2},{1,3},{2,0},{3,1},{4,6},{5,7},{6,4},{7,5},{8,10},{9,11},{10,... | collective-permute-start | bytes 2359304 | tf_op jit(solution)/shard_map/ppermute | solution.py:250
  280.8 43.8 %copy-start.13 = (bf16[1024,1024]{1,0:T(8,128)(2,1)S(1)}, bf16[1024,1024]{1,0:T(8,128)(2,1)}, u32[]{:S(2)}) copy-start(bf16[1024,1024]{1,0:T(8,128)(2,1)} %get-tuple-element.58) | copy-start | bytes 6291460
  280.9 43.8 %copy-start.17 = (bf16[768,512]{1,0:T(8,128)(2,1)S(1)}, bf16[768,512]{1,0:T(8,128)(2,1)}, u32[]{:S(2)}) copy-start(bf16[768,512]{1,0:T(8,128)(2,1)} %shard_map.92) | copy-start | bytes 2359300
  280.9 11.0 %collective-permute-start.11 = (bf16[3,136,512]{2,1,0:T(8,128)(2,1)S(1)}, bf16[3,136,512]{2,1,0:T(8,128)(2,1)S(1)}, u32[]{:S(2)}, u32[]{:S(2)}) collective-permute-start(bf16[3,136,512]{2,1,0:T(8,128)(2,1)S(1)} %pad_maximum_fusion.2), channel_id=1, source_target_pairs={{0,4},{4,8},{8,12},{12,16},{16,20},{20,24},{24,28},{1,5},{5,9},{9,... | collective-permute-start | bytes 1253384 | tf_op jit(solution)/shard_map/ppermute | solution.py:326
  285.2 42.9 %collective-permute-start.15 = (bf16[768,512]{1,0:T(8,128)(2,1)}, bf16[768,512]{1,0:T(8,128)(2,1)}, u32[]{:S(2)}, u32[]{:S(2)}) collective-permute-start(bf16[768,512]{1,0:T(8,128)(2,1)} %shard_map.92), channel_id=1, source_target_pairs={{0,1},{1,0},{2,3},{3,2},{4,5},{5,4},{6,7},{7,6},{8,9},{9,8},{10,11... | collective-permute-start | bytes 2359304 | tf_op jit(solution)/shard_map/ppermute | solution.py:250
  318.9 14.2 %collective-permute-start.13 = (bf16[768,512]{1,0:T(8,128)(2,1)}, bf16[768,512]{1,0:T(8,128)(2,1)S(1)}, u32[]{:S(2)}, u32[]{:S(2)}) collective-permute-start(bf16[768,512]{1,0:T(8,128)(2,1)} %shard_map.91), channel_id=1, source_target_pairs={{0,2},{1,3},{2,0},{3,1},{4,6},{5,7},{6,4},{7,5},{8,10},{9,11},{10,... | collective-permute-start | bytes 2359304 | tf_op jit(solution)/shard_map/ppermute | solution.py:250
  319.2 23.1 %collective-permute-start.12 = (bf16[768,512]{1,0:T(8,128)(2,1)}, bf16[768,512]{1,0:T(8,128)(2,1)S(1)}, u32[]{:S(2)}, u32[]{:S(2)}) collective-permute-start(bf16[768,512]{1,0:T(8,128)(2,1)} %shard_map.91), channel_id=1, source_target_pairs={{0,1},{1,0},{2,3},{3,2},{4,5},{5,4},{6,7},{7,6},{8,9},{9,8},{10,11... | collective-permute-start | bytes 2359304 | tf_op jit(solution)/shard_map/ppermute | solution.py:250
  324.7 5.9 %collective-permute-start.17 = (bf16[768,512]{1,0:T(8,128)(2,1)}, bf16[768,512]{1,0:T(8,128)(2,1)S(1)}, u32[]{:S(2)}, u32[]{:S(2)}) collective-permute-start(bf16[768,512]{1,0:T(8,128)(2,1)} %collective-permute-done.16), channel_id=1, source_target_pairs={{0,1},{1,0},{2,3},{3,2},{4,5},{5,4},{6,7},{7,6},{8,9},{9,8},{10,11... | collective-permute-start | bytes 2359304 | tf_op jit(solution)/shard_map/ppermute | solution.py:250
  330.6 8.5 %copy-start.18 = (bf16[768,512]{1,0:T(8,128)(2,1)S(1)}, bf16[768,512]{1,0:T(8,128)(2,1)}, u32[]{:S(2)}) copy-start(bf16[768,512]{1,0:T(8,128)(2,1)} %shard_map.91) | copy-start | bytes 2359300
  333.1 9.2 %collective-permute-start.18 = (bf16[768,512]{1,0:T(8,128)(2,1)S(1)}, bf16[768,512]{1,0:T(8,128)(2,1)S(1)}, u32[]{:S(2)}, u32[]{:S(2)}) collective-permute-start(bf16[768,512]{1,0:T(8,128)(2,1)S(1)} %collective-permute-done.13), channel_id=1, source_target_pairs={{0,1},{1,0},{2,3},{3,2},{4,5},{5,4},{6,7},{7,6},{8,9},{9,8},{10,11... | collective-permute-start | bytes 2359304 | tf_op jit(solution)/shard_map/ppermute | solution.py:250
  (4 other events, 4.0 us)

commit v7 on v3

--- a/solution.py
+++ b/solution.py
@@ -11,6 +11,7 @@
 
 HALO = 136
 CHUNK = 64
+MAIN = 128
 LANES = 128
 
 
@@ -75,22 +76,22 @@
             shifted[shift, tail:ext, :] = window[8 - shift : 8 - shift + ext - tail]
 
     def chunk_body(index, carry):
-        row = pl.multiple_of(index * CHUNK, CHUNK)
+        row = pl.multiple_of(index * MAIN, MAIN)
         at = pl.multiple_of(row + HALO, 8)
-        total = skip[...] * prod[pl.ds(at, CHUNK), :]
+        total = skip[...] * prod[pl.ds(at, MAIN), :]
         groups = medium.shape[0] // 8
         reach = 8 * (groups - 1)
         start = pl.multiple_of(at - reach, 8)
         for shift in range(8):
-            window = shifted[shift, pl.ds(start, CHUNK + reach), :]
+            window = shifted[shift, pl.ds(start, MAIN + reach), :]
             for group in range(groups):
                 offset = reach - 8 * group
                 weight = medium[pl.ds(8 * group + shift, 1), :]
-                total = total + weight * window[offset : offset + CHUNK]
-        out[pl.ds(row, CHUNK), :] = (smooth_q[pl.ds(row, CHUNK), :] * total).astype(out.dtype)
-        return carry
-
-    lax.fori_loop(0, local // CHUNK, chunk_body, 0)
+                total = total + weight * window[offset : offset + MAIN]
+        out[pl.ds(row, MAIN), :] = (smooth_q[pl.ds(row, MAIN), :] * total).astype(out.dtype)
+        return carry
+
+    lax.fori_loop(0, local // MAIN, chunk_body, 0)
 
 
 def channel_filter(halo, fields, taps, medium, skip, first, tiles):

time: 347 us -> 345 us (level)
  no operation moved by 1% of the time
where the time goes in v7:
time: 345 us; the launch traced here: 344 us
  waiting for transfers between devices  159 us (46%)
  matrix products  76.9 us (22%)
  Pallas kernels  51.2 us (15%)
  starting transfers between devices  29.7 us (9%)
  local copies, waits for them, and re-layouts  14.2 us (4%)
  between operations  11.3 us (3%)
    ppermute x1, waiting for transfers between devices, ring_projection(): behind = lax.ppermute(in_weight, 'ctx', backward)  58.5 us
    dot_general x21, matrix products, product(): jnp.dot(cols, block[:, field, :], preferred_element_type=jnp.float32)  55.1 us
    pallas_call x2, Pallas kernels, channel_filter(): pl.pallas_call(functools.partial(filter_kernel, term_count), grid=(tiles,...  51.2 us
    ppermute x2, waiting for transfers between devices, ring_step(): moved_ahead = lax.ppermute(ahead, 'ctx', forward)  44.7 us
    ppermute x2, waiting for transfers between devices, ring_step(): moved_behind = lax.ppermute(behind, 'ctx', backward)  31.3 us
    ppermute x1, waiting for transfers between devices, ring_projection(): last_ahead = lax.ppermute(ahead[:half], 'ctx', forward)  19.3 us
    dot_general x8, matrix products, output_projection(): jnp.dot(pieces[key], weights[key], preferred_element_type=jnp.float32)  18.3 us
    ppermute x6, starting transfers between devices, output_projection(): lax.ppermute(piece, 'tp', pairs)  14.6 us
  transfers between devices with their start and end apart: 19, of which 7 were waited for; matrix products, arithmetic and copies ran while one was open for 25% of the time, Pallas kernels for 15%

profile of v7, /device:TPU:1, one launch (start us, length us, event | category | flops | bytes accessed | tf_op | source)
XLA Modules:
  0.0 344.4 jit_solution(12776514606580815794)
XLA Ops:
  0.0 2.1 collective-permute-start.2
  2.1 6.9 %constant_dynamic-slice_fusion.2 = (bf16[1024,1024]{1,0:T(8,128)(2,1)}, bf16[1024,1024]{1,0:T(8,128)(2,1)}, bf16[1024,1024]{1,0:T(8,128)(2,1)}, bf16[1024,1024]{1,0:T(8,128)(2,1)}) fusion(bf16[1024,4096]{1,0:T(8,128)(2,1)} %param.15, s32[]{:T(128)S(6)} %select_n.119, s32[]{:T(128)S(6)} %select_n.117, s32[]{:T(128)S(6)} %select_n.116, s32[]{:T(128)S(6)} %select_n.118), kind=kLoop, calls=%fused_computation.163 | loop fusion | bytes 16777232 | tf_op jit(solution)/shard_map/dynamic_slice | solution.py:241
  9.1 2.5 collective-permute-start.6
  11.8 58.5 %collective-permute-done.2 = bf16[512,3,1024]{2,0,1:T(8,128)(2,1)} collective-permute-done((bf16[512,3,1024]{2,0,1:T(8,128)(2,1)}, bf16[512,3,1024]{2,0,1:T(8,128)(2,1)}, u32[]{:S(2)}, u32[]{:S(2)}) %collective-permute-start.2) | collective-permute-done | bytes 3145760 | tf_op jit(solution)/shard_map/ppermute | solution.py:183
  70.3 1.1 collective-permute-start.3
  71.7 4.2 %fusion.31 = f32[768,1024]{1,0:T(8,128)} fusion(bf16[512,3,1024]{2,0,1:T(8,128)(2,1)} %param.10, bf16[768,4096]{1,0:T(8,128)(2,1)} %param.9, s32[]{:T(128)S(6)} %select_n.108), kind=kOutput, calls=%fused_computation.44 | convolution fusion | flops 805306368 | bytes 4980740 | tf_op jit(solution)/shard_map/dot_general | solution.py:147
  83.9 2.6 fusion.27
  86.5 2.5 fusion.29
  89.0 2.2 fusion.6
  91.2 2.2 fusion.7
  93.4 2.2 fusion.8
  95.7 4.0 %add_add_fusion.3 = f32[768,1024]{1,0:T(8,128)} fusion(f32[768,1024]{1,0:T(8,128)S(1)} %fusion.27, f32[768,1024]{1,0:T(8,128)S(1)} %fusion.6, bf16[512,3,1024]{2,0,1:T(8,128)(2,1)} %collective-permute-done.2, bf16[768,4096]{1,0:T(8,128)(2,1)S(1)} %bitcast.134, s32[]{:T(128)S(6)} %select_n.115), kind=kOutput, calls=%fused_computation.4 | convolution fusion | flops 806879232 | bytes 11272196 | tf_op jit(solution)/shard_map/dot_general | solution.py:147
  99.6 4.1 %add_add_fusion.4 = f32[768,1024]{1,0:T(8,128)} fusion(f32[768,1024]{1,0:T(8,128)S(1)} %fusion.29, f32[768,1024]{1,0:T(8,128)S(1)} %fusion.7, bf16[512,3,1024]{2,0,1:T(8,128)(2,1)} %collective-permute-done.2, bf16[768,4096]{1,0:T(8,128)(2,1)S(1)} %bitcast.134, s32[]{:T(128)S(6)} %select_n.115), kind=kOutput, calls=%fused_computation.5 | convolution fusion | flops 806879232 | bytes 11272196 | tf_op jit(solution)/shard_map/dot_general | solution.py:147
  103.7 3.9 %add_add_fusion.5 = f32[768,1024]{1,0:T(8,128)} fusion(f32[768,1024]{1,0:T(8,128)S(1)} %copy-done.9, f32[768,1024]{1,0:T(8,128)S(1)} %fusion.8, bf16[512,3,1024]{2,0,1:T(8,128)(2,1)} %collective-permute-done.2, bf16[768,4096]{1,0:T(8,128)(2,1)S(1)} %bitcast.134, s32[]{:T(128)S(6)} %select_n.115), kind=kOutput, calls=%fused_computation.6 | convolution fusion | flops 806879232 | bytes 11272196 | tf_op jit(solution)/shard_map/dot_general | solution.py:147
  107.6 31.3 %collective-permute-done.3 = bf16[512,3,1024]{2,0,1:T(8,128)(2,1)} collective-permute-done((bf16[512,3,1024]{2,0,1:T(8,128)(2,1)}, bf16[512,3,1024]{2,0,1:T(8,128)(2,1)}, u32[]{:S(2)}, u32[]{:S(2)}) %collective-permute-start.3) | collective-permute-done | bytes 3145760 | tf_op jit(solution)/shard_map/ppermute | solution.py:176
  144.9 1.2 constant_dynamic-slice_fusion.1
  146.1 2.6 fusion.13
  148.7 2.5 fusion.19
  151.2 2.4 fusion.25
  153.6 2.4 add_add_fusion.refs_8_
  156.1 3.2 add_add_fusion.1.refs_4_
  159.4 3.0 add_add_fusion.2.refs_0_
  162.4 44.2 %collective-permute-done.7 = bf16[512,3,1024]{2,0,1:T(8,128)(2,1)} collective-permute-done((bf16[512,3,1024]{2,0,1:T(8,128)(2,1)}, bf16[512,3,1024]{2,0,1:T(8,128)(2,1)}, u32[]{:S(2)}, u32[]{:S(2)}) %collective-permute-start.7) | collective-permute-done | bytes 3145760 | tf_op jit(solution)/shard_map/while/body/eval_jaxpr/ppermute | solution.py:175
  206.6 1.5 slice.261
  208.1 1.1 collective-permute-start.9
  209.8 2.2 fusion.1.refs_9_
  212.1 3.0 fusion.3.refs_5_
  215.1 3.0 fusion.5.refs_1_
  218.1 1.0 fusion.refs_10_
  219.1 1.0 fusion.2.refs_6_
  220.1 1.0 fusion.4.refs_2_
  221.1 19.3 %collective-permute-done.9 = bf16[256,3,1024]{2,0,1:T(8,128)(2,1)S(1)} collective-permute-done((bf16[256,3,1024]{2,0,1:T(8,128)(2,1)S(1)}, bf16[256,3,1024]{2,0,1:T(8,128)(2,1)S(1)}, u32[]{:S(2)}, u32[]{:S(2)}) %collective-permute-start.9) | collective-permute-done | bytes 1572896 | tf_op jit(solution)/shard_map/ppermute | solution.py:195
  240.5 1.1 collective-permute-done.10
  244.2 2.4 collective-permute-start.11
  249.7 3.4 collective-permute-start.15
  255.7 25.6 %shard_map.91 = bf16[768,512]{1,0:T(8,128)(2,1)} custom-call(bf16[3,136,512]{2,1,0:T(8,128)(2,1)} %copy-done.23, f32[768,1024]{1,0:T(8,128)} %copy-done.2, f32[768,1024]{1,0:T(8,128)} %copy-done.5, f32[768,1024]{1,0:T(8,128)} %copy-done.8, f32[768,512]{1,0:T(8,128)} %copy-done.20, f32[768,1024]{1,0:T(8,128)} %copy-done.1, f32[768,1024]{1,0:T(8,128)} %copy-done.4, ...), custom_call_target="tpu_custom_call" | custom-call | tf_op jit(solution)/shard_map/pallas_call | solution.py:106
  281.3 1.3 collective-permute-start.13
  283.3 25.6 %shard_map.92 = bf16[768,512]{1,0:T(8,128)(2,1)} custom-call(bf16[3,136,512]{2,1,0:T(8,128)(2,1)} %copy-done.22, f32[768,1024]{1,0:T(8,128)} %copy-done.2, f32[768,1024]{1,0:T(8,128)} %copy-done.5, f32[768,1024]{1,0:T(8,128)} %copy-done.8, f32[768,512]{1,0:T(8,128)} %copy-done.16, f32[768,1024]{1,0:T(8,128)} %copy-done.1, f32[768,1024]{1,0:T(8,128)} %copy-done.4, ...), custom_call_target="tpu_custom_call" | custom-call | tf_op jit(solution)/shard_map/pallas_call | solution.py:106
  309.3 5.9 %collective-permute-start.12 = (bf16[768,512]{1,0:T(8,128)(2,1)S(1)}, bf16[768,512]{1,0:T(8,128)(2,1)S(1)}, u32[]{:S(2)}, u32[]{:S(2)}) collective-permute-start(bf16[768,512]{1,0:T(8,128)(2,1)S(1)} %copy-done.17), channel_id=1, source_target_pairs={{0,1},{1,0},{2,3},{3,2},{4,5},{5,4},{6,7},{7,6},{8,9},{9,8},{10,11... | collective-permute-start | bytes 2359304 | tf_op jit(solution)/shard_map/ppermute | solution.py:251
  315.2 2.1 fusion.38
  318.8 3.8 %collective-permute-done.17 = bf16[768,512]{1,0:T(8,128)(2,1)S(1)} collective-permute-done((bf16[768,512]{1,0:T(8,128)(2,1)}, bf16[768,512]{1,0:T(8,128)(2,1)S(1)}, u32[]{:S(2)}, u32[]{:S(2)}) %collective-permute-start.17) | collective-permute-done | bytes 786464 | tf_op jit(solution)/shard_map/ppermute | solution.py:251
  322.6 6.5 %collective-permute-start.18 = (bf16[768,512]{1,0:T(8,128)(2,1)S(1)}, bf16[768,512]{1,0:T(8,128)(2,1)S(1)}, u32[]{:S(2)}, u32[]{:S(2)}) collective-permute-start(bf16[768,512]{1,0:T(8,128)(2,1)S(1)} %collective-permute-done.17), channel_id=1, source_target_pairs={{0,1},{1,0},{2,3},{3,2},{4,5},{5,4},{6,7},{7,6},{8,9},{9,8},{10,11... | collective-permute-start | bytes 2359304 | tf_op jit(solution)/shard_map/ppermute | solution.py:251
  329.2 2.2 fusion.34
  331.4 2.4 fusion.42
  333.8 2.2 fusion.36
  336.0 2.2 fusion.44
  338.3 2.2 fusion.40
  340.5 3.9 %add_convert_fusion = bf16[768,1024]{1,0:T(8,128)(2,1)} fusion(f32[768,1024]{1,0:T(8,128)S(1)} %fusion.34, f32[768,1024]{1,0:T(8,128)S(1)} %fusion.38, f32[768,1024]{1,0:T(8,128)S(1)} %fusion.36, f32[768,1024]{1,0:T(8,128)S(1)} %fusion.40, f32[768,1024]{1,0:T(8,128)S(1)} %fusion.42, f32[768,1024]{1,0:T(8,128)S(1)} %fusion.46, f32[768,1024]{1,0:T(8,128)S(1)} %fusion.44, ...), kind=kOutput, calls=%fused_computation | convolution fusion | flops 811597824 | bytes 25427968 | tf_op jit(solution)/shard_map/dot_general | solution.py:255
  (113 shorter events, 15.5 us)
Async XLA Ops:
  0.0 70.3 %collective-permute-start.2 = (bf16[512,3,1024]{2,0,1:T(8,128)(2,1)}, bf16[512,3,1024]{2,0,1:T(8,128)(2,1)}, u32[]{:S(2)}, u32[]{:S(2)}) collective-permute-start(bf16[512,3,1024]{2,0,1:T(8,128)(2,1)} %param.10), channel_id=1, source_target_pairs={{0,4},{8,0},{16,8},{24,16},{28,24},{20,28},{12,20},{4,12},{1,5},{9... | collective-permute-start | bytes 9437192 | tf_op jit(solution)/shard_map/ppermute | solution.py:183
  2.1 69.3 %collective-permute-start = (bf16[512,3,1024]{2,0,1:T(8,128)(2,1)}, bf16[512,3,1024]{2,0,1:T(8,128)(2,1)}, u32[]{:S(2)}, u32[]{:S(2)}) collective-permute-start(bf16[512,3,1024]{2,0,1:T(8,128)(2,1)} %param.10), channel_id=1, source_target_pairs={{0,8},{8,16},{16,24},{24,28},{28,20},{20,12},{12,4},{4,0},{1,9},{9... | collective-permute-start | bytes 9437192 | tf_op jit(solution)/shard_map/ppermute | solution.py:182
  9.1 66.9 %copy-start.27 = (s32[8]{0:T(128)S(1)}, s32[8]{0:T(128)}, u32[]{:S(2)}) copy-start(s32[8]{0:T(128)} %constant.118.clone) | copy-start | bytes 100
  9.1 72.8 %copy-start.25 = (s32[8]{0:T(128)S(1)}, s32[8]{0:T(128)}, u32[]{:S(2)}) copy-start(s32[8]{0:T(128)} %constant.117.clone) | copy-start | bytes 100
  9.1 98.6 %collective-permute-start.6 = (bf16[1024,1024]{1,0:T(8,128)(2,1)}, bf16[1024,1024]{1,0:T(8,128)(2,1)}, u32[]{:S(2)}, u32[]{:S(2)}) collective-permute-start(bf16[1024,1024]{1,0:T(8,128)(2,1)} %get-tuple-element.57), channel_id=1, source_target_pairs={{0,3},{1,2},{2,1},{3,0},{4,7},{5,6},{6,5},{7,4},{8,11},{9,10},{10,... | collective-permute-start | bytes 6291464 | tf_op jit(solution)/shard_map/ppermute | solution.py:242
  11.6 96.1 %collective-permute-start.4 = (bf16[1024,1024]{1,0:T(8,128)(2,1)}, bf16[1024,1024]{1,0:T(8,128)(2,1)}, u32[]{:S(2)}, u32[]{:S(2)}) collective-permute-start(bf16[1024,1024]{1,0:T(8,128)(2,1)} %get-tuple-element.58), channel_id=1, source_target_pairs={{0,1},{1,0},{2,3},{3,2},{4,5},{5,4},{6,7},{7,6},{8,9},{9,8},{10,11... | collective-permute-start | bytes 6291464 | tf_op jit(solution)/shard_map/ppermute | solution.py:242
  11.6 96.1 %collective-permute-start.5 = (bf16[1024,1024]{1,0:T(8,128)(2,1)}, bf16[1024,1024]{1,0:T(8,128)(2,1)}, u32[]{:S(2)}, u32[]{:S(2)}) collective-permute-start(bf16[1024,1024]{1,0:T(8,128)(2,1)} %get-tuple-element.60), channel_id=1, source_target_pairs={{0,2},{1,3},{2,0},{3,1},{4,6},{5,7},{6,4},{7,5},{8,10},{9,11},{10,... | collective-permute-start | bytes 6291464 | tf_op jit(solution)/shard_map/ppermute | solution.py:242
  70.3 68.7 %collective-permute-start.3 = (bf16[512,3,1024]{2,0,1:T(8,128)(2,1)}, bf16[512,3,1024]{2,0,1:T(8,128)(2,1)}, u32[]{:S(2)}, u32[]{:S(2)}) collective-permute-start(bf16[512,3,1024]{2,0,1:T(8,128)(2,1)} %collective-permute-done.2), channel_id=1, source_target_pairs={{0,4},{8,0},{16,8},{24,16},{28,24},{20,28},{12,20},{4,12},{1,5},{9... | collective-permute-start | bytes 9437192 | tf_op jit(solution)/shard_map/ppermute | solution.py:176
  71.4 68.1 %collective-permute-start.1 = (bf16[512,3,1024]{2,0,1:T(8,128)(2,1)}, bf16[512,3,1024]{2,0,1:T(8,128)(2,1)}, u32[]{:S(2)}, u32[]{:S(2)}) collective-permute-start(bf16[512,3,1024]{2,0,1:T(8,128)(2,1)} %collective-permute-done), channel_id=1, source_target_pairs={{0,8},{8,16},{16,24},{24,28},{28,20},{20,12},{12,4},{4,0},{1,9},{9... | collective-permute-start | bytes 9437192 | tf_op jit(solution)/shard_map/ppermute | solution.py:175
  71.7 17.2 %slice-start = ((s8[6291456]{0:T(1024)(128)(4,1)}), s8[2097152]{0:T(1024)(128)(4,1)S(1)}, s32[]{:S(2)}) async-start(s8[6291456]{0:T(1024)(128)(4,1)} %bitcast.133), calls=%async_computation | async-start | bytes 4194304
  83.9 5.1 %slice-start.1 = ((s8[6291456]{0:T(1024)(128)(4,1)}), s8[4194304]{0:T(1024)(128)(4,1)S(1)}, s32[]{:S(2)}) async-start(s8[6291456]{0:T(1024)(128)(4,1)} %bitcast.133), calls=%async_computation.1 | async-start | bytes 8388608
  99.6 4.1 %copy-start.9 = (f32[768,1024]{1,0:T(8,128)S(1)}, f32[768,1024]{1,0:T(8,128)}, u32[]{:S(2)}) copy-start(f32[768,1024]{1,0:T(8,128)} %fusion.31) | copy-start | bytes 9437188
  139.4 67.2 %collective-permute-start.7 = (bf16[512,3,1024]{2,0,1:T(8,128)(2,1)}, bf16[512,3,1024]{2,0,1:T(8,128)(2,1)}, u32[]{:S(2)}, u32[]{:S(2)}) collective-permute-start(bf16[512,3,1024]{2,0,1:T(8,128)(2,1)} %collective-permute-done.1), channel_id=1, source_target_pairs={{0,8},{8,16},{16,24},{24,28},{28,20},{20,12},{12,4},{4,0},{1,9},{9... | collective-permute-start | bytes 9437192 | tf_op jit(solution)/shard_map/while/body/eval_jaxpr/ppermute | solution.py:175
  140.1 69.1 %collective-permute-start.8 = (bf16[512,3,1024]{2,0,1:T(8,128)(2,1)}, bf16[512,3,1024]{2,0,1:T(8,128)(2,1)S(1)}, u32[]{:S(2)}, u32[]{:S(2)}) collective-permute-start(bf16[512,3,1024]{2,0,1:T(8,128)(2,1)} %collective-permute-done.3), channel_id=1, source_target_pairs={{0,4},{8,0},{16,8},{24,16},{28,24},{20,28},{12,20},{4,12},{1,5},{9... | collective-permute-start | bytes 9437192 | tf_op jit(solution)/shard_map/while/body/eval_jaxpr/ppermute | solution.py:176
  146.0 5.2 %slice-start.2 = ((s8[6291456]{0:T(1024)(128)(4,1)}), s8[4194304]{0:T(1024)(128)(4,1)S(1)}, s32[]{:S(2)}) async-start(s8[6291456]{0:T(1024)(128)(4,1)} %bitcast.135), calls=%async_computation.2 | async-start | bytes 8388608
  146.1 5.1 %slice-start.3 = ((s8[6291456]{0:T(1024)(128)(4,1)}), s8[2097152]{0:T(1024)(128)(4,1)S(1)}, s32[]{:S(2)}) async-start(s8[6291456]{0:T(1024)(128)(4,1)} %bitcast.135), calls=%async_computation.3 | async-start | bytes 4194304
  151.2 2.4 copy-start.10
  153.6 2.4 copy-start.11
  156.1 92.3 %copy-start = (f32[768,1024]{1,0:T(8,128)}, f32[768,1024]{1,0:T(8,128)S(1)}, u32[]{:S(2)}) copy-start(f32[768,1024]{1,0:T(8,128)S(1)} %add_add_fusion.refs_8_) | copy-start | bytes 9437188
  156.1 3.3 copy-start.12
  159.4 89.2 %copy-start.1 = (f32[768,1024]{1,0:T(8,128)}, f32[768,1024]{1,0:T(8,128)S(1)}, u32[]{:S(2)}) copy-start(f32[768,1024]{1,0:T(8,128)S(1)} %add_add_fusion.1.refs_4_) | copy-start | bytes 9437188
  162.4 86.0 %copy-start.2 = (f32[768,1024]{1,0:T(8,128)}, f32[768,1024]{1,0:T(8,128)S(1)}, u32[]{:S(2)}) copy-start(f32[768,1024]{1,0:T(8,128)S(1)} %add_add_fusion.2.refs_0_) | copy-start | bytes 9437188
  208.1 32.3 %collective-permute-start.9 = (bf16[256,3,1024]{2,0,1:T(8,128)(2,1)S(1)}, bf16[256,3,1024]{2,0,1:T(8,128)(2,1)S(1)}, u32[]{:S(2)}, u32[]{:S(2)}) collective-permute-start(bf16[256,3,1024]{2,0,1:T(8,128)(2,1)S(1)} %slice.261), channel_id=1, source_target_pairs={{0,8},{8,16},{16,24},{24,28},{28,20},{20,12},{12,4},{4,0},{1,9},{9... | collective-permute-start | bytes 4718600 | tf_op jit(solution)/shard_map/ppermute | solution.py:195
  209.3 32.3 %collective-permute-start.10 = (bf16[256,3,1024]{2,0,1:T(8,128)(2,1)S(1)}, bf16[256,3,1024]{2,0,1:T(8,128)(2,1)S(1)}, u32[]{:S(2)}, u32[]{:S(2)}) collective-permute-start(bf16[256,3,1024]{2,0,1:T(8,128)(2,1)S(1)} %slice.262), channel_id=1, source_target_pairs={{0,4},{8,0},{16,8},{24,16},{28,24},{20,28},{12,20},{4,12},{1,5},{9... | collective-permute-start | bytes 4718600 | tf_op jit(solution)/shard_map/ppermute | solution.py:196
  212.0 36.3 %copy-start.3 = (f32[768,1024]{1,0:T(8,128)}, f32[768,1024]{1,0:T(8,128)S(1)}, u32[]{:S(2)}) copy-start(f32[768,1024]{1,0:T(8,128)S(1)} %fusion.1.refs_9_) | copy-start | bytes 9437188
  215.0 33.6 %copy-start.4 = (f32[768,1024]{1,0:T(8,128)}, f32[768,1024]{1,0:T(8,128)S(1)}, u32[]{:S(2)}) copy-start(f32[768,1024]{1,0:T(8,128)S(1)} %fusion.3.refs_5_) | copy-start | bytes 9437188
  218.1 30.4 %copy-start.5 = (f32[768,1024]{1,0:T(8,128)}, f32[768,1024]{1,0:T(8,128)S(1)}, u32[]{:S(2)}) copy-start(f32[768,1024]{1,0:T(8,128)S(1)} %fusion.5.refs_1_) | copy-start | bytes 9437188
  219.1 29.3 %copy-start.6 = (f32[768,1024]{1,0:T(8,128)}, f32[768,1024]{1,0:T(8,128)S(1)}, u32[]{:S(2)}) copy-start(f32[768,1024]{1,0:T(8,128)S(1)} %fusion.refs_10_) | copy-start | bytes 9437188
  220.1 28.6 %copy-start.7 = (f32[768,1024]{1,0:T(8,128)}, f32[768,1024]{1,0:T(8,128)S(1)}, u32[]{:S(2)}) copy-start(f32[768,1024]{1,0:T(8,128)S(1)} %fusion.2.refs_6_) | copy-start | bytes 9437188
  221.1 27.4 %copy-start.8 = (f32[768,1024]{1,0:T(8,128)}, f32[768,1024]{1,0:T(8,128)S(1)}, u32[]{:S(2)}) copy-start(f32[768,1024]{1,0:T(8,128)S(1)} %fusion.4.refs_2_) | copy-start | bytes 9437188
  242.3 1.3 copy-start.18
  242.9 1.2 copy-start.19
  243.5 3.0 copy-start.20
  244.2 10.7 %collective-permute-start.11 = (bf16[3,136,512]{2,1,0:T(8,128)(2,1)S(1)}, bf16[3,136,512]{2,1,0:T(8,128)(2,1)S(1)}, u32[]{:S(2)}, u32[]{:S(2)}) collective-permute-start(bf16[3,136,512]{2,1,0:T(8,128)(2,1)S(1)} %pad_maximum_fusion.1), channel_id=1, source_target_pairs={{0,4},{4,8},{8,12},{12,16},{16,20},{20,24},{24,28},{1,5},{5,9},{9,... | collective-permute-start | bytes 1253384 | tf_op jit(solution)/shard_map/ppermute | solution.py:325
  247.1 1.4 copy-start.14
  247.7 5.4 %copy-start.26 = (f32[1024]{0:T(1024)S(1)}, f32[1024]{0:T(1024)}, u32[]{:S(2)}) copy-start(f32[1024]{0:T(1024)} %param.13) | copy-start | bytes 12292
  247.7 5.4 %copy-start.21 = (f32[1024,128]{1,0:T(8,128)S(1)}, f32[1024,128]{1,0:T(8,128)}, u32[]{:S(2)}) copy-start(f32[1024,128]{1,0:T(8,128)} %param.12) | copy-start | bytes 1572868
  248.3 1.3 copy-start.16
  248.3 5.0 %copy-start.24 = (f32[3,1024,7]{1,2,0:T(8,128)S(1)}, f32[3,1024,7]{1,2,0:T(8,128)}, u32[]{:S(2)}) copy-start(f32[3,1024,7]{1,2,0:T(8,128)} %param.11) | copy-start | bytes 258052
  249.7 32.9 %collective-permute-start.15 = (bf16[3,136,512]{2,1,0:T(8,128)(2,1)}, bf16[3,136,512]{2,1,0:T(8,128)(2,1)S(1)}, u32[]{:S(2)}, u32[]{:S(2)}) collective-permute-start(bf16[3,136,512]{2,1,0:T(8,128)(2,1)} %pad_maximum_fusion.2), channel_id=1, source_target_pairs={{0,4},{4,8},{8,12},{12,16},{16,20},{20,24},{24,28},{1,5},{5,9},{9,... | collective-permute-start | bytes 1253384 | tf_op jit(solution)/shard_map/ppermute | solution.py:325
  281.2 28.0 %copy-start.17 = (bf16[768,512]{1,0:T(8,128)(2,1)S(1)}, bf16[768,512]{1,0:T(8,128)(2,1)}, u32[]{:S(2)}) copy-start(bf16[768,512]{1,0:T(8,128)(2,1)} %shard_map.91) | copy-start | bytes 2359300
  281.2 33.9 %copy-start.13 = (bf16[1024,1024]{1,0:T(8,128)(2,1)S(1)}, bf16[1024,1024]{1,0:T(8,128)(2,1)}, u32[]{:S(2)}) copy-start(bf16[1024,1024]{1,0:T(8,128)(2,1)} %get-tuple-element.51) | copy-start | bytes 6291460
  281.3 37.0 %collective-permute-start.13 = (bf16[768,512]{1,0:T(8,128)(2,1)}, bf16[768,512]{1,0:T(8,128)(2,1)}, u32[]{:S(2)}, u32[]{:S(2)}) collective-permute-start(bf16[768,512]{1,0:T(8,128)(2,1)} %shard_map.91), channel_id=1, source_target_pairs={{0,2},{1,3},{2,0},{3,1},{4,6},{5,7},{6,4},{7,5},{8,10},{9,11},{10,... | collective-permute-start | bytes 2359304 | tf_op jit(solution)/shard_map/ppermute | solution.py:251
  308.9 13.7 %collective-permute-start.17 = (bf16[768,512]{1,0:T(8,128)(2,1)}, bf16[768,512]{1,0:T(8,128)(2,1)S(1)}, u32[]{:S(2)}, u32[]{:S(2)}) collective-permute-start(bf16[768,512]{1,0:T(8,128)(2,1)} %shard_map.92), channel_id=1, source_target_pairs={{0,2},{1,3},{2,0},{3,1},{4,6},{5,7},{6,4},{7,5},{8,10},{9,11},{10,... | collective-permute-start | bytes 2359304 | tf_op jit(solution)/shard_map/ppermute | solution.py:251
  309.3 26.8 %collective-permute-start.12 = (bf16[768,512]{1,0:T(8,128)(2,1)S(1)}, bf16[768,512]{1,0:T(8,128)(2,1)S(1)}, u32[]{:S(2)}, u32[]{:S(2)}) collective-permute-start(bf16[768,512]{1,0:T(8,128)(2,1)S(1)} %copy-done.17), channel_id=1, source_target_pairs={{0,1},{1,0},{2,3},{3,2},{4,5},{5,4},{6,7},{7,6},{8,9},{9,8},{10,11... | collective-permute-start | bytes 2359304 | tf_op jit(solution)/shard_map/ppermute | solution.py:251
  315.1 18.7 %collective-permute-start.16 = (bf16[768,512]{1,0:T(8,128)(2,1)}, bf16[768,512]{1,0:T(8,128)(2,1)S(1)}, u32[]{:S(2)}, u32[]{:S(2)}) collective-permute-start(bf16[768,512]{1,0:T(8,128)(2,1)} %shard_map.92), channel_id=1, source_target_pairs={{0,1},{1,0},{2,3},{3,2},{4,5},{5,4},{6,7},{7,6},{8,9},{9,8},{10,11... | collective-permute-start | bytes 2359304 | tf_op jit(solution)/shard_map/ppermute | solution.py:251
  318.3 20.0 %collective-permute-start.14 = (bf16[768,512]{1,0:T(8,128)(2,1)}, bf16[768,512]{1,0:T(8,128)(2,1)S(1)}, u32[]{:S(2)}, u32[]{:S(2)}) collective-permute-start(bf16[768,512]{1,0:T(8,128)(2,1)} %collective-permute-done.13), channel_id=1, source_target_pairs={{0,1},{1,0},{2,3},{3,2},{4,5},{5,4},{6,7},{7,6},{8,9},{9,8},{10,11... | collective-permute-start | bytes 2359304 | tf_op jit(solution)/shard_map/ppermute | solution.py:251
  322.6 17.8 %collective-permute-start.18 = (bf16[768,512]{1,0:T(8,128)(2,1)S(1)}, bf16[768,512]{1,0:T(8,128)(2,1)S(1)}, u32[]{:S(2)}, u32[]{:S(2)}) collective-permute-start(bf16[768,512]{1,0:T(8,128)(2,1)S(1)} %collective-permute-done.17), channel_id=1, source_target_pairs={{0,1},{1,0},{2,3},{3,2},{4,5},{5,4},{6,7},{7,6},{8,9},{9,8},{10,11... | collective-permute-start | bytes 2359304 | tf_op jit(solution)/shard_map/ppermute | solution.py:251
  (3 other events, 2.7 us)
